TPU v7x, 256 devices: a whole 4x4x8 slice. The times are simulated.
256 devices in a mesh: gx: 8 (over x, core), gy: 32 (over y, z).
Axes of the slice: x: 4, y: 4, z: 8, core: 2. Of those that a mesh axis runs over, the one named last changes fastest.
Arguments:
- cells: bfloat16 [256, 1048576], P(None, ('gx', 'gy')), may hold values from -25 to 25
- send_index: int32 [8192, 2], P(('gx', 'gy')), may hold values from 0 to 31
- send_count: int32 [8192], P(('gx', 'gy')), may hold values from 1 to 2, as said below
- prolong_block: int32 [8192, 4], P(('gx', 'gy')), may hold values from 0 to 63, as said below
- prolong_level: int32 [8192, 4], P(('gx', 'gy')), may hold values from 0 to 3
- prolong_maps: bfloat16 [4, 128, 512], replicated, may hold values from -0.25 to 0.25
Outputs:
- factor: float32 [256, 256], replicated
- modes: float32 [128, 4194304], P(None, ('gx', 'gy'))
Inputs may be any that keep to these rules, and one draw needn't show every extreme that they name: `send_count`: every sender and owner pair uses 1 to 2 slots; some pair uses all 2. `prolong_block`: the first slot feeding each brick is slot 0 of some sender, a multiple of 2.
All inputs are finite; a program needn't handle non-finite values.
Results may differ from a plain program's by a relative error of at most 0.0041.
Values may be sent and summed in bfloat16 or wider, within the bound.
No kernel may reach another device: no remote copies, remote signals or barrier semaphores. Data moves between devices by JAX's collectives and lax.ppermute only.
A program may use at most 128 MiB of HBM per device.

v0:
```python
import functools

import jax
import jax.numpy as jnp
from jax import lax
from jax.experimental import pallas as pl
from jax.experimental.pallas import tpu as pltpu
from jax.sharding import PartitionSpec as P

RANK = 128
BLK = 128
PER = 8


def from_partner(value, axis, bit):
    mask = 2**bit
    pairs = [(source, source ^ mask) for source in range(lax.axis_size(axis))]
    return lax.ppermute(value, axis, pairs)


def all_sum(value):
    for axis in ("gx", "gy"):
        for bit in range(lax.axis_size(axis).bit_length() - 1):
            value = value + from_partner(value, axis, bit)
    return value


def lift_kernel(feeds, brick_cells, blocks_ref, levels_ref, recv_ref, maps_ref, out_ref):
    step = pl.program_id(0)
    for i in range(PER):
        brick = step * PER + i
        acc = None
        for n in range(feeds):
            slot = blocks_ref[brick * feeds + n]
            level = levels_ref[brick * feeds + n]
            part = jnp.dot(recv_ref[slot], maps_ref[level], preferred_element_type=jnp.float32)
            acc = part if acc is None else acc + part
        out_ref[:, i * brick_cells : (i + 1) * brick_cells] = acc.astype(out_ref.dtype)


def lift(received, blocks, levels, maps):
    slots, rows, blk = received.shape
    bricks, feeds = blocks.shape
    brick_cells = maps.shape[2]
    grid_spec = pltpu.PrefetchScalarGridSpec(
        num_scalar_prefetch=2,
        grid=(bricks // PER,),
        in_specs=[
            pl.BlockSpec((slots, rows, blk), lambda s, b, l: (0, 0, 0)),
            pl.BlockSpec(maps.shape, lambda s, b, l: (0, 0, 0)),
        ],
        out_specs=pl.BlockSpec((rows, PER * brick_cells), lambda s, b, l: (0, s)),
    )
    flops = 2 * rows * blk * brick_cells * bricks * feeds
    return pl.pallas_call(
        functools.partial(lift_kernel, feeds, brick_cells),
        grid_spec=grid_spec,
        out_shape=jax.ShapeDtypeStruct((rows, bricks * brick_cells), jnp.bfloat16),
        cost_estimate=pl.CostEstimate(
            flops=flops,
            bytes_accessed=received.size * 2 + maps.size * 2 + rows * bricks * brick_cells * 2,
            transcendentals=0,
        ),
    )(blocks.reshape(-1), levels.reshape(-1), received, maps)


def gram_of(left, right):
    return lax.dot_general(
        left, right, (((1,), (1,)), ((), ())), preferred_element_type=jnp.float32
    )


def body(cells, send_index, send_count, prolong_block, prolong_level, prolong_maps):
    snaps = cells.shape[0]
    kept = RANK
    local = cells.reshape(snaps, -1, BLK).transpose(1, 0, 2)
    peers, slots = send_index.shape
    live = (jnp.arange(slots, dtype=jnp.int32)[None, :] < send_count[:, None]).reshape(-1)
    outgoing = jnp.take(local, send_index.reshape(-1), axis=0)
    outgoing = outgoing * live[:, None, None].astype(jnp.bfloat16)
    head_out, tail_out = outgoing[:, :kept], outgoing[:, kept:]
    head_in = lax.all_to_all(head_out, "gy", split_axis=0, concat_axis=0, tiled=True)
    head_in, tail_out = lax.optimization_barrier((head_in, tail_out))
    tail_in = lax.all_to_all(tail_out, "gy", split_axis=0, concat_axis=0, tiled=True)
    total_cells = lax.axis_size("gx") * lax.axis_size("gy") * prolong_block.shape[0] * prolong_maps.shape[2]
    head = lift(head_in, prolong_block, prolong_level, prolong_maps)
    c11 = all_sum(gram_of(head, head)) / total_cells
    l11 = jnp.linalg.cholesky(c11)
    inv11 = lax.linalg.triangular_solve(
        l11, jnp.eye(kept, dtype=jnp.float32), left_side=True, lower=True
    )
    inv_hi = inv11.astype(jnp.bfloat16)
    inv_lo = (inv11 - inv_hi.astype(jnp.float32)).astype(jnp.bfloat16)
    modes = jnp.dot(inv_hi, head, preferred_element_type=jnp.float32) + jnp.dot(
        inv_lo, head, preferred_element_type=jnp.float32
    )
    tail_in, modes, l11, inv11 = lax.optimization_barrier((tail_in, modes, l11, inv11))
    tail = lift(tail_in, prolong_block, prolong_level, prolong_maps)
    lower = all_sum(gram_of(tail, jnp.concatenate([head, tail], axis=0))) / total_cells
    c21, c22 = lower[:, :kept], lower[:, kept:]
    l21 = jnp.dot(c21, inv11.T, precision=lax.Precision.HIGHEST)
    schur = c22 - jnp.dot(l21, l21.T, precision=lax.Precision.HIGHEST)
    l22 = jnp.linalg.cholesky(schur)
    factor = jnp.concatenate(
        [
            jnp.concatenate([l11, jnp.zeros((kept, snaps - kept), jnp.float32)], axis=1),
            jnp.concatenate([l21, l22], axis=1),
        ],
        axis=0,
    )
    return (factor, modes)


def solution(mesh):
    in_specs = (
        P(None, ("gx", "gy")),
        P(("gx", "gy"), None),
        P(("gx", "gy")),
        P(("gx", "gy"), None),
        P(("gx", "gy"), None),
        P(),
    )
    out_specs = (P(), P(None, ("gx", "gy")))
    return jax.shard_map(body, mesh=mesh, in_specs=in_specs, out_specs=out_specs, check_vma=False)
```

profile of v0, /device:TPU:6, one launch (start us, length us, event | category | flops | bytes accessed | tf_op | source)
XLA Modules:
  0.0 270.3 jit_solution(9209882178918558055)
XLA Ops:
  2.5 4.1 %copy.33 = bf16[256,4096]{0,1:T(8,128)(2,1)} copy(bf16[256,4096]{1,0:T(8,128)(2,1)} %param.7) | data formatting | bytes 4194304 | tf_op args[0]
  17.3 62.6 %all_to_all.10.recv_ref = bf16[64,128,128]{2,1,0:T(8,128)(2,1)} all-to-all(bf16[64,128,128]{2,1,0:T(8,128)(2,1)S(1)} %get-tuple-element.18), channel_id=1, replica_groups=mesh['gx'=8,'gy'=32] {'gy'}, dimensions={0} | all-to-all | bytes 4194304 | tf_op jit(solution)/shard_map/all_to_all | solution.py:82
  79.9 5.1 %all-to-all-start.1 = ((bf16[64,128,128]{2,1,0:T(8,128)(2,1)}), bf16[64,128,128]{2,1,0:T(8,128)(2,1)S(1)}, u32[]{:S(2)}, u32[]{:S(2)}) async-start(bf16[64,128,128]{2,1,0:T(8,128)(2,1)} %get-tuple-element.9), calls=%async_computation.1 | async-start | bytes 4194304 | tf_op jit(solution)/shard_map/all_to_all | solution.py:84
  86.4 8.4 %shard_map.77 = bf16[128,16384]{1,0:T(8,128)(2,1)} custom-call(s32[128]{0:T(128)} %reshape.83.blocks_ref, s32[128]{0:T(128)} %reshape.84.levels_ref, bf16[64,128,128]{2,1,0:T(8,128)(2,1)} %all_to_all.10.recv_ref, bf16[4,128,512]{2,1,0:T(8,128)(2,1)} %maps_ref.3), custom_call_target="tpu_custom_call" | custom-call | flops 2147483648 | bytes 6815744 | tf_op jit(solution)/shard_map/pallas_call | solution.py:55
  94.8 4.7 %fusion.17 = f32[128,128]{0,1:T(8,128)S(1)} fusion(bf16[128,16384]{1,0:T(8,128)(2,1)} %shard_map.77), kind=kOutput, calls=%fused_computation.42 | convolution fusion | flops 536870912 | bytes 4259840 | tf_op jit(solution)/shard_map/dot_general | solution.py:68
  106.7 4.4 %collective-permute-done.2 = f32[128,128]{0,1:T(8,128)S(1)} collective-permute-done((f32[128,128]{0,1:T(8,128)S(1)}, f32[128,128]{0,1:T(8,128)S(1)}, u32[]{:S(2)}, u32[]{:S(2)}) %collective-permute-start.2) | collective-permute-done | bytes 65568 | tf_op jit(solution)/shard_map/ppermute | solution.py:18
  113.0 19.6 %collective-permute-done.3 = f32[128,128]{0,1:T(8,128)S(1)} collective-permute-done((f32[128,128]{0,1:T(8,128)S(1)}, f32[128,128]{0,1:T(8,128)S(1)}, u32[]{:S(2)}, u32[]{:S(2)}) %collective-permute-start.3) | collective-permute-done | bytes 65568 | tf_op jit(solution)/shard_map/ppermute | solution.py:18
  138.2 5.5 %collective-permute-start.5 = (f32[128,128]{0,1:T(8,128)S(1)}, f32[128,128]{0,1:T(8,128)S(1)}, u32[]{:S(2)}, u32[]{:S(2)}) collective-permute-start(f32[128,128]{0,1:T(8,128)S(1)} %add.91), channel_id=1, source_target_pairs={{0,4},{1,5},{2,6},{3,7},{4,0},{5,1},{6,2},{7,3},{8,12},{9,13},{10,... | collective-permute-start | bytes 196616 | tf_op jit(solution)/shard_map/ppermute | solution.py:18
  151.2 3.5 %collective-permute-start.7 = (f32[128,128]{0,1:T(8,128)S(1)}, f32[128,128]{0,1:T(8,128)S(1)}, u32[]{:S(2)}, u32[]{:S(2)}) collective-permute-start(f32[128,128]{0,1:T(8,128)S(1)} %add.93), channel_id=1, source_target_pairs={{0,16},{1,17},{2,18},{3,19},{4,20},{5,21},{6,22},{7,23},{8,24},{9,... | collective-permute-start | bytes 196616 | tf_op jit(solution)/shard_map/ppermute | solution.py:18
  157.3 11.7 %cholesky.44 = f32[128,128]{1,0:T(8,128)S(1)} custom-call(f32[128,128]{1,0:T(8,128)S(1)} %fusion.9), custom_call_target="Cholesky" | custom-call | tf_op jit(solution)/shard_map/jit(cholesky)/cholesky | solution.py:88
  170.4 9.8 %custom-call.5 = f32[1,128,128]{1,2,0:T(8,128)S(1)} custom-call(f32[1,128,128]{2,1,0:T(8,128)S(1)} %get-tuple-element.15), custom_call_target="InvertDiagBlocksLowerTriangular" | custom-call | tf_op jit(solution)/shard_map/triangular_solve | solution.py:89
  180.5 3.6 %fusion.11 = f32[128,16384]{1,0:T(8,128)S(1)} fusion(bf16[128,16384]{1,0:T(8,128)(2,1)} %shard_map.77, f32[128,128]{1,0:T(8,128)S(1)} %fusion.7), kind=kOutput, calls=%fused_computation.29 | convolution fusion | flops 536887296 | bytes 12648448 | tf_op jit(solution)/shard_map/dot_general | solution.py:94
  184.1 4.6 %convolution_add_fusion = f32[128,16384]{1,0:T(8,128)} fusion(f32[128,16384]{1,0:T(8,128)S(1)} %fusion.11, bf16[128,16384]{1,0:T(8,128)(2,1)S(1)} %copy-done, f32[128,128]{1,0:T(8,128)S(1)} %fusion.7), kind=kOutput, calls=%fused_computation.1 | convolution fusion | flops 539033600 | bytes 21037056 | tf_op jit(solution)/shard_map/dot_general | solution.py:94
  190.1 8.4 %shard_map.78 = bf16[128,16384]{1,0:T(8,128)(2,1)} custom-call(s32[128]{0:T(128)} %reshape.83.blocks_ref, s32[128]{0:T(128)} %reshape.84.levels_ref, bf16[64,128,128]{2,1,0:T(8,128)(2,1)} %copy-done.1, bf16[4,128,512]{2,1,0:T(8,128)(2,1)} %maps_ref.3), custom_call_target="tpu_custom_call" | custom-call | flops 2147483648 | bytes 6815744 | tf_op jit(solution)/shard_map/pallas_call | solution.py:55
  198.4 7.0 %fusion = f32[128,256]{0,1:T(8,128)S(1)} fusion(bf16[128,16384]{1,0:T(8,128)(2,1)} %shard_map.78, bf16[128,16384]{1,0:T(8,128)(2,1)} %shard_map.77), kind=kOutput, calls=%fused_computation.2 | convolution fusion | flops 1090519040 | bytes 8519680 | tf_op jit(solution)/shard_map/dot_general | solution.py:68
  208.0 4.7 %collective-permute-done.9 = f32[128,256]{0,1:T(8,128)S(1)} collective-permute-done((f32[128,256]{0,1:T(8,128)S(1)}, f32[128,256]{0,1:T(8,128)S(1)}, u32[]{:S(2)}, u32[]{:S(2)}) %collective-permute-start.9) | collective-permute-done | bytes 131104 | tf_op jit(solution)/shard_map/ppermute | solution.py:18
  214.2 5.1 %collective-permute-done.10 = f32[128,256]{0,1:T(8,128)S(1)} collective-permute-done((f32[128,256]{0,1:T(8,128)S(1)}, f32[128,256]{0,1:T(8,128)S(1)}, u32[]{:S(2)}, u32[]{:S(2)}) %collective-permute-start.10) | collective-permute-done | bytes 131104 | tf_op jit(solution)/shard_map/ppermute | solution.py:18
  219.9 4.5 %collective-permute-done.11 = f32[128,256]{0,1:T(8,128)S(1)} collective-permute-done((f32[128,256]{0,1:T(8,128)S(1)}, f32[128,256]{0,1:T(8,128)S(1)}, u32[]{:S(2)}, u32[]{:S(2)}) %collective-permute-start.11) | collective-permute-done | bytes 131104 | tf_op jit(solution)/shard_map/ppermute | solution.py:18
  224.4 4.0 %collective-permute-start.12 = (f32[128,256]{0,1:T(8,128)S(1)}, f32[128,256]{0,1:T(8,128)S(1)}, u32[]{:S(2)}, u32[]{:S(2)}) collective-permute-start(f32[128,256]{0,1:T(8,128)S(1)} %add.99), channel_id=1, source_target_pairs={{0,2},{1,3},{2,0},{3,1},{4,6},{5,7},{6,4},{7,5},{8,10},{9,11},{10,... | collective-permute-start | bytes 393224 | tf_op jit(solution)/shard_map/ppermute | solution.py:18
  231.8 8.3 %collective-permute-start.13 = (f32[128,256]{0,1:T(8,128)S(1)}, f32[128,256]{0,1:T(8,128)S(1)}, u32[]{:S(2)}, u32[]{:S(2)}) collective-permute-start(f32[128,256]{0,1:T(8,128)S(1)} %add.100), channel_id=1, source_target_pairs={{0,4},{1,5},{2,6},{3,7},{4,0},{5,1},{6,2},{7,3},{8,12},{9,13},{10,... | collective-permute-start | bytes 393224 | tf_op jit(solution)/shard_map/ppermute | solution.py:18
  240.1 4.0 %collective-permute-done.13 = f32[128,256]{0,1:T(8,128)S(1)} collective-permute-done((f32[128,256]{0,1:T(8,128)S(1)}, f32[128,256]{0,1:T(8,128)S(1)}, u32[]{:S(2)}, u32[]{:S(2)}) %collective-permute-start.13) | collective-permute-done | bytes 131104 | tf_op jit(solution)/shard_map/ppermute | solution.py:18
  244.2 5.0 %collective-permute-done.14 = f32[128,256]{0,1:T(8,128)S(1)} collective-permute-done((f32[128,256]{0,1:T(8,128)S(1)}, f32[128,256]{0,1:T(8,128)S(1)}, u32[]{:S(2)}, u32[]{:S(2)}) %collective-permute-start.14) | collective-permute-done | bytes 131104 | tf_op jit(solution)/shard_map/ppermute | solution.py:18
  251.6 4.1 %collective-permute-done.15 = f32[128,256]{0,1:T(8,128)S(1)} collective-permute-done((f32[128,256]{0,1:T(8,128)S(1)}, f32[128,256]{0,1:T(8,128)S(1)}, u32[]{:S(2)}, u32[]{:S(2)}) %collective-permute-start.15) | collective-permute-done | bytes 131104 | tf_op jit(solution)/shard_map/ppermute | solution.py:18
  256.5 11.7 %cholesky.55 = f32[128,128]{1,0:T(8,128)S(1)} custom-call(f32[128,128]{1,0:T(8,128)S(1)} %fusion.6), custom_call_target="Cholesky" | custom-call | tf_op jit(solution)/shard_map/jit(cholesky)/cholesky | solution.py:103
  (76 shorter events, 54.9 us)
Async XLA Ops:
  17.3 67.7 %copy-start.2 = (s32[32,4]{0,1:T(4,128)S(1)}, s32[32,4]{0,1:T(4,128)}, u32[]{:S(2)}) copy-start(s32[32,4]{0,1:T(4,128)} %param.10) | copy-start | bytes 1540
  17.3 68.4 %copy-start.3 = (s32[32,4]{0,1:T(4,128)S(1)}, s32[32,4]{0,1:T(4,128)}, u32[]{:S(2)}) copy-start(s32[32,4]{0,1:T(4,128)} %param.11) | copy-start | bytes 1540
  79.9 108.8 %all-to-all-start.1 = ((bf16[64,128,128]{2,1,0:T(8,128)(2,1)}), bf16[64,128,128]{2,1,0:T(8,128)(2,1)S(1)}, u32[]{:S(2)}, u32[]{:S(2)}) async-start(bf16[64,128,128]{2,1,0:T(8,128)(2,1)} %get-tuple-element.9), calls=%async_computation.1 | async-start | bytes 4194304 | tf_op jit(solution)/shard_map/all_to_all | solution.py:84
  99.5 1.3 collective-permute-start
  100.9 4.4 %collective-permute-start.1 = (f32[128,128]{0,1:T(8,128)S(1)}, f32[128,128]{0,1:T(8,128)S(1)}, u32[]{:S(2)}, u32[]{:S(2)}) collective-permute-start(f32[128,128]{0,1:T(8,128)S(1)} %add.87), channel_id=1, source_target_pairs={{0,64},{32,96},{64,0},{96,32},{128,192},{160,224},{192,128},{224,1... | collective-permute-start | bytes 196616 | tf_op jit(solution)/shard_map/ppermute | solution.py:18
  105.2 5.9 %collective-permute-start.2 = (f32[128,128]{0,1:T(8,128)S(1)}, f32[128,128]{0,1:T(8,128)S(1)}, u32[]{:S(2)}, u32[]{:S(2)}) collective-permute-start(f32[128,128]{0,1:T(8,128)S(1)} %add.88), channel_id=1, source_target_pairs={{0,128},{32,160},{64,192},{96,224},{128,0},{160,32},{192,64},{224,... | collective-permute-start | bytes 196616 | tf_op jit(solution)/shard_map/ppermute | solution.py:18
  111.1 21.5 %collective-permute-start.3 = (f32[128,128]{0,1:T(8,128)S(1)}, f32[128,128]{0,1:T(8,128)S(1)}, u32[]{:S(2)}, u32[]{:S(2)}) collective-permute-start(f32[128,128]{0,1:T(8,128)S(1)} %add.89), channel_id=1, source_target_pairs={{0,1},{1,0},{2,3},{3,2},{4,5},{5,4},{6,7},{7,6},{8,9},{9,8},{10,11... | collective-permute-start | bytes 196616 | tf_op jit(solution)/shard_map/ppermute | solution.py:18
  132.6 5.5 %collective-permute-start.4 = (f32[128,128]{0,1:T(8,128)S(1)}, f32[128,128]{0,1:T(8,128)S(1)}, u32[]{:S(2)}, u32[]{:S(2)}) collective-permute-start(f32[128,128]{0,1:T(8,128)S(1)} %add.90), channel_id=1, source_target_pairs={{0,2},{1,3},{2,0},{3,1},{4,6},{5,7},{6,4},{7,5},{8,10},{9,11},{10,... | collective-permute-start | bytes 196616 | tf_op jit(solution)/shard_map/ppermute | solution.py:18
  138.2 8.4 %collective-permute-start.5 = (f32[128,128]{0,1:T(8,128)S(1)}, f32[128,128]{0,1:T(8,128)S(1)}, u32[]{:S(2)}, u32[]{:S(2)}) collective-permute-start(f32[128,128]{0,1:T(8,128)S(1)} %add.91), channel_id=1, source_target_pairs={{0,4},{1,5},{2,6},{3,7},{4,0},{5,1},{6,2},{7,3},{8,12},{9,13},{10,... | collective-permute-start | bytes 196616 | tf_op jit(solution)/shard_map/ppermute | solution.py:18
  146.6 4.6 %collective-permute-start.6 = (f32[128,128]{0,1:T(8,128)S(1)}, f32[128,128]{0,1:T(8,128)S(1)}, u32[]{:S(2)}, u32[]{:S(2)}) collective-permute-start(f32[128,128]{0,1:T(8,128)S(1)} %add.92), channel_id=1, source_target_pairs={{0,8},{1,9},{2,10},{3,11},{4,12},{5,13},{6,14},{7,15},{8,0},{9,1},... | collective-permute-start | bytes 196616 | tf_op jit(solution)/shard_map/ppermute | solution.py:18
  151.2 6.0 %collective-permute-start.7 = (f32[128,128]{0,1:T(8,128)S(1)}, f32[128,128]{0,1:T(8,128)S(1)}, u32[]{:S(2)}, u32[]{:S(2)}) collective-permute-start(f32[128,128]{0,1:T(8,128)S(1)} %add.93), channel_id=1, source_target_pairs={{0,16},{1,17},{2,18},{3,19},{4,20},{5,21},{6,22},{7,23},{8,24},{9,... | collective-permute-start | bytes 196616 | tf_op jit(solution)/shard_map/ppermute | solution.py:18
  180.4 3.6 %copy-start = (bf16[128,16384]{1,0:T(8,128)(2,1)S(1)}, bf16[128,16384]{1,0:T(8,128)(2,1)}, u32[]{:S(2)}) copy-start(bf16[128,16384]{1,0:T(8,128)(2,1)} %shard_map.77) | copy-start | bytes 12582916
  188.7 1.4 copy-start.1
  205.4 1.4 collective-permute-start.8
  206.9 5.9 %collective-permute-start.9 = (f32[128,256]{0,1:T(8,128)S(1)}, f32[128,256]{0,1:T(8,128)S(1)}, u32[]{:S(2)}, u32[]{:S(2)}) collective-permute-start(f32[128,256]{0,1:T(8,128)S(1)} %add.96), channel_id=1, source_target_pairs={{0,64},{32,96},{64,0},{96,32},{128,192},{160,224},{192,128},{224,1... | collective-permute-start | bytes 393224 | tf_op jit(solution)/shard_map/ppermute | solution.py:18
  212.8 6.6 %collective-permute-start.10 = (f32[128,256]{0,1:T(8,128)S(1)}, f32[128,256]{0,1:T(8,128)S(1)}, u32[]{:S(2)}, u32[]{:S(2)}) collective-permute-start(f32[128,256]{0,1:T(8,128)S(1)} %add.97), channel_id=1, source_target_pairs={{0,128},{32,160},{64,192},{96,224},{128,0},{160,32},{192,64},{224,... | collective-permute-start | bytes 393224 | tf_op jit(solution)/shard_map/ppermute | solution.py:18
  219.3 5.1 %collective-permute-start.11 = (f32[128,256]{0,1:T(8,128)S(1)}, f32[128,256]{0,1:T(8,128)S(1)}, u32[]{:S(2)}, u32[]{:S(2)}) collective-permute-start(f32[128,256]{0,1:T(8,128)S(1)} %add.98), channel_id=1, source_target_pairs={{0,1},{1,0},{2,3},{3,2},{4,5},{5,4},{6,7},{7,6},{8,9},{9,8},{10,11... | collective-permute-start | bytes 393224 | tf_op jit(solution)/shard_map/ppermute | solution.py:18
  224.4 7.3 %collective-permute-start.12 = (f32[128,256]{0,1:T(8,128)S(1)}, f32[128,256]{0,1:T(8,128)S(1)}, u32[]{:S(2)}, u32[]{:S(2)}) collective-permute-start(f32[128,256]{0,1:T(8,128)S(1)} %add.99), channel_id=1, source_target_pairs={{0,2},{1,3},{2,0},{3,1},{4,6},{5,7},{6,4},{7,5},{8,10},{9,11},{10,... | collective-permute-start | bytes 393224 | tf_op jit(solution)/shard_map/ppermute | solution.py:18
  231.8 12.3 %collective-permute-start.13 = (f32[128,256]{0,1:T(8,128)S(1)}, f32[128,256]{0,1:T(8,128)S(1)}, u32[]{:S(2)}, u32[]{:S(2)}) collective-permute-start(f32[128,256]{0,1:T(8,128)S(1)} %add.100), channel_id=1, source_target_pairs={{0,4},{1,5},{2,6},{3,7},{4,0},{5,1},{6,2},{7,3},{8,12},{9,13},{10,... | collective-permute-start | bytes 393224 | tf_op jit(solution)/shard_map/ppermute | solution.py:18
  244.1 5.1 %collective-permute-start.14 = (f32[128,256]{0,1:T(8,128)S(1)}, f32[128,256]{0,1:T(8,128)S(1)}, u32[]{:S(2)}, u32[]{:S(2)}) collective-permute-start(f32[128,256]{0,1:T(8,128)S(1)} %add.101), channel_id=1, source_target_pairs={{0,8},{1,9},{2,10},{3,11},{4,12},{5,13},{6,14},{7,15},{8,0},{9,1},... | collective-permute-start | bytes 393224 | tf_op jit(solution)/shard_map/ppermute | solution.py:18
  249.2 6.6 %collective-permute-start.15 = (f32[128,256]{0,1:T(8,128)S(1)}, f32[128,256]{0,1:T(8,128)S(1)}, u32[]{:S(2)}, u32[]{:S(2)}) collective-permute-start(f32[128,256]{0,1:T(8,128)S(1)} %add.102), channel_id=1, source_target_pairs={{0,16},{1,17},{2,18},{3,19},{4,20},{5,21},{6,22},{7,23},{8,24},{9,... | collective-permute-start | bytes 393224 | tf_op jit(solution)/shard_map/ppermute | solution.py:18
where the time goes:
time: 271 us; the launch traced here: 270 us
  waiting for transfers between devices  71.7 us (26%)
  blocking collectives  62.6 us (23%)
  starting transfers between devices  41.1 us (15%)
  other arithmetic  40.3 us (15%)
  matrix products  20.6 us (8%)
  Pallas kernels  16.7 us (6%)
  local copies, waits for them, and re-layouts  16.3 us (6%)
    ppermute x16, waiting for transfers between devices, from_partner(): return lax.ppermute(value, axis, pairs)  71.7 us
    all_to_all x1, blocking collectives, body(): lax.all_to_all(head_out, 'gy', split_axis=0, concat_axis=0, tiled=True)  62.6 us
    ppermute x16, starting transfers between devices, from_partner(): return lax.ppermute(value, axis, pairs)  36.1 us
    pallas_call x2, Pallas kernels, lift(): pl.pallas_call(functools.partial(lift_kernel, feeds, brick_cells), grid_s...  16.7 us
    another operation x3, other arithmetic, body(): l11 = jnp.linalg.cholesky(c11)  12.4 us
    another operation x3, other arithmetic, body(): l22 = jnp.linalg.cholesky(schur)  12.4 us
    dot_general x2, matrix products, gram_of(): lax.dot_general(left, right, (((1,), (1,)), ((), ())), preferred_element_...  11.7 us
    another operation x2, other arithmetic, body(): lax.linalg.triangular_solve(l11, jnp.eye(kept, dtype=jnp.float32), left_s...  10.5 us
  transfers between devices with their start and end apart: 17, of which 16 were waited for; matrix products, arithmetic and copies ran while one was open for 14% of the time, Pallas kernels for 3%

commit v1 on v0

--- a/solution.py
+++ b/solution.py
@@ -25,8 +25,18 @@
     return value
 
 
-def lift_kernel(feeds, brick_cells, blocks_ref, levels_ref, recv_ref, maps_ref, out_ref):
+def lift_kernel(feeds, brick_cells, paired, blocks_ref, levels_ref, recv_ref, maps_ref, *refs):
+    if paired:
+        other_ref, out_ref, gram_ref = refs
+    else:
+        out_ref, gram_ref = refs
     step = pl.program_id(0)
+
+    @pl.when(step == 0)
+    def _():
+        gram_ref[...] = jnp.zeros(gram_ref.shape, gram_ref.dtype)
+
+    rows = out_ref.shape[0]
     for i in range(PER):
         brick = step * PER + i
         acc = None
@@ -35,39 +45,62 @@
             level = levels_ref[brick * feeds + n]
             part = jnp.dot(recv_ref[slot], maps_ref[level], preferred_element_type=jnp.float32)
             acc = part if acc is None else acc + part
-        out_ref[:, i * brick_cells : (i + 1) * brick_cells] = acc.astype(out_ref.dtype)
+        cols = slice(i * brick_cells, (i + 1) * brick_cells)
+        lifted = acc.astype(out_ref.dtype)
+        out_ref[:, cols] = lifted
+        contract = (((1,), (1,)), ((), ()))
+        if paired:
+            gram_ref[:, :rows] += lax.dot_general(
+                lifted, other_ref[:, cols], contract, preferred_element_type=jnp.float32
+            )
+            gram_ref[:, rows:] += lax.dot_general(
+                lifted, lifted, contract, preferred_element_type=jnp.float32
+            )
+        else:
+            gram_ref[...] += lax.dot_general(
+                lifted, lifted, contract, preferred_element_type=jnp.float32
+            )
 
 
-def lift(received, blocks, levels, maps):
+def lift(received, blocks, levels, maps, other=None):
     slots, rows, blk = received.shape
     bricks, feeds = blocks.shape
     brick_cells = maps.shape[2]
+    paired = other is not None
+    in_specs = [
+        pl.BlockSpec((slots, rows, blk), lambda s, b, l: (0, 0, 0)),
+        pl.BlockSpec(maps.shape, lambda s, b, l: (0, 0, 0)),
+    ]
+    operands = [received, maps]
+    gram_cols = rows
+    if paired:
+        in_specs.append(pl.BlockSpec((other.shape[0], PER * brick_cells), lambda s, b, l: (0, s)))
+        operands.append(other)
+        gram_cols = other.shape[0] + rows
     grid_spec = pltpu.PrefetchScalarGridSpec(
         num_scalar_prefetch=2,
         grid=(bricks // PER,),
-        in_specs=[
-            pl.BlockSpec((slots, rows, blk), lambda s, b, l: (0, 0, 0)),
-            pl.BlockSpec(maps.shape, lambda s, b, l: (0, 0, 0)),
+        in_specs=in_specs,
+        out_specs=[
+            pl.BlockSpec((rows, PER * brick_cells), lambda s, b, l: (0, s)),
+            pl.BlockSpec((rows, gram_cols), lambda s, b, l: (0, 0)),
         ],
-        out_specs=pl.BlockSpec((rows, PER * brick_cells), lambda s, b, l: (0, s)),
     )
-    flops = 2 * rows * blk * brick_cells * bricks * feeds
+    cells = bricks * brick_cells
+    flops = 2 * rows * blk * cells * feeds + 2 * rows * gram_cols * cells
     return pl.pallas_call(
-        functools.partial(lift_kernel, feeds, brick_cells),
+        functools.partial(lift_kernel, feeds, brick_cells, paired),
         grid_spec=grid_spec,
-        out_shape=jax.ShapeDtypeStruct((rows, bricks * brick_cells), jnp.bfloat16),
+        out_shape=[
+            jax.ShapeDtypeStruct((rows, cells), jnp.bfloat16),
+            jax.ShapeDtypeStruct((rows, gram_cols), jnp.float32),
+        ],
         cost_estimate=pl.CostEstimate(
             flops=flops,
-            bytes_accessed=received.size * 2 + maps.size * 2 + rows * bricks * brick_cells * 2,
+            bytes_accessed=received.size * 2 + maps.size * 2 + rows * cells * 2 * (2 if paired else 1),
             transcendentals=0,
         ),
-    )(blocks.reshape(-1), levels.reshape(-1), received, maps)
-
-
-def gram_of(left, right):
-    return lax.dot_general(
-        left, right, (((1,), (1,)), ((), ())), preferred_element_type=jnp.float32
-    )
+    )(blocks.reshape(-1), levels.reshape(-1), *operands)
 
 
 def body(cells, send_index, send_count, prolong_block, prolong_level, prolong_maps):
@@ -83,20 +116,21 @@
     head_in, tail_out = lax.optimization_barrier((head_in, tail_out))
     tail_in = lax.all_to_all(tail_out, "gy", split_axis=0, concat_axis=0, tiled=True)
     total_cells = lax.axis_size("gx") * lax.axis_size("gy") * prolong_block.shape[0] * prolong_maps.shape[2]
-    head = lift(head_in, prolong_block, prolong_level, prolong_maps)
-    c11 = all_sum(gram_of(head, head)) / total_cells
+    head, g11 = lift(head_in, prolong_block, prolong_level, prolong_maps)
+    c11 = all_sum(g11) / total_cells
     l11 = jnp.linalg.cholesky(c11)
     inv11 = lax.linalg.triangular_solve(
         l11, jnp.eye(kept, dtype=jnp.float32), left_side=True, lower=True
     )
-    inv_hi = inv11.astype(jnp.bfloat16)
-    inv_lo = (inv11 - inv_hi.astype(jnp.float32)).astype(jnp.bfloat16)
+    inv_top = lax.reduce_precision(inv11, exponent_bits=8, mantissa_bits=7)
+    inv_hi = inv_top.astype(jnp.bfloat16)
+    inv_lo = (inv11 - inv_top).astype(jnp.bfloat16)
     modes = jnp.dot(inv_hi, head, preferred_element_type=jnp.float32) + jnp.dot(
         inv_lo, head, preferred_element_type=jnp.float32
     )
     tail_in, modes, l11, inv11 = lax.optimization_barrier((tail_in, modes, l11, inv11))
-    tail = lift(tail_in, prolong_block, prolong_level, prolong_maps)
-    lower = all_sum(gram_of(tail, jnp.concatenate([head, tail], axis=0))) / total_cells
+    tail, g2 = lift(tail_in, prolong_block, prolong_level, prolong_maps, other=head)
+    lower = all_sum(g2) / total_cells
     c21, c22 = lower[:, :kept], lower[:, kept:]
     l21 = jnp.dot(c21, inv11.T, precision=lax.Precision.HIGHEST)
     schur = c22 - jnp.dot(l21, l21.T, precision=lax.Precision.HIGHEST)

time: 271 us -> 271 us (level)
  matrix products: 20.6 us -> 8.97 us
  Pallas kernels: 16.7 us -> 25.8 us
    dot_general x2 -> x0, matrix products: 11.7 us -> none  [gram_of(): lax.dot_general(left, right, (((1,), (1,)), ((), ())), preferred_element_...]
    pallas_call x2, Pallas kernels: 16.7 us -> 25.8 us  [lift(): pl.pallas_call(functools.partial(lift_kernel, feeds, brick_cells, paired)...]
  transfers between devices with their start and end apart: 17 -> 17, of which waited for: 16 -> 16; matrix products, arithmetic and copies ran while one was open for 14% -> 13% of each run, Pallas kernels for 3% -> 4%
where the time goes in v1:
time: 271 us; the launch traced here: 270 us
  waiting for transfers between devices  72.1 us (27%)
  blocking collectives  62.6 us (23%)
  starting transfers between devices  41.2 us (15%)
  other arithmetic  40.3 us (15%)
  Pallas kernels  25.8 us (10%)
  local copies, waits for them, and re-layouts  18.2 us (7%)
  matrix products  8.97 us (3%)
    ppermute x16, waiting for transfers between devices, from_partner(): return lax.ppermute(value, axis, pairs)  72.1 us
    all_to_all x1, blocking collectives, body(): lax.all_to_all(head_out, 'gy', split_axis=0, concat_axis=0, tiled=True)  62.6 us
    ppermute x16, starting transfers between devices, from_partner(): return lax.ppermute(value, axis, pairs)  36.2 us
    pallas_call x2, Pallas kernels, lift(): pl.pallas_call(functools.partial(lift_kernel, feeds, brick_cells, paired)...  25.8 us
    another operation x3, other arithmetic, body(): l11 = jnp.linalg.cholesky(c11)  12.4 us
    another operation x3, other arithmetic, body(): l22 = jnp.linalg.cholesky(schur)  12.4 us
    another operation x2, other arithmetic, body(): lax.linalg.triangular_solve(l11, jnp.eye(kept, dtype=jnp.float32), left_s...  10.5 us
    unnamed x12, local copies, waits for them, and re-layouts  6.4 us
  transfers between devices with their start and end apart: 17, of which 16 were waited for; matrix products, arithmetic and copies ran while one was open for 13% of the time, Pallas kernels for 4%

profile of v1, /device:TPU:6, one launch (start us, length us, event | category | flops | bytes accessed | tf_op | source)
XLA Modules:
  0.0 270.2 jit_solution(17560761640145716672)
XLA Ops:
  2.5 4.1 %copy.33 = bf16[256,4096]{0,1:T(8,128)(2,1)} copy(bf16[256,4096]{1,0:T(8,128)(2,1)} %param.7) | data formatting | bytes 4194304 | tf_op args[0]
  17.3 62.6 %all_to_all.10.recv_ref = bf16[64,128,128]{2,1,0:T(8,128)(2,1)} all-to-all(bf16[64,128,128]{2,1,0:T(8,128)(2,1)S(1)} %get-tuple-element.24), channel_id=1, replica_groups=mesh['gx'=8,'gy'=32] {'gy'}, dimensions={0} | all-to-all | bytes 4194304 | tf_op jit(solution)/shard_map/all_to_all | solution.py:115
  79.9 5.1 %all-to-all-start.1 = ((bf16[64,128,128]{2,1,0:T(8,128)(2,1)}), bf16[64,128,128]{2,1,0:T(8,128)(2,1)S(1)}, u32[]{:S(2)}, u32[]{:S(2)}) async-start(bf16[64,128,128]{2,1,0:T(8,128)(2,1)} %get-tuple-element.12), calls=%async_computation.1 | async-start | bytes 4194304 | tf_op jit(solution)/shard_map/all_to_all | solution.py:117
  86.5 11.6 %shard_map.77 = (bf16[128,16384]{1,0:T(8,128)(2,1)}, f32[128,128]{1,0:T(8,128)}) custom-call(s32[128]{0:T(128)} %reshape.83.blocks_ref, s32[128]{0:T(128)} %reshape.84.levels_ref, bf16[64,128,128]{2,1,0:T(8,128)(2,1)} %all_to_all.10.recv_ref, bf16[4,128,512]{2,1,0:T(8,128)(2,1)} %maps_ref.3), custom_call_target="tpu_custom_call" | custom-call | flops 2684354560 | bytes 6815744 | tf_op jit(solution)/shard_map/pallas_call | solution.py:91
  101.3 3.4 %collective-permute-done.1 = f32[128,128]{0,1:T(8,128)S(1)} collective-permute-done((f32[128,128]{0,1:T(8,128)S(1)}, f32[128,128]{0,1:T(8,128)S(1)}, u32[]{:S(2)}, u32[]{:S(2)}) %collective-permute-start.1) | collective-permute-done | bytes 65568 | tf_op jit(solution)/shard_map/ppermute | solution.py:18
  106.3 4.3 %collective-permute-done.2 = f32[128,128]{0,1:T(8,128)S(1)} collective-permute-done((f32[128,128]{0,1:T(8,128)S(1)}, f32[128,128]{0,1:T(8,128)S(1)}, u32[]{:S(2)}, u32[]{:S(2)}) %collective-permute-start.2) | collective-permute-done | bytes 65568 | tf_op jit(solution)/shard_map/ppermute | solution.py:18
  112.5 20.1 %collective-permute-done.3 = f32[128,128]{0,1:T(8,128)S(1)} collective-permute-done((f32[128,128]{0,1:T(8,128)S(1)}, f32[128,128]{0,1:T(8,128)S(1)}, u32[]{:S(2)}, u32[]{:S(2)}) %collective-permute-start.3) | collective-permute-done | bytes 65568 | tf_op jit(solution)/shard_map/ppermute | solution.py:18
  138.2 5.5 %collective-permute-start.5 = (f32[128,128]{0,1:T(8,128)S(1)}, f32[128,128]{0,1:T(8,128)S(1)}, u32[]{:S(2)}, u32[]{:S(2)}) collective-permute-start(f32[128,128]{0,1:T(8,128)S(1)} %add.91), channel_id=1, source_target_pairs={{0,4},{1,5},{2,6},{3,7},{4,0},{5,1},{6,2},{7,3},{8,12},{9,13},{10,... | collective-permute-start | bytes 196616 | tf_op jit(solution)/shard_map/ppermute | solution.py:18
  151.2 3.5 %collective-permute-start.7 = (f32[128,128]{0,1:T(8,128)S(1)}, f32[128,128]{0,1:T(8,128)S(1)}, u32[]{:S(2)}, u32[]{:S(2)}) collective-permute-start(f32[128,128]{0,1:T(8,128)S(1)} %add.93), channel_id=1, source_target_pairs={{0,16},{1,17},{2,18},{3,19},{4,20},{5,21},{6,22},{7,23},{8,24},{9,... | collective-permute-start | bytes 196616 | tf_op jit(solution)/shard_map/ppermute | solution.py:18
  157.3 11.7 %cholesky.44 = f32[128,128]{1,0:T(8,128)S(1)} custom-call(f32[128,128]{1,0:T(8,128)S(1)} %fusion.6), custom_call_target="Cholesky" | custom-call | tf_op jit(solution)/shard_map/jit(cholesky)/cholesky | solution.py:121
  170.4 9.8 %custom-call.5 = f32[1,128,128]{1,2,0:T(8,128)S(1)} custom-call(f32[1,128,128]{2,1,0:T(8,128)S(1)} %get-tuple-element.21), custom_call_target="InvertDiagBlocksLowerTriangular" | custom-call | tf_op jit(solution)/shard_map/triangular_solve | solution.py:122
  180.5 3.6 %fusion.8 = f32[128,16384]{1,0:T(8,128)S(1)} fusion(bf16[128,16384]{1,0:T(8,128)(2,1)} %get-tuple-element.15.refs_0_, f32[128,128]{1,0:T(8,128)S(1)} %fusion.4), kind=kOutput, calls=%fused_computation.26 | convolution fusion | flops 536903680 | bytes 12648448 | tf_op jit(solution)/shard_map/dot_general | solution.py:128
  184.1 4.6 %convolution_add_fusion = f32[128,16384]{1,0:T(8,128)} fusion(f32[128,16384]{1,0:T(8,128)S(1)} %fusion.8, bf16[128,16384]{1,0:T(8,128)(2,1)S(1)} %copy-done, f32[128,128]{1,0:T(8,128)S(1)} %fusion.4), kind=kOutput, calls=%fused_computation.1 | convolution fusion | flops 539017216 | bytes 21037056 | tf_op jit(solution)/shard_map/dot_general | solution.py:128
  190.1 14.2 %shard_map.78 = (bf16[128,16384]{1,0:T(8,128)(2,1)}, f32[128,256]{1,0:T(8,128)}) custom-call(s32[128]{0:T(128)} %reshape.83.blocks_ref, s32[128]{0:T(128)} %reshape.84.levels_ref, bf16[64,128,128]{2,1,0:T(8,128)(2,1)} %copy-done.1, bf16[4,128,512]{2,1,0:T(8,128)(2,1)} %maps_ref.3, bf16[128,16384]{1,0:T(8,128)(2,1)} %get-tuple-element.15.refs_0_), custom_call_target="tpu_custom_call" | custom-call | flops 3221225472 | bytes 11010048 | tf_op jit(solution)/shard_map/pallas_call | solution.py:91
  207.6 4.7 %collective-permute-done.9 = f32[128,256]{0,1:T(8,128)S(1)} collective-permute-done((f32[128,256]{0,1:T(8,128)S(1)}, f32[128,256]{0,1:T(8,128)S(1)}, u32[]{:S(2)}, u32[]{:S(2)}) %collective-permute-start.9) | collective-permute-done | bytes 131104 | tf_op jit(solution)/shard_map/ppermute | solution.py:18
  213.9 5.1 %collective-permute-done.10 = f32[128,256]{0,1:T(8,128)S(1)} collective-permute-done((f32[128,256]{0,1:T(8,128)S(1)}, f32[128,256]{0,1:T(8,128)S(1)}, u32[]{:S(2)}, u32[]{:S(2)}) %collective-permute-start.10) | collective-permute-done | bytes 131104 | tf_op jit(solution)/shard_map/ppermute | solution.py:18
  219.7 4.5 %collective-permute-done.11 = f32[128,256]{0,1:T(8,128)S(1)} collective-permute-done((f32[128,256]{0,1:T(8,128)S(1)}, f32[128,256]{0,1:T(8,128)S(1)}, u32[]{:S(2)}, u32[]{:S(2)}) %collective-permute-start.11) | collective-permute-done | bytes 131104 | tf_op jit(solution)/shard_map/ppermute | solution.py:18
  224.2 4.0 %collective-permute-start.12 = (f32[128,256]{0,1:T(8,128)S(1)}, f32[128,256]{0,1:T(8,128)S(1)}, u32[]{:S(2)}, u32[]{:S(2)}) collective-permute-start(f32[128,256]{0,1:T(8,128)S(1)} %add.99), channel_id=1, source_target_pairs={{0,2},{1,3},{2,0},{3,1},{4,6},{5,7},{6,4},{7,5},{8,10},{9,11},{10,... | collective-permute-start | bytes 393224 | tf_op jit(solution)/shard_map/ppermute | solution.py:18
  228.3 3.3 %collective-permute-done.12 = f32[128,256]{0,1:T(8,128)S(1)} collective-permute-done((f32[128,256]{0,1:T(8,128)S(1)}, f32[128,256]{0,1:T(8,128)S(1)}, u32[]{:S(2)}, u32[]{:S(2)}) %collective-permute-start.12) | collective-permute-done | bytes 131104 | tf_op jit(solution)/shard_map/ppermute | solution.py:18
  231.6 8.3 %collective-permute-start.13 = (f32[128,256]{0,1:T(8,128)S(1)}, f32[128,256]{0,1:T(8,128)S(1)}, u32[]{:S(2)}, u32[]{:S(2)}) collective-permute-start(f32[128,256]{0,1:T(8,128)S(1)} %add.100), channel_id=1, source_target_pairs={{0,4},{1,5},{2,6},{3,7},{4,0},{5,1},{6,2},{7,3},{8,12},{9,13},{10,... | collective-permute-start | bytes 393224 | tf_op jit(solution)/shard_map/ppermute | solution.py:18
  239.9 4.0 %collective-permute-done.13 = f32[128,256]{0,1:T(8,128)S(1)} collective-permute-done((f32[128,256]{0,1:T(8,128)S(1)}, f32[128,256]{0,1:T(8,128)S(1)}, u32[]{:S(2)}, u32[]{:S(2)}) %collective-permute-start.13) | collective-permute-done | bytes 131104 | tf_op jit(solution)/shard_map/ppermute | solution.py:18
  244.1 5.0 %collective-permute-done.14 = f32[128,256]{0,1:T(8,128)S(1)} collective-permute-done((f32[128,256]{0,1:T(8,128)S(1)}, f32[128,256]{0,1:T(8,128)S(1)}, u32[]{:S(2)}, u32[]{:S(2)}) %collective-permute-start.14) | collective-permute-done | bytes 131104 | tf_op jit(solution)/shard_map/ppermute | solution.py:18
  251.5 4.2 %collective-permute-done.15 = f32[128,256]{0,1:T(8,128)S(1)} collective-permute-done((f32[128,256]{0,1:T(8,128)S(1)}, f32[128,256]{0,1:T(8,128)S(1)}, u32[]{:S(2)}, u32[]{:S(2)}) %collective-permute-start.15) | collective-permute-done | bytes 131104 | tf_op jit(solution)/shard_map/ppermute | solution.py:18
  256.4 11.7 %cholesky.55 = f32[128,128]{1,0:T(8,128)S(1)} custom-call(f32[128,128]{1,0:T(8,128)S(1)} %fusion.3), custom_call_target="Cholesky" | custom-call | tf_op jit(solution)/shard_map/jit(cholesky)/cholesky | solution.py:137
  (76 shorter events, 50.2 us)
Async XLA Ops:
  17.3 67.7 %copy-start.2 = (s32[32,4]{0,1:T(4,128)S(1)}, s32[32,4]{0,1:T(4,128)}, u32[]{:S(2)}) copy-start(s32[32,4]{0,1:T(4,128)} %param.10) | copy-start | bytes 1540
  17.3 68.4 %copy-start.3 = (s32[32,4]{0,1:T(4,128)S(1)}, s32[32,4]{0,1:T(4,128)}, u32[]{:S(2)}) copy-start(s32[32,4]{0,1:T(4,128)} %param.11) | copy-start | bytes 1540
  79.9 108.8 %all-to-all-start.1 = ((bf16[64,128,128]{2,1,0:T(8,128)(2,1)}), bf16[64,128,128]{2,1,0:T(8,128)(2,1)S(1)}, u32[]{:S(2)}, u32[]{:S(2)}) async-start(bf16[64,128,128]{2,1,0:T(8,128)(2,1)} %get-tuple-element.12), calls=%async_computation.1 | async-start | bytes 4194304 | tf_op jit(solution)/shard_map/all_to_all | solution.py:117
  99.1 1.3 collective-permute-start
  100.4 4.4 %collective-permute-start.1 = (f32[128,128]{0,1:T(8,128)S(1)}, f32[128,128]{0,1:T(8,128)S(1)}, u32[]{:S(2)}, u32[]{:S(2)}) collective-permute-start(f32[128,128]{0,1:T(8,128)S(1)} %add.87), channel_id=1, source_target_pairs={{0,64},{32,96},{64,0},{96,32},{128,192},{160,224},{192,128},{224,1... | collective-permute-start | bytes 196616 | tf_op jit(solution)/shard_map/ppermute | solution.py:18
  104.8 5.9 %collective-permute-start.2 = (f32[128,128]{0,1:T(8,128)S(1)}, f32[128,128]{0,1:T(8,128)S(1)}, u32[]{:S(2)}, u32[]{:S(2)}) collective-permute-start(f32[128,128]{0,1:T(8,128)S(1)} %add.88), channel_id=1, source_target_pairs={{0,128},{32,160},{64,192},{96,224},{128,0},{160,32},{192,64},{224,... | collective-permute-start | bytes 196616 | tf_op jit(solution)/shard_map/ppermute | solution.py:18
  110.6 22.0 %collective-permute-start.3 = (f32[128,128]{0,1:T(8,128)S(1)}, f32[128,128]{0,1:T(8,128)S(1)}, u32[]{:S(2)}, u32[]{:S(2)}) collective-permute-start(f32[128,128]{0,1:T(8,128)S(1)} %add.89), channel_id=1, source_target_pairs={{0,1},{1,0},{2,3},{3,2},{4,5},{5,4},{6,7},{7,6},{8,9},{9,8},{10,11... | collective-permute-start | bytes 196616 | tf_op jit(solution)/shard_map/ppermute | solution.py:18
  132.6 5.5 %collective-permute-start.4 = (f32[128,128]{0,1:T(8,128)S(1)}, f32[128,128]{0,1:T(8,128)S(1)}, u32[]{:S(2)}, u32[]{:S(2)}) collective-permute-start(f32[128,128]{0,1:T(8,128)S(1)} %add.90), channel_id=1, source_target_pairs={{0,2},{1,3},{2,0},{3,1},{4,6},{5,7},{6,4},{7,5},{8,10},{9,11},{10,... | collective-permute-start | bytes 196616 | tf_op jit(solution)/shard_map/ppermute | solution.py:18
  138.2 8.4 %collective-permute-start.5 = (f32[128,128]{0,1:T(8,128)S(1)}, f32[128,128]{0,1:T(8,128)S(1)}, u32[]{:S(2)}, u32[]{:S(2)}) collective-permute-start(f32[128,128]{0,1:T(8,128)S(1)} %add.91), channel_id=1, source_target_pairs={{0,4},{1,5},{2,6},{3,7},{4,0},{5,1},{6,2},{7,3},{8,12},{9,13},{10,... | collective-permute-start | bytes 196616 | tf_op jit(solution)/shard_map/ppermute | solution.py:18
  146.6 4.6 %collective-permute-start.6 = (f32[128,128]{0,1:T(8,128)S(1)}, f32[128,128]{0,1:T(8,128)S(1)}, u32[]{:S(2)}, u32[]{:S(2)}) collective-permute-start(f32[128,128]{0,1:T(8,128)S(1)} %add.92), channel_id=1, source_target_pairs={{0,8},{1,9},{2,10},{3,11},{4,12},{5,13},{6,14},{7,15},{8,0},{9,1},... | collective-permute-start | bytes 196616 | tf_op jit(solution)/shard_map/ppermute | solution.py:18
  151.2 6.0 %collective-permute-start.7 = (f32[128,128]{0,1:T(8,128)S(1)}, f32[128,128]{0,1:T(8,128)S(1)}, u32[]{:S(2)}, u32[]{:S(2)}) collective-permute-start(f32[128,128]{0,1:T(8,128)S(1)} %add.93), channel_id=1, source_target_pairs={{0,16},{1,17},{2,18},{3,19},{4,20},{5,21},{6,22},{7,23},{8,24},{9,... | collective-permute-start | bytes 196616 | tf_op jit(solution)/shard_map/ppermute | solution.py:18
  180.5 3.6 %copy-start = (bf16[128,16384]{1,0:T(8,128)(2,1)S(1)}, bf16[128,16384]{1,0:T(8,128)(2,1)}, u32[]{:S(2)}) copy-start(bf16[128,16384]{1,0:T(8,128)(2,1)} %get-tuple-element.15.refs_0_) | copy-start | bytes 12582916
  188.7 1.4 copy-start.1
  205.3 1.4 collective-permute-start.8
  206.7 5.6 %collective-permute-start.9 = (f32[128,256]{0,1:T(8,128)S(1)}, f32[128,256]{0,1:T(8,128)S(1)}, u32[]{:S(2)}, u32[]{:S(2)}) collective-permute-start(f32[128,256]{0,1:T(8,128)S(1)} %add.96), channel_id=1, source_target_pairs={{0,64},{32,96},{64,0},{96,32},{128,192},{160,224},{192,128},{224,1... | collective-permute-start | bytes 393224 | tf_op jit(solution)/shard_map/ppermute | solution.py:18
  212.4 6.6 %collective-permute-start.10 = (f32[128,256]{0,1:T(8,128)S(1)}, f32[128,256]{0,1:T(8,128)S(1)}, u32[]{:S(2)}, u32[]{:S(2)}) collective-permute-start(f32[128,256]{0,1:T(8,128)S(1)} %add.97), channel_id=1, source_target_pairs={{0,128},{32,160},{64,192},{96,224},{128,0},{160,32},{192,64},{224,... | collective-permute-start | bytes 393224 | tf_op jit(solution)/shard_map/ppermute | solution.py:18
  219.0 5.3 %collective-permute-start.11 = (f32[128,256]{0,1:T(8,128)S(1)}, f32[128,256]{0,1:T(8,128)S(1)}, u32[]{:S(2)}, u32[]{:S(2)}) collective-permute-start(f32[128,256]{0,1:T(8,128)S(1)} %add.98), channel_id=1, source_target_pairs={{0,1},{1,0},{2,3},{3,2},{4,5},{5,4},{6,7},{7,6},{8,9},{9,8},{10,11... | collective-permute-start | bytes 393224 | tf_op jit(solution)/shard_map/ppermute | solution.py:18
  224.2 7.3 %collective-permute-start.12 = (f32[128,256]{0,1:T(8,128)S(1)}, f32[128,256]{0,1:T(8,128)S(1)}, u32[]{:S(2)}, u32[]{:S(2)}) collective-permute-start(f32[128,256]{0,1:T(8,128)S(1)} %add.99), channel_id=1, source_target_pairs={{0,2},{1,3},{2,0},{3,1},{4,6},{5,7},{6,4},{7,5},{8,10},{9,11},{10,... | collective-permute-start | bytes 393224 | tf_op jit(solution)/shard_map/ppermute | solution.py:18
  231.6 12.4 %collective-permute-start.13 = (f32[128,256]{0,1:T(8,128)S(1)}, f32[128,256]{0,1:T(8,128)S(1)}, u32[]{:S(2)}, u32[]{:S(2)}) collective-permute-start(f32[128,256]{0,1:T(8,128)S(1)} %add.100), channel_id=1, source_target_pairs={{0,4},{1,5},{2,6},{3,7},{4,0},{5,1},{6,2},{7,3},{8,12},{9,13},{10,... | collective-permute-start | bytes 393224 | tf_op jit(solution)/shard_map/ppermute | solution.py:18
  244.0 5.1 %collective-permute-start.14 = (f32[128,256]{0,1:T(8,128)S(1)}, f32[128,256]{0,1:T(8,128)S(1)}, u32[]{:S(2)}, u32[]{:S(2)}) collective-permute-start(f32[128,256]{0,1:T(8,128)S(1)} %add.101), channel_id=1, source_target_pairs={{0,8},{1,9},{2,10},{3,11},{4,12},{5,13},{6,14},{7,15},{8,0},{9,1},... | collective-permute-start | bytes 393224 | tf_op jit(solution)/shard_map/ppermute | solution.py:18
  249.1 6.6 %collective-permute-start.15 = (f32[128,256]{0,1:T(8,128)S(1)}, f32[128,256]{0,1:T(8,128)S(1)}, u32[]{:S(2)}, u32[]{:S(2)}) collective-permute-start(f32[128,256]{0,1:T(8,128)S(1)} %add.102), channel_id=1, source_target_pairs={{0,16},{1,17},{2,18},{3,19},{4,20},{5,21},{6,22},{7,23},{8,24},{9,... | collective-permute-start | bytes 393224 | tf_op jit(solution)/shard_map/ppermute | solution.py:18

commit v2 on v1

--- a/solution.py
+++ b/solution.py
@@ -119,6 +119,9 @@
     head, g11 = lift(head_in, prolong_block, prolong_level, prolong_maps)
     c11 = all_sum(g11) / total_cells
     l11 = jnp.linalg.cholesky(c11)
+    tail_in, l11, head = lax.optimization_barrier((tail_in, l11, head))
+    tail, g2 = lift(tail_in, prolong_block, prolong_level, prolong_maps, other=head)
+    g2, l11, head = lax.optimization_barrier((g2, l11, head))
     inv11 = lax.linalg.triangular_solve(
         l11, jnp.eye(kept, dtype=jnp.float32), left_side=True, lower=True
     )
@@ -128,8 +131,6 @@
     modes = jnp.dot(inv_hi, head, preferred_element_type=jnp.float32) + jnp.dot(
         inv_lo, head, preferred_element_type=jnp.float32
     )
-    tail_in, modes, l11, inv11 = lax.optimization_barrier((tail_in, modes, l11, inv11))
-    tail, g2 = lift(tail_in, prolong_block, prolong_level, prolong_maps, other=head)
     lower = all_sum(g2) / total_cells
     c21, c22 = lower[:, :kept], lower[:, kept:]
     l21 = jnp.dot(c21, inv11.T, precision=lax.Precision.HIGHEST)

time: 271 us -> 256 us (0.945)
  waiting for transfers between devices: 72.1 us -> 63.7 us
  starting transfers between devices: 41.2 us -> 35.4 us
    ppermute x16, waiting for transfers between devices: 72.1 us -> 63.7 us  [from_partner(): return lax.ppermute(value, axis, pairs)]
    ppermute x16, starting transfers between devices: 36.2 us -> 30.3 us  [from_partner(): return lax.ppermute(value, axis, pairs)]
    unnamed x12 -> x14, local copies, waits for them, and re-layouts: 6.4 us -> 6.36 us
  transfers between devices with their start and end apart: 17 -> 17, of which waited for: 16 -> 14; matrix products, arithmetic and copies ran while one was open for 13% -> 13% of each run, Pallas kernels for 4% -> 5%
where the time goes in v2:
time: 256 us; the launch traced here: 255 us
  waiting for transfers between devices  63.7 us (25%)
  blocking collectives  62.6 us (24%)
  other arithmetic  39.6 us (15%)
  starting transfers between devices  35.4 us (14%)
  Pallas kernels  25.8 us (10%)
  local copies, waits for them, and re-layouts  18.2 us (7%)
  matrix products  9 us (4%)
    ppermute x16, waiting for transfers between devices, from_partner(): return lax.ppermute(value, axis, pairs)  63.7 us
    all_to_all x1, blocking collectives, body(): lax.all_to_all(head_out, 'gy', split_axis=0, concat_axis=0, tiled=True)  62.6 us
    ppermute x16, starting transfers between devices, from_partner(): return lax.ppermute(value, axis, pairs)  30.3 us
    pallas_call x2, Pallas kernels, lift(): pl.pallas_call(functools.partial(lift_kernel, feeds, brick_cells, paired)...  25.8 us
    another operation x3, other arithmetic, body(): l11 = jnp.linalg.cholesky(c11)  12.4 us
    another operation x3, other arithmetic, body(): l22 = jnp.linalg.cholesky(schur)  12.4 us
    another operation x2, other arithmetic, body(): lax.linalg.triangular_solve(l11, jnp.eye(kept, dtype=jnp.float32), left_s...  9.82 us
    unnamed x14, local copies, waits for them, and re-layouts  6.36 us
  transfers between devices with their start and end apart: 17, of which 14 were waited for; matrix products, arithmetic and copies ran while one was open for 13% of the time, Pallas kernels for 5%

profile of v2, /device:TPU:6, one launch (start us, length us, event | category | flops | bytes accessed | tf_op | source)
XLA Modules:
  0.0 255.3 jit_solution(11873911374373370244)
XLA Ops:
  1.6 4.1 %copy.35 = bf16[256,4096]{0,1:T(8,128)(2,1)} copy(bf16[256,4096]{1,0:T(8,128)(2,1)} %param.7) | data formatting | bytes 4194304 | tf_op args[0]
  5.7 3.2 %copy.36 = bf16[256,32,128]{2,0,1:T(8,128)(2,1)S(1)} copy(bf16[256,32,128]{0,2,1:T(8,128)(2,1)} %bitcast.23) | data formatting | bytes 4194304 | tf_op jit(solution)/shard_map/reshape | solution.py:109
  9.2 3.1 %gather_fusion = bf16[64,256,128]{2,1,0:T(8,128)(2,1)} fusion(bf16[32,256,128]{2,1,0:T(8,128)(2,1)S(1)} %bitcast.22, s32[1024]{0:T(1024)S(1)} %pad_clamp_fusion), kind=kCustom, calls=%fused_computation | custom fusion | bytes 8388864 | tf_op jit(solution)/shard_map/jit(_take)/gather | solution.py:112
  16.7 62.6 %all_to_all.10.recv_ref = bf16[64,128,128]{2,1,0:T(8,128)(2,1)} all-to-all(bf16[64,128,128]{2,1,0:T(8,128)(2,1)S(1)} %get-tuple-element.26), channel_id=1, replica_groups=mesh['gx'=8,'gy'=32] {'gy'}, dimensions={0} | all-to-all | bytes 4194304 | tf_op jit(solution)/shard_map/all_to_all | solution.py:115
  79.3 5.1 %all-to-all-start.1 = ((bf16[64,128,128]{2,1,0:T(8,128)(2,1)}), bf16[64,128,128]{2,1,0:T(8,128)(2,1)S(1)}, u32[]{:S(2)}, u32[]{:S(2)}) async-start(bf16[64,128,128]{2,1,0:T(8,128)(2,1)} %get-tuple-element.14), calls=%async_computation.1 | async-start | bytes 4194304 | tf_op jit(solution)/shard_map/all_to_all | solution.py:117
  85.8 11.6 %shard_map.77 = (bf16[128,16384]{1,0:T(8,128)(2,1)}, f32[128,128]{1,0:T(8,128)}) custom-call(s32[128]{0:T(128)} %reshape.80.blocks_ref, s32[128]{0:T(128)} %reshape.81.levels_ref, bf16[64,128,128]{2,1,0:T(8,128)(2,1)} %all_to_all.10.recv_ref, bf16[4,128,512]{2,1,0:T(8,128)(2,1)} %maps_ref.3), custom_call_target="tpu_custom_call" | custom-call | flops 2684354560 | bytes 6815744 | tf_op jit(solution)/shard_map/pallas_call | solution.py:91
  100.6 3.4 %collective-permute-done.1 = f32[128,128]{0,1:T(8,128)S(1)} collective-permute-done((f32[128,128]{0,1:T(8,128)S(1)}, f32[128,128]{0,1:T(8,128)S(1)}, u32[]{:S(2)}, u32[]{:S(2)}) %collective-permute-start.1) | collective-permute-done | bytes 65568 | tf_op jit(solution)/shard_map/ppermute | solution.py:18
  105.6 4.4 %collective-permute-done.2 = f32[128,128]{0,1:T(8,128)S(1)} collective-permute-done((f32[128,128]{0,1:T(8,128)S(1)}, f32[128,128]{0,1:T(8,128)S(1)}, u32[]{:S(2)}, u32[]{:S(2)}) %collective-permute-start.2) | collective-permute-done | bytes 65568 | tf_op jit(solution)/shard_map/ppermute | solution.py:18
  111.8 20.2 %collective-permute-done.3 = f32[128,128]{0,1:T(8,128)S(1)} collective-permute-done((f32[128,128]{0,1:T(8,128)S(1)}, f32[128,128]{0,1:T(8,128)S(1)}, u32[]{:S(2)}, u32[]{:S(2)}) %collective-permute-start.3) | collective-permute-done | bytes 65568 | tf_op jit(solution)/shard_map/ppermute | solution.py:18
  134.5 3.1 %collective-permute-done.4 = f32[128,128]{0,1:T(8,128)S(1)} collective-permute-done((f32[128,128]{0,1:T(8,128)S(1)}, f32[128,128]{0,1:T(8,128)S(1)}, u32[]{:S(2)}, u32[]{:S(2)}) %collective-permute-start.4) | collective-permute-done | bytes 65568 | tf_op jit(solution)/shard_map/ppermute | solution.py:18
  137.5 5.5 %collective-permute-start.5 = (f32[128,128]{0,1:T(8,128)S(1)}, f32[128,128]{0,1:T(8,128)S(1)}, u32[]{:S(2)}, u32[]{:S(2)}) collective-permute-start(f32[128,128]{0,1:T(8,128)S(1)} %add.91), channel_id=1, source_target_pairs={{0,4},{1,5},{2,6},{3,7},{4,0},{5,1},{6,2},{7,3},{8,12},{9,13},{10,... | collective-permute-start | bytes 196616 | tf_op jit(solution)/shard_map/ppermute | solution.py:18
  143.1 2.8 %collective-permute-done.5 = f32[128,128]{0,1:T(8,128)S(1)} collective-permute-done((f32[128,128]{0,1:T(8,128)S(1)}, f32[128,128]{0,1:T(8,128)S(1)}, u32[]{:S(2)}, u32[]{:S(2)}) %collective-permute-start.5) | collective-permute-done | bytes 65568 | tf_op jit(solution)/shard_map/ppermute | solution.py:18
  150.5 3.5 %collective-permute-start.7 = (f32[128,128]{0,1:T(8,128)S(1)}, f32[128,128]{0,1:T(8,128)S(1)}, u32[]{:S(2)}, u32[]{:S(2)}) collective-permute-start(f32[128,128]{0,1:T(8,128)S(1)} %add.93), channel_id=1, source_target_pairs={{0,16},{1,17},{2,18},{3,19},{4,20},{5,21},{6,22},{7,23},{8,24},{9,... | collective-permute-start | bytes 196616 | tf_op jit(solution)/shard_map/ppermute | solution.py:18
  156.7 11.7 %cholesky.44 = f32[128,128]{1,0:T(8,128)S(1)} custom-call(f32[128,128]{1,0:T(8,128)S(1)} %fusion.6), custom_call_target="Cholesky" | custom-call | tf_op jit(solution)/shard_map/jit(cholesky)/cholesky | solution.py:121
  171.1 14.2 %shard_map.78 = (bf16[128,16384]{1,0:T(8,128)(2,1)}, f32[128,256]{1,0:T(8,128)}) custom-call(s32[128]{0:T(128)} %reshape.80.blocks_ref, s32[128]{0:T(128)} %reshape.81.levels_ref, bf16[64,128,128]{2,1,0:T(8,128)(2,1)} %copy-done.1, bf16[4,128,512]{2,1,0:T(8,128)(2,1)} %maps_ref.3, bf16[128,16384]{1,0:T(8,128)(2,1)} %get-tuple-element.24.refs_0_), custom_call_target="tpu_custom_call" | custom-call | flops 3221225472 | bytes 11010048 | tf_op jit(solution)/shard_map/pallas_call | solution.py:91
  188.7 4.7 %collective-permute-done.9 = f32[128,256]{0,1:T(8,128)S(1)} collective-permute-done((f32[128,256]{0,1:T(8,128)S(1)}, f32[128,256]{0,1:T(8,128)S(1)}, u32[]{:S(2)}, u32[]{:S(2)}) %collective-permute-start.9) | collective-permute-done | bytes 131104 | tf_op jit(solution)/shard_map/ppermute | solution.py:18
  194.9 5.1 %collective-permute-done.10 = f32[128,256]{0,1:T(8,128)S(1)} collective-permute-done((f32[128,256]{0,1:T(8,128)S(1)}, f32[128,256]{0,1:T(8,128)S(1)}, u32[]{:S(2)}, u32[]{:S(2)}) %collective-permute-start.10) | collective-permute-done | bytes 131104 | tf_op jit(solution)/shard_map/ppermute | solution.py:18
  200.5 4.5 %collective-permute-done.11 = f32[128,256]{0,1:T(8,128)S(1)} collective-permute-done((f32[128,256]{0,1:T(8,128)S(1)}, f32[128,256]{0,1:T(8,128)S(1)}, u32[]{:S(2)}, u32[]{:S(2)}) %collective-permute-start.11) | collective-permute-done | bytes 131104 | tf_op jit(solution)/shard_map/ppermute | solution.py:18
  205.1 4.0 %collective-permute-start.12 = (f32[128,256]{0,1:T(8,128)S(1)}, f32[128,256]{0,1:T(8,128)S(1)}, u32[]{:S(2)}, u32[]{:S(2)}) collective-permute-start(f32[128,256]{0,1:T(8,128)S(1)} %add.98), channel_id=1, source_target_pairs={{0,2},{1,3},{2,0},{3,1},{4,6},{5,7},{6,4},{7,5},{8,10},{9,11},{10,... | collective-permute-start | bytes 393224 | tf_op jit(solution)/shard_map/ppermute | solution.py:18
  209.1 9.8 %custom-call.5 = f32[1,128,128]{1,2,0:T(8,128)S(1)} custom-call(f32[1,128,128]{2,1,0:T(8,128)S(1)} %fusion.8), custom_call_target="InvertDiagBlocksLowerTriangular" | custom-call | tf_op jit(solution)/shard_map/triangular_solve | solution.py:125
  220.7 7.2 %collective-permute-done.13 = f32[128,256]{0,1:T(8,128)S(1)} collective-permute-done((f32[128,256]{0,1:T(8,128)S(1)}, f32[128,256]{0,1:T(8,128)S(1)}, u32[]{:S(2)}, u32[]{:S(2)}) %collective-permute-start.13) | collective-permute-done | bytes 131104 | tf_op jit(solution)/shard_map/ppermute | solution.py:18
  229.0 3.6 %fusion.10 = f32[128,16384]{1,0:T(8,128)S(1)} fusion(bf16[128,16384]{1,0:T(8,128)(2,1)} %get-tuple-element.24.refs_0_, f32[128,128]{1,0:T(8,128)S(1)} %fusion.4), kind=kOutput, calls=%fused_computation.27 | convolution fusion | flops 536903680 | bytes 12648448 | tf_op jit(solution)/shard_map/dot_general | solution.py:131
  236.1 4.6 %convolution_add_fusion = f32[128,16384]{1,0:T(8,128)} fusion(f32[128,16384]{1,0:T(8,128)S(1)} %fusion.10, bf16[128,16384]{1,0:T(8,128)(2,1)S(1)} %copy-done, f32[128,128]{1,0:T(8,128)S(1)} %fusion.4), kind=kOutput, calls=%fused_computation.1 | convolution fusion | flops 539017216 | bytes 21037056 | tf_op jit(solution)/shard_map/dot_general | solution.py:131
  241.5 11.7 %cholesky.55 = f32[128,128]{1,0:T(8,128)S(1)} custom-call(f32[128,128]{1,0:T(8,128)S(1)} %fusion.3), custom_call_target="Cholesky" | custom-call | tf_op jit(solution)/shard_map/jit(cholesky)/cholesky | solution.py:138
  (79 shorter events, 40.5 us)
Async XLA Ops:
  1.6 7.3 %copy-start.4 = (s32[32]{0:T(128)S(1)}, s32[32]{0:T(128)}, u32[]{:S(2)}) copy-start(s32[32]{0:T(128)} %param.9) | copy-start | bytes 388
  16.7 67.7 %copy-start.2 = (s32[32,4]{0,1:T(4,128)S(1)}, s32[32,4]{0,1:T(4,128)}, u32[]{:S(2)}) copy-start(s32[32,4]{0,1:T(4,128)} %param.10) | copy-start | bytes 1540
  16.7 68.4 %copy-start.3 = (s32[32,4]{0,1:T(4,128)S(1)}, s32[32,4]{0,1:T(4,128)}, u32[]{:S(2)}) copy-start(s32[32,4]{0,1:T(4,128)} %param.11) | copy-start | bytes 1540
  79.3 90.5 %all-to-all-start.1 = ((bf16[64,128,128]{2,1,0:T(8,128)(2,1)}), bf16[64,128,128]{2,1,0:T(8,128)(2,1)S(1)}, u32[]{:S(2)}, u32[]{:S(2)}) async-start(bf16[64,128,128]{2,1,0:T(8,128)(2,1)} %get-tuple-element.14), calls=%async_computation.1 | async-start | bytes 4194304 | tf_op jit(solution)/shard_map/all_to_all | solution.py:117
  98.3 1.3 collective-permute-start
  99.7 4.4 %collective-permute-start.1 = (f32[128,128]{0,1:T(8,128)S(1)}, f32[128,128]{0,1:T(8,128)S(1)}, u32[]{:S(2)}, u32[]{:S(2)}) collective-permute-start(f32[128,128]{0,1:T(8,128)S(1)} %add.87), channel_id=1, source_target_pairs={{0,64},{32,96},{64,0},{96,32},{128,192},{160,224},{192,128},{224,1... | collective-permute-start | bytes 196616 | tf_op jit(solution)/shard_map/ppermute | solution.py:18
  104.1 5.9 %collective-permute-start.2 = (f32[128,128]{0,1:T(8,128)S(1)}, f32[128,128]{0,1:T(8,128)S(1)}, u32[]{:S(2)}, u32[]{:S(2)}) collective-permute-start(f32[128,128]{0,1:T(8,128)S(1)} %add.88), channel_id=1, source_target_pairs={{0,128},{32,160},{64,192},{96,224},{128,0},{160,32},{192,64},{224,... | collective-permute-start | bytes 196616 | tf_op jit(solution)/shard_map/ppermute | solution.py:18
  109.9 22.1 %collective-permute-start.3 = (f32[128,128]{0,1:T(8,128)S(1)}, f32[128,128]{0,1:T(8,128)S(1)}, u32[]{:S(2)}, u32[]{:S(2)}) collective-permute-start(f32[128,128]{0,1:T(8,128)S(1)} %add.89), channel_id=1, source_target_pairs={{0,1},{1,0},{2,3},{3,2},{4,5},{5,4},{6,7},{7,6},{8,9},{9,8},{10,11... | collective-permute-start | bytes 196616 | tf_op jit(solution)/shard_map/ppermute | solution.py:18
  132.0 5.5 %collective-permute-start.4 = (f32[128,128]{0,1:T(8,128)S(1)}, f32[128,128]{0,1:T(8,128)S(1)}, u32[]{:S(2)}, u32[]{:S(2)}) collective-permute-start(f32[128,128]{0,1:T(8,128)S(1)} %add.90), channel_id=1, source_target_pairs={{0,2},{1,3},{2,0},{3,1},{4,6},{5,7},{6,4},{7,5},{8,10},{9,11},{10,... | collective-permute-start | bytes 196616 | tf_op jit(solution)/shard_map/ppermute | solution.py:18
  137.5 8.4 %collective-permute-start.5 = (f32[128,128]{0,1:T(8,128)S(1)}, f32[128,128]{0,1:T(8,128)S(1)}, u32[]{:S(2)}, u32[]{:S(2)}) collective-permute-start(f32[128,128]{0,1:T(8,128)S(1)} %add.91), channel_id=1, source_target_pairs={{0,4},{1,5},{2,6},{3,7},{4,0},{5,1},{6,2},{7,3},{8,12},{9,13},{10,... | collective-permute-start | bytes 196616 | tf_op jit(solution)/shard_map/ppermute | solution.py:18
  145.9 4.6 %collective-permute-start.6 = (f32[128,128]{0,1:T(8,128)S(1)}, f32[128,128]{0,1:T(8,128)S(1)}, u32[]{:S(2)}, u32[]{:S(2)}) collective-permute-start(f32[128,128]{0,1:T(8,128)S(1)} %add.92), channel_id=1, source_target_pairs={{0,8},{1,9},{2,10},{3,11},{4,12},{5,13},{6,14},{7,15},{8,0},{9,1},... | collective-permute-start | bytes 196616 | tf_op jit(solution)/shard_map/ppermute | solution.py:18
  150.5 6.0 %collective-permute-start.7 = (f32[128,128]{0,1:T(8,128)S(1)}, f32[128,128]{0,1:T(8,128)S(1)}, u32[]{:S(2)}, u32[]{:S(2)}) collective-permute-start(f32[128,128]{0,1:T(8,128)S(1)} %add.93), channel_id=1, source_target_pairs={{0,16},{1,17},{2,18},{3,19},{4,20},{5,21},{6,22},{7,23},{8,24},{9,... | collective-permute-start | bytes 196616 | tf_op jit(solution)/shard_map/ppermute | solution.py:18
  169.8 1.3 copy-start.1
  186.3 1.4 collective-permute-start.8
  187.8 5.6 %collective-permute-start.9 = (f32[128,256]{0,1:T(8,128)S(1)}, f32[128,256]{0,1:T(8,128)S(1)}, u32[]{:S(2)}, u32[]{:S(2)}) collective-permute-start(f32[128,256]{0,1:T(8,128)S(1)} %add.95), channel_id=1, source_target_pairs={{0,64},{32,96},{64,0},{96,32},{128,192},{160,224},{192,128},{224,1... | collective-permute-start | bytes 393224 | tf_op jit(solution)/shard_map/ppermute | solution.py:18
  193.4 6.6 %collective-permute-start.10 = (f32[128,256]{0,1:T(8,128)S(1)}, f32[128,256]{0,1:T(8,128)S(1)}, u32[]{:S(2)}, u32[]{:S(2)}) collective-permute-start(f32[128,256]{0,1:T(8,128)S(1)} %add.96), channel_id=1, source_target_pairs={{0,128},{32,160},{64,192},{96,224},{128,0},{160,32},{192,64},{224,... | collective-permute-start | bytes 393224 | tf_op jit(solution)/shard_map/ppermute | solution.py:18
  200.0 5.1 %collective-permute-start.11 = (f32[128,256]{0,1:T(8,128)S(1)}, f32[128,256]{0,1:T(8,128)S(1)}, u32[]{:S(2)}, u32[]{:S(2)}) collective-permute-start(f32[128,256]{0,1:T(8,128)S(1)} %add.97), channel_id=1, source_target_pairs={{0,1},{1,0},{2,3},{3,2},{4,5},{5,4},{6,7},{7,6},{8,9},{9,8},{10,11... | collective-permute-start | bytes 393224 | tf_op jit(solution)/shard_map/ppermute | solution.py:18
  205.1 13.8 %collective-permute-start.12 = (f32[128,256]{0,1:T(8,128)S(1)}, f32[128,256]{0,1:T(8,128)S(1)}, u32[]{:S(2)}, u32[]{:S(2)}) collective-permute-start(f32[128,256]{0,1:T(8,128)S(1)} %add.98), channel_id=1, source_target_pairs={{0,2},{1,3},{2,0},{3,1},{4,6},{5,7},{6,4},{7,5},{8,10},{9,11},{10,... | collective-permute-start | bytes 393224 | tf_op jit(solution)/shard_map/ppermute | solution.py:18
  218.9 9.0 %collective-permute-start.13 = (f32[128,256]{0,1:T(8,128)S(1)}, f32[128,256]{0,1:T(8,128)S(1)}, u32[]{:S(2)}, u32[]{:S(2)}) collective-permute-start(f32[128,256]{0,1:T(8,128)S(1)} %add.99), channel_id=1, source_target_pairs={{0,4},{1,5},{2,6},{3,7},{4,0},{5,1},{6,2},{7,3},{8,12},{9,13},{10,... | collective-permute-start | bytes 393224 | tf_op jit(solution)/shard_map/ppermute | solution.py:18
  227.9 8.2 %copy-start = (bf16[128,16384]{1,0:T(8,128)(2,1)S(1)}, bf16[128,16384]{1,0:T(8,128)(2,1)}, u32[]{:S(2)}) copy-start(bf16[128,16384]{1,0:T(8,128)(2,1)} %get-tuple-element.24.refs_0_) | copy-start | bytes 12582916
  227.9 5.4 %collective-permute-start.14 = (f32[128,256]{0,1:T(8,128)S(1)}, f32[128,256]{0,1:T(8,128)S(1)}, u32[]{:S(2)}, u32[]{:S(2)}) collective-permute-start(f32[128,256]{0,1:T(8,128)S(1)} %add.100), channel_id=1, source_target_pairs={{0,8},{1,9},{2,10},{3,11},{4,12},{5,13},{6,14},{7,15},{8,0},{9,1},... | collective-permute-start | bytes 393224 | tf_op jit(solution)/shard_map/ppermute | solution.py:18
  233.4 7.3 %collective-permute-start.15 = (f32[128,256]{0,1:T(8,128)S(1)}, f32[128,256]{0,1:T(8,128)S(1)}, u32[]{:S(2)}, u32[]{:S(2)}) collective-permute-start(f32[128,256]{0,1:T(8,128)S(1)} %add.101), channel_id=1, source_target_pairs={{0,16},{1,17},{2,18},{3,19},{4,20},{5,21},{6,22},{7,23},{8,24},{9,... | collective-permute-start | bytes 393224 | tf_op jit(solution)/shard_map/ppermute | solution.py:18

commit v3 on v2

--- a/solution.py
+++ b/solution.py
@@ -103,15 +103,56 @@
     )(blocks.reshape(-1), levels.reshape(-1), *operands)
 
 
+def gather_kernel(rows, index_ref, live_ref, cells_ref, head_ref, tail_ref, sems):
+    count = head_ref.shape[0]
+    blk = head_ref.shape[2]
+    copies = []
+    for k in range(count):
+        start = pl.multiple_of(index_ref[k] * blk, blk)
+        for part, dst in enumerate((head_ref, tail_ref)):
+            copy = pltpu.make_async_copy(
+                cells_ref.at[pl.ds(part * rows, rows), pl.ds(start, blk)],
+                dst.at[k],
+                sems.at[part, k],
+            )
+            copy.start()
+            copies.append(copy)
+    for copy in copies:
+        copy.wait()
+    for k in range(count):
+        keep = live_ref[k] > 0
+        for dst in (head_ref, tail_ref):
+            dst[k] = jnp.where(keep, dst[k], jnp.zeros_like(dst[k]))
+
+
+def gather(cells, index, live, rows):
+    count = index.shape[0]
+    out = jax.ShapeDtypeStruct((count, rows, BLK), cells.dtype)
+    return pl.pallas_call(
+        functools.partial(gather_kernel, rows),
+        out_shape=[out, out],
+        in_specs=[
+            pl.BlockSpec(memory_space=pltpu.SMEM),
+            pl.BlockSpec(memory_space=pltpu.SMEM),
+            pl.BlockSpec(memory_space=pl.ANY),
+        ],
+        out_specs=[
+            pl.BlockSpec(memory_space=pltpu.VMEM),
+            pl.BlockSpec(memory_space=pltpu.VMEM),
+        ],
+        scratch_shapes=[pltpu.SemaphoreType.DMA((2, count))],
+        cost_estimate=pl.CostEstimate(
+            flops=0, bytes_accessed=4 * count * rows * BLK * 2, transcendentals=0
+        ),
+    )(index, live, cells)
+
+
 def body(cells, send_index, send_count, prolong_block, prolong_level, prolong_maps):
     snaps = cells.shape[0]
     kept = RANK
-    local = cells.reshape(snaps, -1, BLK).transpose(1, 0, 2)
     peers, slots = send_index.shape
     live = (jnp.arange(slots, dtype=jnp.int32)[None, :] < send_count[:, None]).reshape(-1)
-    outgoing = jnp.take(local, send_index.reshape(-1), axis=0)
-    outgoing = outgoing * live[:, None, None].astype(jnp.bfloat16)
-    head_out, tail_out = outgoing[:, :kept], outgoing[:, kept:]
+    head_out, tail_out = gather(cells, send_index.reshape(-1), live.astype(jnp.int32), kept)
     head_in = lax.all_to_all(head_out, "gy", split_axis=0, concat_axis=0, tiled=True)
     head_in, tail_out = lax.optimization_barrier((head_in, tail_out))
     tail_in = lax.all_to_all(tail_out, "gy", split_axis=0, concat_axis=0, tiled=True)

time: 256 us -> 250 us (0.977)
  local copies, waits for them, and re-layouts: 18.2 us -> 7.04 us
  Pallas kernels: 25.8 us -> 32.9 us
    pallas_call x0 -> x1, Pallas kernels: none -> 7.13 us  [gather(): pl.pallas_call(functools.partial(gather_kernel, rows), out_shape=[out, ou...]
    unnamed x14 -> x11, local copies, waits for them, and re-layouts: 6.36 us -> 2.28 us
    gather x1 -> x0, local copies, waits for them, and re-layouts: 3.1 us -> none  [body(): outgoing = jnp.take(local, send_index.reshape(-1), axis=0)]
    reshape x3 -> x1, local copies, waits for them, and re-layouts: 3.42 us -> 0.62 us  [body(): send_index.reshape(-1)]
    mul x1 -> x0, other arithmetic: 2.68 us -> none  [body(): outgoing = outgoing * live[:, None, None].astype(jnp.bfloat16)]
  transfers between devices with their start and end apart: 17 -> 17, of which waited for: 14 -> 14; matrix products, arithmetic and copies ran while one was open for 13% -> 14% of each run, Pallas kernels for 5% -> 5%
where the time goes in v3:
time: 250 us; the launch traced here: 249 us
  waiting for transfers between devices  63.5 us (25%)
  blocking collectives  62.8 us (25%)
  other arithmetic  37.6 us (15%)
  starting transfers between devices  35.5 us (14%)
  Pallas kernels  32.9 us (13%)
  matrix products  8.98 us (4%)
  local copies, waits for them, and re-layouts  7.04 us (3%)
    ppermute x16, waiting for transfers between devices, from_partner(): return lax.ppermute(value, axis, pairs)  63.5 us
    all_to_all x1, blocking collectives, body(): lax.all_to_all(head_out, 'gy', split_axis=0, concat_axis=0, tiled=True)  62.8 us
    ppermute x16, starting transfers between devices, from_partner(): return lax.ppermute(value, axis, pairs)  30.5 us
    pallas_call x2, Pallas kernels, lift(): pl.pallas_call(functools.partial(lift_kernel, feeds, brick_cells, paired)...  25.8 us
    another operation x3, other arithmetic, body(): l22 = jnp.linalg.cholesky(schur)  12.4 us
    another operation x3, other arithmetic, body(): l11 = jnp.linalg.cholesky(c11)  12.4 us
    another operation x2, other arithmetic, body(): lax.linalg.triangular_solve(l11, jnp.eye(kept, dtype=jnp.float32), left_s...  9.82 us
    pallas_call x1, Pallas kernels, gather(): pl.pallas_call(functools.partial(gather_kernel, rows), out_shape=[out, ou...  7.13 us
  transfers between devices with their start and end apart: 17, of which 14 were waited for; matrix products, arithmetic and copies ran while one was open for 14% of the time, Pallas kernels for 5%

profile of v3, /device:TPU:6, one launch (start us, length us, event | category | flops | bytes accessed | tf_op | source)
XLA Modules:
  0.0 249.2 jit_solution(9610660100265947854)
XLA Ops:
  3.4 7.1 %shard_map.77 = (bf16[64,128,128]{2,1,0:T(8,128)(2,1)}, bf16[64,128,128]{2,1,0:T(8,128)(2,1)}) custom-call(s32[64]{0:T(128)} %reshape.32.index_ref, s32[64]{0:T(128)} %reshape.33.live_ref, bf16[256,4096]{1,0:T(8,128)(2,1)} %cells_ref.1), custom_call_target="tpu_custom_call" | custom-call | bytes 8388608 | tf_op jit(solution)/shard_map/pallas_call | solution.py:131
  10.5 62.8 %all_to_all.10.recv_ref = bf16[64,128,128]{2,1,0:T(8,128)(2,1)} all-to-all(bf16[64,128,128]{2,1,0:T(8,128)(2,1)} %get-tuple-element.16), channel_id=1, replica_groups=mesh['gx'=8,'gy'=32] {'gy'}, dimensions={0} | all-to-all | bytes 4194304 | tf_op jit(solution)/shard_map/all_to_all | solution.py:156
  73.4 5.0 %all-to-all-start.1 = ((bf16[64,128,128]{2,1,0:T(8,128)(2,1)}), bf16[64,128,128]{2,1,0:T(8,128)(2,1)S(1)}, u32[]{:S(2)}, u32[]{:S(2)}) async-start(bf16[64,128,128]{2,1,0:T(8,128)(2,1)} %get-tuple-element.18), calls=%async_computation.1 | async-start | bytes 4194304 | tf_op jit(solution)/shard_map/all_to_all | solution.py:158
  79.9 11.6 %shard_map.78 = (bf16[128,16384]{1,0:T(8,128)(2,1)}, f32[128,128]{1,0:T(8,128)}) custom-call(s32[128]{0:T(128)} %reshape.30.blocks_ref, s32[128]{0:T(128)} %reshape.31.levels_ref, bf16[64,128,128]{2,1,0:T(8,128)(2,1)} %all_to_all.10.recv_ref, bf16[4,128,512]{2,1,0:T(8,128)(2,1)} %maps_ref.3), custom_call_target="tpu_custom_call" | custom-call | flops 2684354560 | bytes 6815744 | tf_op jit(solution)/shard_map/pallas_call | solution.py:91
  94.8 3.4 %collective-permute-done.1 = f32[128,128]{0,1:T(8,128)S(1)} collective-permute-done((f32[128,128]{0,1:T(8,128)S(1)}, f32[128,128]{0,1:T(8,128)S(1)}, u32[]{:S(2)}, u32[]{:S(2)}) %collective-permute-start.1) | collective-permute-done | bytes 65568 | tf_op jit(solution)/shard_map/ppermute | solution.py:18
  99.7 4.3 %collective-permute-done.2 = f32[128,128]{0,1:T(8,128)S(1)} collective-permute-done((f32[128,128]{0,1:T(8,128)S(1)}, f32[128,128]{0,1:T(8,128)S(1)}, u32[]{:S(2)}, u32[]{:S(2)}) %collective-permute-start.2) | collective-permute-done | bytes 65568 | tf_op jit(solution)/shard_map/ppermute | solution.py:18
  105.9 20.1 %collective-permute-done.3 = f32[128,128]{0,1:T(8,128)S(1)} collective-permute-done((f32[128,128]{0,1:T(8,128)S(1)}, f32[128,128]{0,1:T(8,128)S(1)}, u32[]{:S(2)}, u32[]{:S(2)}) %collective-permute-start.3) | collective-permute-done | bytes 65568 | tf_op jit(solution)/shard_map/ppermute | solution.py:18
  128.5 3.1 %collective-permute-done.4 = f32[128,128]{0,1:T(8,128)S(1)} collective-permute-done((f32[128,128]{0,1:T(8,128)S(1)}, f32[128,128]{0,1:T(8,128)S(1)}, u32[]{:S(2)}, u32[]{:S(2)}) %collective-permute-start.4) | collective-permute-done | bytes 65568 | tf_op jit(solution)/shard_map/ppermute | solution.py:18
  131.6 5.5 %collective-permute-start.5 = (f32[128,128]{0,1:T(8,128)S(1)}, f32[128,128]{0,1:T(8,128)S(1)}, u32[]{:S(2)}, u32[]{:S(2)}) collective-permute-start(f32[128,128]{0,1:T(8,128)S(1)} %add.66), channel_id=1, source_target_pairs={{0,4},{1,5},{2,6},{3,7},{4,0},{5,1},{6,2},{7,3},{8,12},{9,13},{10,... | collective-permute-start | bytes 196616 | tf_op jit(solution)/shard_map/ppermute | solution.py:18
  137.1 2.8 %collective-permute-done.5 = f32[128,128]{0,1:T(8,128)S(1)} collective-permute-done((f32[128,128]{0,1:T(8,128)S(1)}, f32[128,128]{0,1:T(8,128)S(1)}, u32[]{:S(2)}, u32[]{:S(2)}) %collective-permute-start.5) | collective-permute-done | bytes 65568 | tf_op jit(solution)/shard_map/ppermute | solution.py:18
  144.6 3.5 %collective-permute-start.7 = (f32[128,128]{0,1:T(8,128)S(1)}, f32[128,128]{0,1:T(8,128)S(1)}, u32[]{:S(2)}, u32[]{:S(2)}) collective-permute-start(f32[128,128]{0,1:T(8,128)S(1)} %add.68), channel_id=1, source_target_pairs={{0,16},{1,17},{2,18},{3,19},{4,20},{5,21},{6,22},{7,23},{8,24},{9,... | collective-permute-start | bytes 196616 | tf_op jit(solution)/shard_map/ppermute | solution.py:18
  148.1 2.5 %collective-permute-done.7 = f32[128,128]{0,1:T(8,128)S(1)} collective-permute-done((f32[128,128]{0,1:T(8,128)S(1)}, f32[128,128]{0,1:T(8,128)S(1)}, u32[]{:S(2)}, u32[]{:S(2)}) %collective-permute-start.7) | collective-permute-done | bytes 65568 | tf_op jit(solution)/shard_map/ppermute | solution.py:18
  150.7 11.7 %cholesky.44 = f32[128,128]{1,0:T(8,128)S(1)} custom-call(f32[128,128]{1,0:T(8,128)S(1)} %fusion.6), custom_call_target="Cholesky" | custom-call | tf_op jit(solution)/shard_map/jit(cholesky)/cholesky | solution.py:162
  165.1 14.2 %shard_map.79 = (bf16[128,16384]{1,0:T(8,128)(2,1)}, f32[128,256]{1,0:T(8,128)}) custom-call(s32[128]{0:T(128)} %reshape.30.blocks_ref, s32[128]{0:T(128)} %reshape.31.levels_ref, bf16[64,128,128]{2,1,0:T(8,128)(2,1)} %copy-done.1, bf16[4,128,512]{2,1,0:T(8,128)(2,1)} %maps_ref.3, bf16[128,16384]{1,0:T(8,128)(2,1)} %get-tuple-element.28.refs_0_), custom_call_target="tpu_custom_call" | custom-call | flops 3221225472 | bytes 11010048 | tf_op jit(solution)/shard_map/pallas_call | solution.py:91
  182.8 4.6 %collective-permute-done.9 = f32[128,256]{0,1:T(8,128)S(1)} collective-permute-done((f32[128,256]{0,1:T(8,128)S(1)}, f32[128,256]{0,1:T(8,128)S(1)}, u32[]{:S(2)}, u32[]{:S(2)}) %collective-permute-start.9) | collective-permute-done | bytes 131104 | tf_op jit(solution)/shard_map/ppermute | solution.py:18
  188.9 5.0 %collective-permute-done.10 = f32[128,256]{0,1:T(8,128)S(1)} collective-permute-done((f32[128,256]{0,1:T(8,128)S(1)}, f32[128,256]{0,1:T(8,128)S(1)}, u32[]{:S(2)}, u32[]{:S(2)}) %collective-permute-start.10) | collective-permute-done | bytes 131104 | tf_op jit(solution)/shard_map/ppermute | solution.py:18
  194.5 4.5 %collective-permute-done.11 = f32[128,256]{0,1:T(8,128)S(1)} collective-permute-done((f32[128,256]{0,1:T(8,128)S(1)}, f32[128,256]{0,1:T(8,128)S(1)}, u32[]{:S(2)}, u32[]{:S(2)}) %collective-permute-start.11) | collective-permute-done | bytes 131104 | tf_op jit(solution)/shard_map/ppermute | solution.py:18
  199.1 4.0 %collective-permute-start.12 = (f32[128,256]{0,1:T(8,128)S(1)}, f32[128,256]{0,1:T(8,128)S(1)}, u32[]{:S(2)}, u32[]{:S(2)}) collective-permute-start(f32[128,256]{0,1:T(8,128)S(1)} %add.73), channel_id=1, source_target_pairs={{0,2},{1,3},{2,0},{3,1},{4,6},{5,7},{6,4},{7,5},{8,10},{9,11},{10,... | collective-permute-start | bytes 393224 | tf_op jit(solution)/shard_map/ppermute | solution.py:18
  203.1 9.8 %custom-call.5 = f32[1,128,128]{1,2,0:T(8,128)S(1)} custom-call(f32[1,128,128]{2,1,0:T(8,128)S(1)} %fusion.8), custom_call_target="InvertDiagBlocksLowerTriangular" | custom-call | tf_op jit(solution)/shard_map/triangular_solve | solution.py:166
  214.7 7.2 %collective-permute-done.13 = f32[128,256]{0,1:T(8,128)S(1)} collective-permute-done((f32[128,256]{0,1:T(8,128)S(1)}, f32[128,256]{0,1:T(8,128)S(1)}, u32[]{:S(2)}, u32[]{:S(2)}) %collective-permute-start.13) | collective-permute-done | bytes 131104 | tf_op jit(solution)/shard_map/ppermute | solution.py:18
  223.0 3.6 %fusion.10 = f32[128,16384]{1,0:T(8,128)S(1)} fusion(bf16[128,16384]{1,0:T(8,128)(2,1)} %get-tuple-element.28.refs_0_, f32[128,128]{1,0:T(8,128)S(1)} %fusion.4), kind=kOutput, calls=%fused_computation.25 | convolution fusion | flops 536903680 | bytes 12648448 | tf_op jit(solution)/shard_map/dot_general | solution.py:172
  227.4 2.7 %collective-permute-start.15 = (f32[128,256]{0,1:T(8,128)S(1)}, f32[128,256]{0,1:T(8,128)S(1)}, u32[]{:S(2)}, u32[]{:S(2)}) collective-permute-start(f32[128,256]{0,1:T(8,128)S(1)} %add.76), channel_id=1, source_target_pairs={{0,16},{1,17},{2,18},{3,19},{4,20},{5,21},{6,22},{7,23},{8,24},{9,... | collective-permute-start | bytes 393224 | tf_op jit(solution)/shard_map/ppermute | solution.py:18
  230.1 4.6 %convolution_add_fusion = f32[128,16384]{1,0:T(8,128)} fusion(f32[128,16384]{1,0:T(8,128)S(1)} %fusion.10, bf16[128,16384]{1,0:T(8,128)(2,1)S(1)} %copy-done, f32[128,128]{1,0:T(8,128)S(1)} %fusion.4), kind=kOutput, calls=%fused_computation | convolution fusion | flops 539017216 | bytes 21037056 | tf_op jit(solution)/shard_map/dot_general | solution.py:172
  235.5 11.7 %cholesky.55 = f32[128,128]{1,0:T(8,128)S(1)} custom-call(f32[128,128]{1,0:T(8,128)S(1)} %fusion.3), custom_call_target="Cholesky" | custom-call | tf_op jit(solution)/shard_map/jit(cholesky)/cholesky | solution.py:179
  (69 shorter events, 32.7 us)
Async XLA Ops:
  10.5 67.9 %copy-start.2 = (s32[32,4]{0,1:T(4,128)S(1)}, s32[32,4]{0,1:T(4,128)}, u32[]{:S(2)}) copy-start(s32[32,4]{0,1:T(4,128)} %param.10) | copy-start | bytes 1540
  10.5 68.7 %copy-start.3 = (s32[32,4]{0,1:T(4,128)S(1)}, s32[32,4]{0,1:T(4,128)}, u32[]{:S(2)}) copy-start(s32[32,4]{0,1:T(4,128)} %param.11) | copy-start | bytes 1540
  73.4 90.4 %all-to-all-start.1 = ((bf16[64,128,128]{2,1,0:T(8,128)(2,1)}), bf16[64,128,128]{2,1,0:T(8,128)(2,1)S(1)}, u32[]{:S(2)}, u32[]{:S(2)}) async-start(bf16[64,128,128]{2,1,0:T(8,128)(2,1)} %get-tuple-element.18), calls=%async_computation.1 | async-start | bytes 4194304 | tf_op jit(solution)/shard_map/all_to_all | solution.py:158
  92.4 1.3 collective-permute-start
  93.8 4.4 %collective-permute-start.1 = (f32[128,128]{0,1:T(8,128)S(1)}, f32[128,128]{0,1:T(8,128)S(1)}, u32[]{:S(2)}, u32[]{:S(2)}) collective-permute-start(f32[128,128]{0,1:T(8,128)S(1)} %add.62), channel_id=1, source_target_pairs={{0,64},{32,96},{64,0},{96,32},{128,192},{160,224},{192,128},{224,1... | collective-permute-start | bytes 196616 | tf_op jit(solution)/shard_map/ppermute | solution.py:18
  98.2 5.9 %collective-permute-start.2 = (f32[128,128]{0,1:T(8,128)S(1)}, f32[128,128]{0,1:T(8,128)S(1)}, u32[]{:S(2)}, u32[]{:S(2)}) collective-permute-start(f32[128,128]{0,1:T(8,128)S(1)} %add.63), channel_id=1, source_target_pairs={{0,128},{32,160},{64,192},{96,224},{128,0},{160,32},{192,64},{224,... | collective-permute-start | bytes 196616 | tf_op jit(solution)/shard_map/ppermute | solution.py:18
  104.0 22.0 %collective-permute-start.3 = (f32[128,128]{0,1:T(8,128)S(1)}, f32[128,128]{0,1:T(8,128)S(1)}, u32[]{:S(2)}, u32[]{:S(2)}) collective-permute-start(f32[128,128]{0,1:T(8,128)S(1)} %add.64), channel_id=1, source_target_pairs={{0,1},{1,0},{2,3},{3,2},{4,5},{5,4},{6,7},{7,6},{8,9},{9,8},{10,11... | collective-permute-start | bytes 196616 | tf_op jit(solution)/shard_map/ppermute | solution.py:18
  126.0 5.5 %collective-permute-start.4 = (f32[128,128]{0,1:T(8,128)S(1)}, f32[128,128]{0,1:T(8,128)S(1)}, u32[]{:S(2)}, u32[]{:S(2)}) collective-permute-start(f32[128,128]{0,1:T(8,128)S(1)} %add.65), channel_id=1, source_target_pairs={{0,2},{1,3},{2,0},{3,1},{4,6},{5,7},{6,4},{7,5},{8,10},{9,11},{10,... | collective-permute-start | bytes 196616 | tf_op jit(solution)/shard_map/ppermute | solution.py:18
  131.6 8.4 %collective-permute-start.5 = (f32[128,128]{0,1:T(8,128)S(1)}, f32[128,128]{0,1:T(8,128)S(1)}, u32[]{:S(2)}, u32[]{:S(2)}) collective-permute-start(f32[128,128]{0,1:T(8,128)S(1)} %add.66), channel_id=1, source_target_pairs={{0,4},{1,5},{2,6},{3,7},{4,0},{5,1},{6,2},{7,3},{8,12},{9,13},{10,... | collective-permute-start | bytes 196616 | tf_op jit(solution)/shard_map/ppermute | solution.py:18
  140.0 4.6 %collective-permute-start.6 = (f32[128,128]{0,1:T(8,128)S(1)}, f32[128,128]{0,1:T(8,128)S(1)}, u32[]{:S(2)}, u32[]{:S(2)}) collective-permute-start(f32[128,128]{0,1:T(8,128)S(1)} %add.67), channel_id=1, source_target_pairs={{0,8},{1,9},{2,10},{3,11},{4,12},{5,13},{6,14},{7,15},{8,0},{9,1},... | collective-permute-start | bytes 196616 | tf_op jit(solution)/shard_map/ppermute | solution.py:18
  144.6 6.0 %collective-permute-start.7 = (f32[128,128]{0,1:T(8,128)S(1)}, f32[128,128]{0,1:T(8,128)S(1)}, u32[]{:S(2)}, u32[]{:S(2)}) collective-permute-start(f32[128,128]{0,1:T(8,128)S(1)} %add.68), channel_id=1, source_target_pairs={{0,16},{1,17},{2,18},{3,19},{4,20},{5,21},{6,22},{7,23},{8,24},{9,... | collective-permute-start | bytes 196616 | tf_op jit(solution)/shard_map/ppermute | solution.py:18
  163.8 1.3 copy-start.1
  180.3 1.4 collective-permute-start.8
  181.8 5.6 %collective-permute-start.9 = (f32[128,256]{0,1:T(8,128)S(1)}, f32[128,256]{0,1:T(8,128)S(1)}, u32[]{:S(2)}, u32[]{:S(2)}) collective-permute-start(f32[128,256]{0,1:T(8,128)S(1)} %add.70), channel_id=1, source_target_pairs={{0,64},{32,96},{64,0},{96,32},{128,192},{160,224},{192,128},{224,1... | collective-permute-start | bytes 393224 | tf_op jit(solution)/shard_map/ppermute | solution.py:18
  187.4 6.6 %collective-permute-start.10 = (f32[128,256]{0,1:T(8,128)S(1)}, f32[128,256]{0,1:T(8,128)S(1)}, u32[]{:S(2)}, u32[]{:S(2)}) collective-permute-start(f32[128,256]{0,1:T(8,128)S(1)} %add.71), channel_id=1, source_target_pairs={{0,128},{32,160},{64,192},{96,224},{128,0},{160,32},{192,64},{224,... | collective-permute-start | bytes 393224 | tf_op jit(solution)/shard_map/ppermute | solution.py:18
  194.0 5.1 %collective-permute-start.11 = (f32[128,256]{0,1:T(8,128)S(1)}, f32[128,256]{0,1:T(8,128)S(1)}, u32[]{:S(2)}, u32[]{:S(2)}) collective-permute-start(f32[128,256]{0,1:T(8,128)S(1)} %add.72), channel_id=1, source_target_pairs={{0,1},{1,0},{2,3},{3,2},{4,5},{5,4},{6,7},{7,6},{8,9},{9,8},{10,11... | collective-permute-start | bytes 393224 | tf_op jit(solution)/shard_map/ppermute | solution.py:18
  199.1 13.8 %collective-permute-start.12 = (f32[128,256]{0,1:T(8,128)S(1)}, f32[128,256]{0,1:T(8,128)S(1)}, u32[]{:S(2)}, u32[]{:S(2)}) collective-permute-start(f32[128,256]{0,1:T(8,128)S(1)} %add.73), channel_id=1, source_target_pairs={{0,2},{1,3},{2,0},{3,1},{4,6},{5,7},{6,4},{7,5},{8,10},{9,11},{10,... | collective-permute-start | bytes 393224 | tf_op jit(solution)/shard_map/ppermute | solution.py:18
  212.9 9.0 %collective-permute-start.13 = (f32[128,256]{0,1:T(8,128)S(1)}, f32[128,256]{0,1:T(8,128)S(1)}, u32[]{:S(2)}, u32[]{:S(2)}) collective-permute-start(f32[128,256]{0,1:T(8,128)S(1)} %add.74), channel_id=1, source_target_pairs={{0,4},{1,5},{2,6},{3,7},{4,0},{5,1},{6,2},{7,3},{8,12},{9,13},{10,... | collective-permute-start | bytes 393224 | tf_op jit(solution)/shard_map/ppermute | solution.py:18
  221.9 8.2 %copy-start = (bf16[128,16384]{1,0:T(8,128)(2,1)S(1)}, bf16[128,16384]{1,0:T(8,128)(2,1)}, u32[]{:S(2)}) copy-start(bf16[128,16384]{1,0:T(8,128)(2,1)} %get-tuple-element.28.refs_0_) | copy-start | bytes 12582916
  221.9 5.4 %collective-permute-start.14 = (f32[128,256]{0,1:T(8,128)S(1)}, f32[128,256]{0,1:T(8,128)S(1)}, u32[]{:S(2)}, u32[]{:S(2)}) collective-permute-start(f32[128,256]{0,1:T(8,128)S(1)} %add.75), channel_id=1, source_target_pairs={{0,8},{1,9},{2,10},{3,11},{4,12},{5,13},{6,14},{7,15},{8,0},{9,1},... | collective-permute-start | bytes 393224 | tf_op jit(solution)/shard_map/ppermute | solution.py:18
  227.4 7.3 %collective-permute-start.15 = (f32[128,256]{0,1:T(8,128)S(1)}, f32[128,256]{0,1:T(8,128)S(1)}, u32[]{:S(2)}, u32[]{:S(2)}) collective-permute-start(f32[128,256]{0,1:T(8,128)S(1)} %add.76), channel_id=1, source_target_pairs={{0,16},{1,17},{2,18},{3,19},{4,20},{5,21},{6,22},{7,23},{8,24},{9,... | collective-permute-start | bytes 393224 | tf_op jit(solution)/shard_map/ppermute | solution.py:18

commit v4 on v3

--- a/solution.py
+++ b/solution.py
@@ -27,9 +27,9 @@
 
 def lift_kernel(feeds, brick_cells, paired, blocks_ref, levels_ref, recv_ref, maps_ref, *refs):
     if paired:
-        other_ref, out_ref, gram_ref = refs
+        other_ref, out_ref, gram_ref, lhs_ref, rhs_ref = refs
     else:
-        out_ref, gram_ref = refs
+        out_ref, gram_ref, lhs_ref, rhs_ref = refs
     step = pl.program_id(0)
 
     @pl.when(step == 0)
@@ -39,12 +39,13 @@
     rows = out_ref.shape[0]
     for i in range(PER):
         brick = step * PER + i
-        acc = None
+        blk = recv_ref.shape[2]
         for n in range(feeds):
             slot = blocks_ref[brick * feeds + n]
             level = levels_ref[brick * feeds + n]
-            part = jnp.dot(recv_ref[slot], maps_ref[level], preferred_element_type=jnp.float32)
-            acc = part if acc is None else acc + part
+            lhs_ref[:, n * blk : (n + 1) * blk] = recv_ref[slot]
+            rhs_ref[n * blk : (n + 1) * blk, :] = maps_ref[level]
+        acc = jnp.dot(lhs_ref[...], rhs_ref[...], preferred_element_type=jnp.float32)
         cols = slice(i * brick_cells, (i + 1) * brick_cells)
         lifted = acc.astype(out_ref.dtype)
         out_ref[:, cols] = lifted
@@ -85,6 +86,10 @@
             pl.BlockSpec((rows, PER * brick_cells), lambda s, b, l: (0, s)),
             pl.BlockSpec((rows, gram_cols), lambda s, b, l: (0, 0)),
         ],
+        scratch_shapes=[
+            pltpu.VMEM((rows, feeds * blk), received.dtype),
+            pltpu.VMEM((feeds * blk, brick_cells), maps.dtype),
+        ],
     )
     cells = bricks * brick_cells
     flops = 2 * rows * blk * cells * feeds + 2 * rows * gram_cols * cells

time: 250 us -> 248 us (level)
  Pallas kernels: 32.9 us -> 28.9 us
  waiting for transfers between devices: 63.5 us -> 66.1 us
    pallas_call x2, Pallas kernels: 25.8 us -> 21.7 us  [lift(): pl.pallas_call(functools.partial(lift_kernel, feeds, brick_cells, paired)...]
    ppermute x16, waiting for transfers between devices: 63.5 us -> 66.1 us  [from_partner(): return lax.ppermute(value, axis, pairs)]
  transfers between devices with their start and end apart: 17 -> 17, of which waited for: 14 -> 14; matrix products, arithmetic and copies ran while one was open for 14% -> 14% of each run, Pallas kernels for 5% -> 4%
where the time goes in v4:
time: 248 us; the launch traced here: 247 us
  waiting for transfers between devices  66.1 us (27%)
  blocking collectives  62.8 us (25%)
  other arithmetic  37.6 us (15%)
  starting transfers between devices  34.9 us (14%)
  Pallas kernels  28.9 us (12%)
  matrix products  8.99 us (4%)
  local copies, waits for them, and re-layouts  7.04 us (3%)
    ppermute x16, waiting for transfers between devices, from_partner(): return lax.ppermute(value, axis, pairs)  66.1 us
    all_to_all x1, blocking collectives, body(): lax.all_to_all(head_out, 'gy', split_axis=0, concat_axis=0, tiled=True)  62.8 us
    ppermute x16, starting transfers between devices, from_partner(): return lax.ppermute(value, axis, pairs)  29.9 us
    pallas_call x2, Pallas kernels, lift(): pl.pallas_call(functools.partial(lift_kernel, feeds, brick_cells, paired)...  21.7 us
    another operation x3, other arithmetic, body(): l11 = jnp.linalg.cholesky(c11)  12.4 us
    another operation x3, other arithmetic, body(): l22 = jnp.linalg.cholesky(schur)  12.4 us
    another operation x2, other arithmetic, body(): lax.linalg.triangular_solve(l11, jnp.eye(kept, dtype=jnp.float32), left_s...  9.82 us
    pallas_call x1, Pallas kernels, gather(): pl.pallas_call(functools.partial(gather_kernel, rows), out_shape=[out, ou...  7.2 us
  transfers between devices with their start and end apart: 17, of which 14 were waited for; matrix products, arithmetic and copies ran while one was open for 14% of the time, Pallas kernels for 4%

profile of v4, /device:TPU:6, one launch (start us, length us, event | category | flops | bytes accessed | tf_op | source)
XLA Modules:
  0.0 247.2 jit_solution(13135841523495392026)
XLA Ops:
  3.4 7.2 %shard_map.77 = (bf16[64,128,128]{2,1,0:T(8,128)(2,1)}, bf16[64,128,128]{2,1,0:T(8,128)(2,1)}) custom-call(s32[64]{0:T(128)} %reshape.32.index_ref, s32[64]{0:T(128)} %reshape.33.live_ref, bf16[256,4096]{1,0:T(8,128)(2,1)} %cells_ref.1), custom_call_target="tpu_custom_call" | custom-call | bytes 8388608 | tf_op jit(solution)/shard_map/pallas_call | solution.py:136
  10.6 62.8 %all_to_all.10.recv_ref = bf16[64,128,128]{2,1,0:T(8,128)(2,1)} all-to-all(bf16[64,128,128]{2,1,0:T(8,128)(2,1)} %get-tuple-element.16), channel_id=1, replica_groups=mesh['gx'=8,'gy'=32] {'gy'}, dimensions={0} | all-to-all | bytes 4194304 | tf_op jit(solution)/shard_map/all_to_all | solution.py:161
  73.4 5.0 %all-to-all-start.1 = ((bf16[64,128,128]{2,1,0:T(8,128)(2,1)}), bf16[64,128,128]{2,1,0:T(8,128)(2,1)S(1)}, u32[]{:S(2)}, u32[]{:S(2)}) async-start(bf16[64,128,128]{2,1,0:T(8,128)(2,1)} %get-tuple-element.18), calls=%async_computation.1 | async-start | bytes 4194304 | tf_op jit(solution)/shard_map/all_to_all | solution.py:163
  79.9 9.6 %shard_map.78 = (bf16[128,16384]{1,0:T(8,128)(2,1)}, f32[128,128]{1,0:T(8,128)}) custom-call(s32[128]{0:T(128)} %reshape.30.blocks_ref, s32[128]{0:T(128)} %reshape.31.levels_ref, bf16[64,128,128]{2,1,0:T(8,128)(2,1)} %all_to_all.10.recv_ref, bf16[4,128,512]{2,1,0:T(8,128)(2,1)} %maps_ref.3), custom_call_target="tpu_custom_call" | custom-call | flops 2684354560 | bytes 6815744 | tf_op jit(solution)/shard_map/pallas_call | solution.py:96
  92.7 3.5 %collective-permute-done.1 = f32[128,128]{0,1:T(8,128)S(1)} collective-permute-done((f32[128,128]{0,1:T(8,128)S(1)}, f32[128,128]{0,1:T(8,128)S(1)}, u32[]{:S(2)}, u32[]{:S(2)}) %collective-permute-start.1) | collective-permute-done | bytes 65568 | tf_op jit(solution)/shard_map/ppermute | solution.py:18
  97.5 4.5 %collective-permute-done.2 = f32[128,128]{0,1:T(8,128)S(1)} collective-permute-done((f32[128,128]{0,1:T(8,128)S(1)}, f32[128,128]{0,1:T(8,128)S(1)}, u32[]{:S(2)}, u32[]{:S(2)}) %collective-permute-start.2) | collective-permute-done | bytes 65568 | tf_op jit(solution)/shard_map/ppermute | solution.py:18
  103.9 22.1 %collective-permute-done.3 = f32[128,128]{0,1:T(8,128)S(1)} collective-permute-done((f32[128,128]{0,1:T(8,128)S(1)}, f32[128,128]{0,1:T(8,128)S(1)}, u32[]{:S(2)}, u32[]{:S(2)}) %collective-permute-start.3) | collective-permute-done | bytes 65568 | tf_op jit(solution)/shard_map/ppermute | solution.py:18
  128.5 3.1 %collective-permute-done.4 = f32[128,128]{0,1:T(8,128)S(1)} collective-permute-done((f32[128,128]{0,1:T(8,128)S(1)}, f32[128,128]{0,1:T(8,128)S(1)}, u32[]{:S(2)}, u32[]{:S(2)}) %collective-permute-start.4) | collective-permute-done | bytes 65568 | tf_op jit(solution)/shard_map/ppermute | solution.py:18
  131.6 5.5 %collective-permute-start.5 = (f32[128,128]{0,1:T(8,128)S(1)}, f32[128,128]{0,1:T(8,128)S(1)}, u32[]{:S(2)}, u32[]{:S(2)}) collective-permute-start(f32[128,128]{0,1:T(8,128)S(1)} %add.66), channel_id=1, source_target_pairs={{0,4},{1,5},{2,6},{3,7},{4,0},{5,1},{6,2},{7,3},{8,12},{9,13},{10,... | collective-permute-start | bytes 196616 | tf_op jit(solution)/shard_map/ppermute | solution.py:18
  137.1 2.8 %collective-permute-done.5 = f32[128,128]{0,1:T(8,128)S(1)} collective-permute-done((f32[128,128]{0,1:T(8,128)S(1)}, f32[128,128]{0,1:T(8,128)S(1)}, u32[]{:S(2)}, u32[]{:S(2)}) %collective-permute-start.5) | collective-permute-done | bytes 65568 | tf_op jit(solution)/shard_map/ppermute | solution.py:18
  144.6 3.5 %collective-permute-start.7 = (f32[128,128]{0,1:T(8,128)S(1)}, f32[128,128]{0,1:T(8,128)S(1)}, u32[]{:S(2)}, u32[]{:S(2)}) collective-permute-start(f32[128,128]{0,1:T(8,128)S(1)} %add.68), channel_id=1, source_target_pairs={{0,16},{1,17},{2,18},{3,19},{4,20},{5,21},{6,22},{7,23},{8,24},{9,... | collective-permute-start | bytes 196616 | tf_op jit(solution)/shard_map/ppermute | solution.py:18
  148.1 2.5 %collective-permute-done.7 = f32[128,128]{0,1:T(8,128)S(1)} collective-permute-done((f32[128,128]{0,1:T(8,128)S(1)}, f32[128,128]{0,1:T(8,128)S(1)}, u32[]{:S(2)}, u32[]{:S(2)}) %collective-permute-start.7) | collective-permute-done | bytes 65568 | tf_op jit(solution)/shard_map/ppermute | solution.py:18
  150.8 11.7 %cholesky.44 = f32[128,128]{1,0:T(8,128)S(1)} custom-call(f32[128,128]{1,0:T(8,128)S(1)} %fusion.6), custom_call_target="Cholesky" | custom-call | tf_op jit(solution)/shard_map/jit(cholesky)/cholesky | solution.py:167
  165.2 12.1 %shard_map.79 = (bf16[128,16384]{1,0:T(8,128)(2,1)}, f32[128,256]{1,0:T(8,128)}) custom-call(s32[128]{0:T(128)} %reshape.30.blocks_ref, s32[128]{0:T(128)} %reshape.31.levels_ref, bf16[64,128,128]{2,1,0:T(8,128)(2,1)} %copy-done.1, bf16[4,128,512]{2,1,0:T(8,128)(2,1)} %maps_ref.3, bf16[128,16384]{1,0:T(8,128)(2,1)} %get-tuple-element.28.refs_0_), custom_call_target="tpu_custom_call" | custom-call | flops 3221225472 | bytes 11010048 | tf_op jit(solution)/shard_map/pallas_call | solution.py:96
  180.5 4.8 %collective-permute-done.9 = f32[128,256]{0,1:T(8,128)S(1)} collective-permute-done((f32[128,256]{0,1:T(8,128)S(1)}, f32[128,256]{0,1:T(8,128)S(1)}, u32[]{:S(2)}, u32[]{:S(2)}) %collective-permute-start.9) | collective-permute-done | bytes 131104 | tf_op jit(solution)/shard_map/ppermute | solution.py:18
  186.7 5.2 %collective-permute-done.10 = f32[128,256]{0,1:T(8,128)S(1)} collective-permute-done((f32[128,256]{0,1:T(8,128)S(1)}, f32[128,256]{0,1:T(8,128)S(1)}, u32[]{:S(2)}, u32[]{:S(2)}) %collective-permute-start.10) | collective-permute-done | bytes 131104 | tf_op jit(solution)/shard_map/ppermute | solution.py:18
  192.5 4.5 %collective-permute-done.11 = f32[128,256]{0,1:T(8,128)S(1)} collective-permute-done((f32[128,256]{0,1:T(8,128)S(1)}, f32[128,256]{0,1:T(8,128)S(1)}, u32[]{:S(2)}, u32[]{:S(2)}) %collective-permute-start.11) | collective-permute-done | bytes 131104 | tf_op jit(solution)/shard_map/ppermute | solution.py:18
  197.0 4.0 %collective-permute-start.12 = (f32[128,256]{0,1:T(8,128)S(1)}, f32[128,256]{0,1:T(8,128)S(1)}, u32[]{:S(2)}, u32[]{:S(2)}) collective-permute-start(f32[128,256]{0,1:T(8,128)S(1)} %add.73), channel_id=1, source_target_pairs={{0,2},{1,3},{2,0},{3,1},{4,6},{5,7},{6,4},{7,5},{8,10},{9,11},{10,... | collective-permute-start | bytes 393224 | tf_op jit(solution)/shard_map/ppermute | solution.py:18
  201.0 9.8 %custom-call.5 = f32[1,128,128]{1,2,0:T(8,128)S(1)} custom-call(f32[1,128,128]{2,1,0:T(8,128)S(1)} %fusion.8), custom_call_target="InvertDiagBlocksLowerTriangular" | custom-call | tf_op jit(solution)/shard_map/triangular_solve | solution.py:171
  212.6 7.2 %collective-permute-done.13 = f32[128,256]{0,1:T(8,128)S(1)} collective-permute-done((f32[128,256]{0,1:T(8,128)S(1)}, f32[128,256]{0,1:T(8,128)S(1)}, u32[]{:S(2)}, u32[]{:S(2)}) %collective-permute-start.13) | collective-permute-done | bytes 131104 | tf_op jit(solution)/shard_map/ppermute | solution.py:18
  220.9 3.6 %fusion.10 = f32[128,16384]{1,0:T(8,128)S(1)} fusion(bf16[128,16384]{1,0:T(8,128)(2,1)} %get-tuple-element.28.refs_0_, f32[128,128]{1,0:T(8,128)S(1)} %fusion.4), kind=kOutput, calls=%fused_computation.25 | convolution fusion | flops 536903680 | bytes 12648448 | tf_op jit(solution)/shard_map/dot_general | solution.py:177
  225.3 2.7 %collective-permute-start.15 = (f32[128,256]{0,1:T(8,128)S(1)}, f32[128,256]{0,1:T(8,128)S(1)}, u32[]{:S(2)}, u32[]{:S(2)}) collective-permute-start(f32[128,256]{0,1:T(8,128)S(1)} %add.76), channel_id=1, source_target_pairs={{0,16},{1,17},{2,18},{3,19},{4,20},{5,21},{6,22},{7,23},{8,24},{9,... | collective-permute-start | bytes 393224 | tf_op jit(solution)/shard_map/ppermute | solution.py:18
  228.0 4.6 %convolution_add_fusion = f32[128,16384]{1,0:T(8,128)} fusion(f32[128,16384]{1,0:T(8,128)S(1)} %fusion.10, bf16[128,16384]{1,0:T(8,128)(2,1)S(1)} %copy-done, f32[128,128]{1,0:T(8,128)S(1)} %fusion.4), kind=kOutput, calls=%fused_computation | convolution fusion | flops 539017216 | bytes 21037056 | tf_op jit(solution)/shard_map/dot_general | solution.py:177
  233.4 11.7 %cholesky.55 = f32[128,128]{1,0:T(8,128)S(1)} custom-call(f32[128,128]{1,0:T(8,128)S(1)} %fusion.3), custom_call_target="Cholesky" | custom-call | tf_op jit(solution)/shard_map/jit(cholesky)/cholesky | solution.py:184
  (69 shorter events, 32.0 us)
Async XLA Ops:
  10.6 67.8 %copy-start.2 = (s32[32,4]{0,1:T(4,128)S(1)}, s32[32,4]{0,1:T(4,128)}, u32[]{:S(2)}) copy-start(s32[32,4]{0,1:T(4,128)} %param.10) | copy-start | bytes 1540
  10.6 68.6 %copy-start.3 = (s32[32,4]{0,1:T(4,128)S(1)}, s32[32,4]{0,1:T(4,128)}, u32[]{:S(2)}) copy-start(s32[32,4]{0,1:T(4,128)} %param.11) | copy-start | bytes 1540
  73.4 90.4 %all-to-all-start.1 = ((bf16[64,128,128]{2,1,0:T(8,128)(2,1)}), bf16[64,128,128]{2,1,0:T(8,128)(2,1)S(1)}, u32[]{:S(2)}, u32[]{:S(2)}) async-start(bf16[64,128,128]{2,1,0:T(8,128)(2,1)} %get-tuple-element.18), calls=%async_computation.1 | async-start | bytes 4194304 | tf_op jit(solution)/shard_map/all_to_all | solution.py:163
  90.5 1.3 collective-permute-start
  91.8 4.4 %collective-permute-start.1 = (f32[128,128]{0,1:T(8,128)S(1)}, f32[128,128]{0,1:T(8,128)S(1)}, u32[]{:S(2)}, u32[]{:S(2)}) collective-permute-start(f32[128,128]{0,1:T(8,128)S(1)} %add.62), channel_id=1, source_target_pairs={{0,64},{32,96},{64,0},{96,32},{128,192},{160,224},{192,128},{224,1... | collective-permute-start | bytes 196616 | tf_op jit(solution)/shard_map/ppermute | solution.py:18
  96.2 5.9 %collective-permute-start.2 = (f32[128,128]{0,1:T(8,128)S(1)}, f32[128,128]{0,1:T(8,128)S(1)}, u32[]{:S(2)}, u32[]{:S(2)}) collective-permute-start(f32[128,128]{0,1:T(8,128)S(1)} %add.63), channel_id=1, source_target_pairs={{0,128},{32,160},{64,192},{96,224},{128,0},{160,32},{192,64},{224,... | collective-permute-start | bytes 196616 | tf_op jit(solution)/shard_map/ppermute | solution.py:18
  102.1 24.0 %collective-permute-start.3 = (f32[128,128]{0,1:T(8,128)S(1)}, f32[128,128]{0,1:T(8,128)S(1)}, u32[]{:S(2)}, u32[]{:S(2)}) collective-permute-start(f32[128,128]{0,1:T(8,128)S(1)} %add.64), channel_id=1, source_target_pairs={{0,1},{1,0},{2,3},{3,2},{4,5},{5,4},{6,7},{7,6},{8,9},{9,8},{10,11... | collective-permute-start | bytes 196616 | tf_op jit(solution)/shard_map/ppermute | solution.py:18
  126.1 5.5 %collective-permute-start.4 = (f32[128,128]{0,1:T(8,128)S(1)}, f32[128,128]{0,1:T(8,128)S(1)}, u32[]{:S(2)}, u32[]{:S(2)}) collective-permute-start(f32[128,128]{0,1:T(8,128)S(1)} %add.65), channel_id=1, source_target_pairs={{0,2},{1,3},{2,0},{3,1},{4,6},{5,7},{6,4},{7,5},{8,10},{9,11},{10,... | collective-permute-start | bytes 196616 | tf_op jit(solution)/shard_map/ppermute | solution.py:18
  131.6 8.4 %collective-permute-start.5 = (f32[128,128]{0,1:T(8,128)S(1)}, f32[128,128]{0,1:T(8,128)S(1)}, u32[]{:S(2)}, u32[]{:S(2)}) collective-permute-start(f32[128,128]{0,1:T(8,128)S(1)} %add.66), channel_id=1, source_target_pairs={{0,4},{1,5},{2,6},{3,7},{4,0},{5,1},{6,2},{7,3},{8,12},{9,13},{10,... | collective-permute-start | bytes 196616 | tf_op jit(solution)/shard_map/ppermute | solution.py:18
  140.0 4.6 %collective-permute-start.6 = (f32[128,128]{0,1:T(8,128)S(1)}, f32[128,128]{0,1:T(8,128)S(1)}, u32[]{:S(2)}, u32[]{:S(2)}) collective-permute-start(f32[128,128]{0,1:T(8,128)S(1)} %add.67), channel_id=1, source_target_pairs={{0,8},{1,9},{2,10},{3,11},{4,12},{5,13},{6,14},{7,15},{8,0},{9,1},... | collective-permute-start | bytes 196616 | tf_op jit(solution)/shard_map/ppermute | solution.py:18
  144.6 6.0 %collective-permute-start.7 = (f32[128,128]{0,1:T(8,128)S(1)}, f32[128,128]{0,1:T(8,128)S(1)}, u32[]{:S(2)}, u32[]{:S(2)}) collective-permute-start(f32[128,128]{0,1:T(8,128)S(1)} %add.68), channel_id=1, source_target_pairs={{0,16},{1,17},{2,18},{3,19},{4,20},{5,21},{6,22},{7,23},{8,24},{9,... | collective-permute-start | bytes 196616 | tf_op jit(solution)/shard_map/ppermute | solution.py:18
  163.8 1.3 copy-start.1
  178.2 1.4 collective-permute-start.8
  179.7 5.6 %collective-permute-start.9 = (f32[128,256]{0,1:T(8,128)S(1)}, f32[128,256]{0,1:T(8,128)S(1)}, u32[]{:S(2)}, u32[]{:S(2)}) collective-permute-start(f32[128,256]{0,1:T(8,128)S(1)} %add.70), channel_id=1, source_target_pairs={{0,64},{32,96},{64,0},{96,32},{128,192},{160,224},{192,128},{224,1... | collective-permute-start | bytes 393224 | tf_op jit(solution)/shard_map/ppermute | solution.py:18
  185.4 6.6 %collective-permute-start.10 = (f32[128,256]{0,1:T(8,128)S(1)}, f32[128,256]{0,1:T(8,128)S(1)}, u32[]{:S(2)}, u32[]{:S(2)}) collective-permute-start(f32[128,256]{0,1:T(8,128)S(1)} %add.71), channel_id=1, source_target_pairs={{0,128},{32,160},{64,192},{96,224},{128,0},{160,32},{192,64},{224,... | collective-permute-start | bytes 393224 | tf_op jit(solution)/shard_map/ppermute | solution.py:18
  191.9 5.1 %collective-permute-start.11 = (f32[128,256]{0,1:T(8,128)S(1)}, f32[128,256]{0,1:T(8,128)S(1)}, u32[]{:S(2)}, u32[]{:S(2)}) collective-permute-start(f32[128,256]{0,1:T(8,128)S(1)} %add.72), channel_id=1, source_target_pairs={{0,1},{1,0},{2,3},{3,2},{4,5},{5,4},{6,7},{7,6},{8,9},{9,8},{10,11... | collective-permute-start | bytes 393224 | tf_op jit(solution)/shard_map/ppermute | solution.py:18
  197.0 13.9 %collective-permute-start.12 = (f32[128,256]{0,1:T(8,128)S(1)}, f32[128,256]{0,1:T(8,128)S(1)}, u32[]{:S(2)}, u32[]{:S(2)}) collective-permute-start(f32[128,256]{0,1:T(8,128)S(1)} %add.73), channel_id=1, source_target_pairs={{0,2},{1,3},{2,0},{3,1},{4,6},{5,7},{6,4},{7,5},{8,10},{9,11},{10,... | collective-permute-start | bytes 393224 | tf_op jit(solution)/shard_map/ppermute | solution.py:18
  210.9 9.0 %collective-permute-start.13 = (f32[128,256]{0,1:T(8,128)S(1)}, f32[128,256]{0,1:T(8,128)S(1)}, u32[]{:S(2)}, u32[]{:S(2)}) collective-permute-start(f32[128,256]{0,1:T(8,128)S(1)} %add.74), channel_id=1, source_target_pairs={{0,4},{1,5},{2,6},{3,7},{4,0},{5,1},{6,2},{7,3},{8,12},{9,13},{10,... | collective-permute-start | bytes 393224 | tf_op jit(solution)/shard_map/ppermute | solution.py:18
  219.9 8.2 %copy-start = (bf16[128,16384]{1,0:T(8,128)(2,1)S(1)}, bf16[128,16384]{1,0:T(8,128)(2,1)}, u32[]{:S(2)}) copy-start(bf16[128,16384]{1,0:T(8,128)(2,1)} %get-tuple-element.28.refs_0_) | copy-start | bytes 12582916
  219.9 5.4 %collective-permute-start.14 = (f32[128,256]{0,1:T(8,128)S(1)}, f32[128,256]{0,1:T(8,128)S(1)}, u32[]{:S(2)}, u32[]{:S(2)}) collective-permute-start(f32[128,256]{0,1:T(8,128)S(1)} %add.75), channel_id=1, source_target_pairs={{0,8},{1,9},{2,10},{3,11},{4,12},{5,13},{6,14},{7,15},{8,0},{9,1},... | collective-permute-start | bytes 393224 | tf_op jit(solution)/shard_map/ppermute | solution.py:18
  225.3 7.3 %collective-permute-start.15 = (f32[128,256]{0,1:T(8,128)S(1)}, f32[128,256]{0,1:T(8,128)S(1)}, u32[]{:S(2)}, u32[]{:S(2)}) collective-permute-start(f32[128,256]{0,1:T(8,128)S(1)} %add.76), channel_id=1, source_target_pairs={{0,16},{1,17},{2,18},{3,19},{4,20},{5,21},{6,22},{7,23},{8,24},{9,... | collective-permute-start | bytes 393224 | tf_op jit(solution)/shard_map/ppermute | solution.py:18

commit v5 on v4

--- a/solution.py
+++ b/solution.py
@@ -164,10 +164,10 @@
     total_cells = lax.axis_size("gx") * lax.axis_size("gy") * prolong_block.shape[0] * prolong_maps.shape[2]
     head, g11 = lift(head_in, prolong_block, prolong_level, prolong_maps)
     c11 = all_sum(g11) / total_cells
+    tail_in, c11, head = lax.optimization_barrier((tail_in, c11, head))
+    tail, g2 = lift(tail_in, prolong_block, prolong_level, prolong_maps, other=head)
+    g2, c11, head = lax.optimization_barrier((g2, c11, head))
     l11 = jnp.linalg.cholesky(c11)
-    tail_in, l11, head = lax.optimization_barrier((tail_in, l11, head))
-    tail, g2 = lift(tail_in, prolong_block, prolong_level, prolong_maps, other=head)
-    g2, l11, head = lax.optimization_barrier((g2, l11, head))
     inv11 = lax.linalg.triangular_solve(
         l11, jnp.eye(kept, dtype=jnp.float32), left_side=True, lower=True
     )

time: 248 us -> 243 us (0.980)
  waiting for transfers between devices: 66.1 us -> 61.5 us
    ppermute x16, waiting for transfers between devices: 66.1 us -> 61.5 us  [from_partner(): return lax.ppermute(value, axis, pairs)]
  transfers between devices with their start and end apart: 17 -> 17, of which waited for: 14 -> 13; matrix products, arithmetic and copies ran while one was open for 14% -> 14% of each run, Pallas kernels for 4% -> 4%
where the time goes in v5:
time: 243 us; the launch traced here: 242 us
  blocking collectives  62.7 us (26%)
  waiting for transfers between devices  61.5 us (25%)
  other arithmetic  37.6 us (15%)
  starting transfers between devices  34.8 us (14%)
  Pallas kernels  28.9 us (12%)
  matrix products  8.96 us (4%)
  local copies, waits for them, and re-layouts  6.99 us (3%)
    all_to_all x1, blocking collectives, body(): lax.all_to_all(head_out, 'gy', split_axis=0, concat_axis=0, tiled=True)  62.7 us
    ppermute x16, waiting for transfers between devices, from_partner(): return lax.ppermute(value, axis, pairs)  61.5 us
    ppermute x16, starting transfers between devices, from_partner(): return lax.ppermute(value, axis, pairs)  29.9 us
    pallas_call x2, Pallas kernels, lift(): pl.pallas_call(functools.partial(lift_kernel, feeds, brick_cells, paired)...  21.7 us
    another operation x3, other arithmetic, body(): l22 = jnp.linalg.cholesky(schur)  12.4 us
    another operation x3, other arithmetic, body(): l11 = jnp.linalg.cholesky(c11)  12.4 us
    another operation x2, other arithmetic, body(): lax.linalg.triangular_solve(l11, jnp.eye(kept, dtype=jnp.float32), left_s...  10.5 us
    pallas_call x1, Pallas kernels, gather(): pl.pallas_call(functools.partial(gather_kernel, rows), out_shape=[out, ou...  7.21 us
  transfers between devices with their start and end apart: 17, of which 13 were waited for; matrix products, arithmetic and copies ran while one was open for 14% of the time, Pallas kernels for 4%

profile of v5, /device:TPU:6, one launch (start us, length us, event | category | flops | bytes accessed | tf_op | source)
XLA Modules:
  0.0 242.3 jit_solution(14768921153305913473)
XLA Ops:
  3.4 7.2 %shard_map.77 = (bf16[64,128,128]{2,1,0:T(8,128)(2,1)}, bf16[64,128,128]{2,1,0:T(8,128)(2,1)}) custom-call(s32[64]{0:T(128)} %reshape.32.index_ref, s32[64]{0:T(128)} %reshape.33.live_ref, bf16[256,4096]{1,0:T(8,128)(2,1)} %cells_ref.1), custom_call_target="tpu_custom_call" | custom-call | bytes 8388608 | tf_op jit(solution)/shard_map/pallas_call | solution.py:136
  10.6 62.7 %all_to_all.10.recv_ref = bf16[64,128,128]{2,1,0:T(8,128)(2,1)} all-to-all(bf16[64,128,128]{2,1,0:T(8,128)(2,1)} %get-tuple-element.16), channel_id=1, replica_groups=mesh['gx'=8,'gy'=32] {'gy'}, dimensions={0} | all-to-all | bytes 4194304 | tf_op jit(solution)/shard_map/all_to_all | solution.py:161
  73.3 4.9 %all-to-all-start.1 = ((bf16[64,128,128]{2,1,0:T(8,128)(2,1)}), bf16[64,128,128]{2,1,0:T(8,128)(2,1)S(1)}, u32[]{:S(2)}, u32[]{:S(2)}) async-start(bf16[64,128,128]{2,1,0:T(8,128)(2,1)} %get-tuple-element.18), calls=%async_computation.1 | async-start | bytes 4194304 | tf_op jit(solution)/shard_map/all_to_all | solution.py:163
  79.7 9.6 %shard_map.78 = (bf16[128,16384]{1,0:T(8,128)(2,1)}, f32[128,128]{1,0:T(8,128)}) custom-call(s32[128]{0:T(128)} %reshape.30.blocks_ref, s32[128]{0:T(128)} %reshape.31.levels_ref, bf16[64,128,128]{2,1,0:T(8,128)(2,1)} %all_to_all.10.recv_ref, bf16[4,128,512]{2,1,0:T(8,128)(2,1)} %maps_ref.3), custom_call_target="tpu_custom_call" | custom-call | flops 2684354560 | bytes 6815744 | tf_op jit(solution)/shard_map/pallas_call | solution.py:96
  92.6 3.3 %collective-permute-done.1 = f32[128,128]{0,1:T(8,128)S(1)} collective-permute-done((f32[128,128]{0,1:T(8,128)S(1)}, f32[128,128]{0,1:T(8,128)S(1)}, u32[]{:S(2)}, u32[]{:S(2)}) %collective-permute-start.1) | collective-permute-done | bytes 65568 | tf_op jit(solution)/shard_map/ppermute | solution.py:18
  97.7 4.1 %collective-permute-done.2 = f32[128,128]{0,1:T(8,128)S(1)} collective-permute-done((f32[128,128]{0,1:T(8,128)S(1)}, f32[128,128]{0,1:T(8,128)S(1)}, u32[]{:S(2)}, u32[]{:S(2)}) %collective-permute-start.2) | collective-permute-done | bytes 65568 | tf_op jit(solution)/shard_map/ppermute | solution.py:18
  103.7 22.2 %collective-permute-done.3 = f32[128,128]{0,1:T(8,128)S(1)} collective-permute-done((f32[128,128]{0,1:T(8,128)S(1)}, f32[128,128]{0,1:T(8,128)S(1)}, u32[]{:S(2)}, u32[]{:S(2)}) %collective-permute-start.3) | collective-permute-done | bytes 65568 | tf_op jit(solution)/shard_map/ppermute | solution.py:18
  128.4 3.1 %collective-permute-done.4 = f32[128,128]{0,1:T(8,128)S(1)} collective-permute-done((f32[128,128]{0,1:T(8,128)S(1)}, f32[128,128]{0,1:T(8,128)S(1)}, u32[]{:S(2)}, u32[]{:S(2)}) %collective-permute-start.4) | collective-permute-done | bytes 65568 | tf_op jit(solution)/shard_map/ppermute | solution.py:18
  131.4 5.5 %collective-permute-start.5 = (f32[128,128]{0,1:T(8,128)S(1)}, f32[128,128]{0,1:T(8,128)S(1)}, u32[]{:S(2)}, u32[]{:S(2)}) collective-permute-start(f32[128,128]{0,1:T(8,128)S(1)} %add.66), channel_id=1, source_target_pairs={{0,4},{1,5},{2,6},{3,7},{4,0},{5,1},{6,2},{7,3},{8,12},{9,13},{10,... | collective-permute-start | bytes 196616 | tf_op jit(solution)/shard_map/ppermute | solution.py:18
  137.0 2.8 %collective-permute-done.5 = f32[128,128]{0,1:T(8,128)S(1)} collective-permute-done((f32[128,128]{0,1:T(8,128)S(1)}, f32[128,128]{0,1:T(8,128)S(1)}, u32[]{:S(2)}, u32[]{:S(2)}) %collective-permute-start.5) | collective-permute-done | bytes 65568 | tf_op jit(solution)/shard_map/ppermute | solution.py:18
  142.0 2.6 %collective-permute-done.6 = f32[128,128]{0,1:T(8,128)S(1)} collective-permute-done((f32[128,128]{0,1:T(8,128)S(1)}, f32[128,128]{0,1:T(8,128)S(1)}, u32[]{:S(2)}, u32[]{:S(2)}) %collective-permute-start.6) | collective-permute-done | bytes 65568 | tf_op jit(solution)/shard_map/ppermute | solution.py:18
  144.5 3.3 %collective-permute-start.7 = (f32[128,128]{0,1:T(8,128)S(1)}, f32[128,128]{0,1:T(8,128)S(1)}, u32[]{:S(2)}, u32[]{:S(2)}) collective-permute-start(f32[128,128]{0,1:T(8,128)S(1)} %add.68), channel_id=1, source_target_pairs={{0,16},{1,17},{2,18},{3,19},{4,20},{5,21},{6,22},{7,23},{8,24},{9,... | collective-permute-start | bytes 196616 | tf_op jit(solution)/shard_map/ppermute | solution.py:18
  147.8 2.6 %collective-permute-done.7 = f32[128,128]{0,1:T(8,128)S(1)} collective-permute-done((f32[128,128]{0,1:T(8,128)S(1)}, f32[128,128]{0,1:T(8,128)S(1)}, u32[]{:S(2)}, u32[]{:S(2)}) %collective-permute-start.7) | collective-permute-done | bytes 65568 | tf_op jit(solution)/shard_map/ppermute | solution.py:18
  151.7 12.1 %shard_map.79 = (bf16[128,16384]{1,0:T(8,128)(2,1)}, f32[128,256]{1,0:T(8,128)}) custom-call(s32[128]{0:T(128)} %reshape.30.blocks_ref, s32[128]{0:T(128)} %reshape.31.levels_ref, bf16[64,128,128]{2,1,0:T(8,128)(2,1)} %copy-done.1, bf16[4,128,512]{2,1,0:T(8,128)(2,1)} %maps_ref.3, bf16[128,16384]{1,0:T(8,128)(2,1)} %get-tuple-element.28.refs_0_), custom_call_target="tpu_custom_call" | custom-call | flops 3221225472 | bytes 11010048 | tf_op jit(solution)/shard_map/pallas_call | solution.py:96
  167.4 4.6 %collective-permute-done.9 = f32[128,256]{0,1:T(8,128)S(1)} collective-permute-done((f32[128,256]{0,1:T(8,128)S(1)}, f32[128,256]{0,1:T(8,128)S(1)}, u32[]{:S(2)}, u32[]{:S(2)}) %collective-permute-start.9) | collective-permute-done | bytes 131104 | tf_op jit(solution)/shard_map/ppermute | solution.py:18
  173.9 11.7 %cholesky.44 = f32[128,128]{1,0:T(8,128)S(1)} custom-call(f32[128,128]{1,0:T(8,128)S(1)} %fusion.6), custom_call_target="Cholesky" | custom-call | tf_op jit(solution)/shard_map/jit(cholesky)/cholesky | solution.py:170
  186.8 3.9 %collective-permute-done.11 = f32[128,256]{0,1:T(8,128)S(1)} collective-permute-done((f32[128,256]{0,1:T(8,128)S(1)}, f32[128,256]{0,1:T(8,128)S(1)}, u32[]{:S(2)}, u32[]{:S(2)}) %collective-permute-start.11) | collective-permute-done | bytes 131104 | tf_op jit(solution)/shard_map/ppermute | solution.py:18
  190.7 3.9 %collective-permute-start.12 = (f32[128,256]{0,1:T(8,128)S(1)}, f32[128,256]{0,1:T(8,128)S(1)}, u32[]{:S(2)}, u32[]{:S(2)}) collective-permute-start(f32[128,256]{0,1:T(8,128)S(1)} %add.73), channel_id=1, source_target_pairs={{0,2},{1,3},{2,0},{3,1},{4,6},{5,7},{6,4},{7,5},{8,10},{9,11},{10,... | collective-permute-start | bytes 393224 | tf_op jit(solution)/shard_map/ppermute | solution.py:18
  195.3 9.8 %custom-call.5 = f32[1,128,128]{1,2,0:T(8,128)S(1)} custom-call(f32[1,128,128]{2,1,0:T(8,128)S(1)} %get-tuple-element.29), custom_call_target="InvertDiagBlocksLowerTriangular" | custom-call | tf_op jit(solution)/shard_map/triangular_solve | solution.py:171
  207.1 7.1 %collective-permute-done.13 = f32[128,256]{0,1:T(8,128)S(1)} collective-permute-done((f32[128,256]{0,1:T(8,128)S(1)}, f32[128,256]{0,1:T(8,128)S(1)}, u32[]{:S(2)}, u32[]{:S(2)}) %collective-permute-start.13) | collective-permute-done | bytes 131104 | tf_op jit(solution)/shard_map/ppermute | solution.py:18
  214.4 3.6 %fusion.10 = f32[128,16384]{1,0:T(8,128)S(1)} fusion(bf16[128,16384]{1,0:T(8,128)(2,1)} %get-tuple-element.28.refs_0_, f32[128,128]{1,0:T(8,128)S(1)} %fusion.4), kind=kOutput, calls=%fused_computation.25 | convolution fusion | flops 536903680 | bytes 12648448 | tf_op jit(solution)/shard_map/dot_general | solution.py:177
  218.0 2.6 %collective-permute-done.14 = f32[128,256]{0,1:T(8,128)S(1)} collective-permute-done((f32[128,256]{0,1:T(8,128)S(1)}, f32[128,256]{0,1:T(8,128)S(1)}, u32[]{:S(2)}, u32[]{:S(2)}) %collective-permute-start.14) | collective-permute-done | bytes 131104 | tf_op jit(solution)/shard_map/ppermute | solution.py:18
  223.1 4.6 %convolution_add_fusion = f32[128,16384]{1,0:T(8,128)} fusion(f32[128,16384]{1,0:T(8,128)S(1)} %fusion.10, bf16[128,16384]{1,0:T(8,128)(2,1)S(1)} %copy-done, f32[128,128]{1,0:T(8,128)S(1)} %fusion.4), kind=kOutput, calls=%fused_computation | convolution fusion | flops 539017216 | bytes 21037056 | tf_op jit(solution)/shard_map/dot_general | solution.py:177
  228.5 11.7 %cholesky.55 = f32[128,128]{1,0:T(8,128)S(1)} custom-call(f32[128,128]{1,0:T(8,128)S(1)} %fusion.3), custom_call_target="Cholesky" | custom-call | tf_op jit(solution)/shard_map/jit(cholesky)/cholesky | solution.py:184
  (68 shorter events, 31.8 us)
Async XLA Ops:
  10.6 67.7 %copy-start.2 = (s32[32,4]{0,1:T(4,128)S(1)}, s32[32,4]{0,1:T(4,128)}, u32[]{:S(2)}) copy-start(s32[32,4]{0,1:T(4,128)} %param.10) | copy-start | bytes 1540
  10.6 68.4 %copy-start.3 = (s32[32,4]{0,1:T(4,128)S(1)}, s32[32,4]{0,1:T(4,128)}, u32[]{:S(2)}) copy-start(s32[32,4]{0,1:T(4,128)} %param.11) | copy-start | bytes 1540
  73.3 77.1 %all-to-all-start.1 = ((bf16[64,128,128]{2,1,0:T(8,128)(2,1)}), bf16[64,128,128]{2,1,0:T(8,128)(2,1)S(1)}, u32[]{:S(2)}, u32[]{:S(2)}) async-start(bf16[64,128,128]{2,1,0:T(8,128)(2,1)} %get-tuple-element.18), calls=%async_computation.1 | async-start | bytes 4194304 | tf_op jit(solution)/shard_map/all_to_all | solution.py:163
  90.2 1.3 collective-permute-start
  91.6 4.4 %collective-permute-start.1 = (f32[128,128]{0,1:T(8,128)S(1)}, f32[128,128]{0,1:T(8,128)S(1)}, u32[]{:S(2)}, u32[]{:S(2)}) collective-permute-start(f32[128,128]{0,1:T(8,128)S(1)} %add.62), channel_id=1, source_target_pairs={{0,64},{32,96},{64,0},{96,32},{128,192},{160,224},{192,128},{224,1... | collective-permute-start | bytes 196616 | tf_op jit(solution)/shard_map/ppermute | solution.py:18
  96.0 5.9 %collective-permute-start.2 = (f32[128,128]{0,1:T(8,128)S(1)}, f32[128,128]{0,1:T(8,128)S(1)}, u32[]{:S(2)}, u32[]{:S(2)}) collective-permute-start(f32[128,128]{0,1:T(8,128)S(1)} %add.63), channel_id=1, source_target_pairs={{0,128},{32,160},{64,192},{96,224},{128,0},{160,32},{192,64},{224,... | collective-permute-start | bytes 196616 | tf_op jit(solution)/shard_map/ppermute | solution.py:18
  101.8 24.1 %collective-permute-start.3 = (f32[128,128]{0,1:T(8,128)S(1)}, f32[128,128]{0,1:T(8,128)S(1)}, u32[]{:S(2)}, u32[]{:S(2)}) collective-permute-start(f32[128,128]{0,1:T(8,128)S(1)} %add.64), channel_id=1, source_target_pairs={{0,1},{1,0},{2,3},{3,2},{4,5},{5,4},{6,7},{7,6},{8,9},{9,8},{10,11... | collective-permute-start | bytes 196616 | tf_op jit(solution)/shard_map/ppermute | solution.py:18
  125.9 5.5 %collective-permute-start.4 = (f32[128,128]{0,1:T(8,128)S(1)}, f32[128,128]{0,1:T(8,128)S(1)}, u32[]{:S(2)}, u32[]{:S(2)}) collective-permute-start(f32[128,128]{0,1:T(8,128)S(1)} %add.65), channel_id=1, source_target_pairs={{0,2},{1,3},{2,0},{3,1},{4,6},{5,7},{6,4},{7,5},{8,10},{9,11},{10,... | collective-permute-start | bytes 196616 | tf_op jit(solution)/shard_map/ppermute | solution.py:18
  131.4 8.4 %collective-permute-start.5 = (f32[128,128]{0,1:T(8,128)S(1)}, f32[128,128]{0,1:T(8,128)S(1)}, u32[]{:S(2)}, u32[]{:S(2)}) collective-permute-start(f32[128,128]{0,1:T(8,128)S(1)} %add.66), channel_id=1, source_target_pairs={{0,4},{1,5},{2,6},{3,7},{4,0},{5,1},{6,2},{7,3},{8,12},{9,13},{10,... | collective-permute-start | bytes 196616 | tf_op jit(solution)/shard_map/ppermute | solution.py:18
  139.8 4.7 %collective-permute-start.6 = (f32[128,128]{0,1:T(8,128)S(1)}, f32[128,128]{0,1:T(8,128)S(1)}, u32[]{:S(2)}, u32[]{:S(2)}) collective-permute-start(f32[128,128]{0,1:T(8,128)S(1)} %add.67), channel_id=1, source_target_pairs={{0,8},{1,9},{2,10},{3,11},{4,12},{5,13},{6,14},{7,15},{8,0},{9,1},... | collective-permute-start | bytes 196616 | tf_op jit(solution)/shard_map/ppermute | solution.py:18
  144.5 5.9 %collective-permute-start.7 = (f32[128,128]{0,1:T(8,128)S(1)}, f32[128,128]{0,1:T(8,128)S(1)}, u32[]{:S(2)}, u32[]{:S(2)}) collective-permute-start(f32[128,128]{0,1:T(8,128)S(1)} %add.68), channel_id=1, source_target_pairs={{0,16},{1,17},{2,18},{3,19},{4,20},{5,21},{6,22},{7,23},{8,24},{9,... | collective-permute-start | bytes 196616 | tf_op jit(solution)/shard_map/ppermute | solution.py:18
  150.4 1.3 copy-start.1
  164.9 1.4 collective-permute-start.8
  166.3 5.6 %collective-permute-start.9 = (f32[128,256]{0,1:T(8,128)S(1)}, f32[128,256]{0,1:T(8,128)S(1)}, u32[]{:S(2)}, u32[]{:S(2)}) collective-permute-start(f32[128,256]{0,1:T(8,128)S(1)} %add.70), channel_id=1, source_target_pairs={{0,64},{32,96},{64,0},{96,32},{128,192},{160,224},{192,128},{224,1... | collective-permute-start | bytes 393224 | tf_op jit(solution)/shard_map/ppermute | solution.py:18
  172.0 13.6 %collective-permute-start.10 = (f32[128,256]{0,1:T(8,128)S(1)}, f32[128,256]{0,1:T(8,128)S(1)}, u32[]{:S(2)}, u32[]{:S(2)}) collective-permute-start(f32[128,256]{0,1:T(8,128)S(1)} %add.71), channel_id=1, source_target_pairs={{0,128},{32,160},{64,192},{96,224},{128,0},{160,32},{192,64},{224,... | collective-permute-start | bytes 393224 | tf_op jit(solution)/shard_map/ppermute | solution.py:18
  185.6 5.1 %collective-permute-start.11 = (f32[128,256]{0,1:T(8,128)S(1)}, f32[128,256]{0,1:T(8,128)S(1)}, u32[]{:S(2)}, u32[]{:S(2)}) collective-permute-start(f32[128,256]{0,1:T(8,128)S(1)} %add.72), channel_id=1, source_target_pairs={{0,1},{1,0},{2,3},{3,2},{4,5},{5,4},{6,7},{7,6},{8,9},{9,8},{10,11... | collective-permute-start | bytes 393224 | tf_op jit(solution)/shard_map/ppermute | solution.py:18
  190.7 14.4 %collective-permute-start.12 = (f32[128,256]{0,1:T(8,128)S(1)}, f32[128,256]{0,1:T(8,128)S(1)}, u32[]{:S(2)}, u32[]{:S(2)}) collective-permute-start(f32[128,256]{0,1:T(8,128)S(1)} %add.73), channel_id=1, source_target_pairs={{0,2},{1,3},{2,0},{3,1},{4,6},{5,7},{6,4},{7,5},{8,10},{9,11},{10,... | collective-permute-start | bytes 393224 | tf_op jit(solution)/shard_map/ppermute | solution.py:18
  205.1 9.0 %collective-permute-start.13 = (f32[128,256]{0,1:T(8,128)S(1)}, f32[128,256]{0,1:T(8,128)S(1)}, u32[]{:S(2)}, u32[]{:S(2)}) collective-permute-start(f32[128,256]{0,1:T(8,128)S(1)} %add.74), channel_id=1, source_target_pairs={{0,4},{1,5},{2,6},{3,7},{4,0},{5,1},{6,2},{7,3},{8,12},{9,13},{10,... | collective-permute-start | bytes 393224 | tf_op jit(solution)/shard_map/ppermute | solution.py:18
  214.1 9.0 %copy-start = (bf16[128,16384]{1,0:T(8,128)(2,1)S(1)}, bf16[128,16384]{1,0:T(8,128)(2,1)}, u32[]{:S(2)}) copy-start(bf16[128,16384]{1,0:T(8,128)(2,1)} %get-tuple-element.28.refs_0_) | copy-start | bytes 12582916
  214.1 6.4 %collective-permute-start.14 = (f32[128,256]{0,1:T(8,128)S(1)}, f32[128,256]{0,1:T(8,128)S(1)}, u32[]{:S(2)}, u32[]{:S(2)}) collective-permute-start(f32[128,256]{0,1:T(8,128)S(1)} %add.75), channel_id=1, source_target_pairs={{0,8},{1,9},{2,10},{3,11},{4,12},{5,13},{6,14},{7,15},{8,0},{9,1},... | collective-permute-start | bytes 393224 | tf_op jit(solution)/shard_map/ppermute | solution.py:18
  220.6 7.2 %collective-permute-start.15 = (f32[128,256]{0,1:T(8,128)S(1)}, f32[128,256]{0,1:T(8,128)S(1)}, u32[]{:S(2)}, u32[]{:S(2)}) collective-permute-start(f32[128,256]{0,1:T(8,128)S(1)} %add.76), channel_id=1, source_target_pairs={{0,16},{1,17},{2,18},{3,19},{4,20},{5,21},{6,22},{7,23},{8,24},{9,... | collective-permute-start | bytes 393224 | tf_op jit(solution)/shard_map/ppermute | solution.py:18

commit v6 on v5

--- a/solution.py
+++ b/solution.py
@@ -108,46 +108,37 @@
     )(blocks.reshape(-1), levels.reshape(-1), *operands)
 
 
-def gather_kernel(rows, index_ref, live_ref, cells_ref, head_ref, tail_ref, sems):
-    count = head_ref.shape[0]
-    blk = head_ref.shape[2]
+def gather_kernel(first, index_ref, live_ref, cells_ref, out_ref, sems):
+    count, rows, blk = out_ref.shape
     copies = []
     for k in range(count):
         start = pl.multiple_of(index_ref[k] * blk, blk)
-        for part, dst in enumerate((head_ref, tail_ref)):
-            copy = pltpu.make_async_copy(
-                cells_ref.at[pl.ds(part * rows, rows), pl.ds(start, blk)],
-                dst.at[k],
-                sems.at[part, k],
-            )
-            copy.start()
-            copies.append(copy)
+        copy = pltpu.make_async_copy(
+            cells_ref.at[pl.ds(first, rows), pl.ds(start, blk)], out_ref.at[k], sems.at[k]
+        )
+        copy.start()
+        copies.append(copy)
     for copy in copies:
         copy.wait()
     for k in range(count):
         keep = live_ref[k] > 0
-        for dst in (head_ref, tail_ref):
-            dst[k] = jnp.where(keep, dst[k], jnp.zeros_like(dst[k]))
+        out_ref[k] = jnp.where(keep, out_ref[k], jnp.zeros_like(out_ref[k]))
 
 
-def gather(cells, index, live, rows):
+def gather(cells, index, live, first, rows):
     count = index.shape[0]
-    out = jax.ShapeDtypeStruct((count, rows, BLK), cells.dtype)
     return pl.pallas_call(
-        functools.partial(gather_kernel, rows),
-        out_shape=[out, out],
+        functools.partial(gather_kernel, first),
+        out_shape=jax.ShapeDtypeStruct((count, rows, BLK), cells.dtype),
         in_specs=[
             pl.BlockSpec(memory_space=pltpu.SMEM),
             pl.BlockSpec(memory_space=pltpu.SMEM),
             pl.BlockSpec(memory_space=pl.ANY),
         ],
-        out_specs=[
-            pl.BlockSpec(memory_space=pltpu.VMEM),
-            pl.BlockSpec(memory_space=pltpu.VMEM),
-        ],
-        scratch_shapes=[pltpu.SemaphoreType.DMA((2, count))],
+        out_specs=pl.BlockSpec(memory_space=pltpu.VMEM),
+        scratch_shapes=[pltpu.SemaphoreType.DMA((count,))],
         cost_estimate=pl.CostEstimate(
-            flops=0, bytes_accessed=4 * count * rows * BLK * 2, transcendentals=0
+            flops=0, bytes_accessed=2 * count * rows * BLK * 2, transcendentals=0
         ),
     )(index, live, cells)
 
@@ -157,7 +148,9 @@
     kept = RANK
     peers, slots = send_index.shape
     live = (jnp.arange(slots, dtype=jnp.int32)[None, :] < send_count[:, None]).reshape(-1)
-    head_out, tail_out = gather(cells, send_index.reshape(-1), live.astype(jnp.int32), kept)
+    flat_index, flat_live = send_index.reshape(-1), live.astype(jnp.int32)
+    head_out = gather(cells, flat_index, flat_live, 0, kept)
+    tail_out = gather(cells, flat_index, flat_live, kept, snaps - kept)
     head_in = lax.all_to_all(head_out, "gy", split_axis=0, concat_axis=0, tiled=True)
     head_in, tail_out = lax.optimization_barrier((head_in, tail_out))
     tail_in = lax.all_to_all(tail_out, "gy", split_axis=0, concat_axis=0, tiled=True)

time: 243 us -> 244 us (level)
  blocking collectives: 62.7 us -> 0 us
  waiting for transfers between devices: 61.5 us -> 109 us
  starting transfers between devices: 34.8 us -> 45 us
  Pallas kernels: 28.9 us -> 31.6 us
    all_to_all x1 -> x0, blocking collectives: 62.7 us -> none  [body(): lax.all_to_all(head_out, 'gy', split_axis=0, concat_axis=0, tiled=True)]
    all_to_all x0 -> x1, waiting for transfers between devices: none -> 45.4 us  [body(): lax.all_to_all(head_out, 'gy', split_axis=0, concat_axis=0, tiled=True)]
    all_to_all x0 -> x1, starting transfers between devices: none -> 11.1 us  [body(): lax.all_to_all(head_out, 'gy', split_axis=0, concat_axis=0, tiled=True)]
    pallas_call x1 -> x2, Pallas kernels: 7.21 us -> 9.93 us  [gather(): pl.pallas_call(functools.partial(gather_kernel, first), out_shape=jax.Sha...]
  transfers between devices with their start and end apart: 17 -> 18, of which waited for: 13 -> 14; matrix products, arithmetic and copies ran while one was open for 14% -> 14% of each run, Pallas kernels for 4% -> 6%
where the time goes in v6:
time: 244 us; the launch traced here: 241 us
  waiting for transfers between devices  109 us (45%)
  starting transfers between devices  45 us (18%)
  other arithmetic  37.6 us (15%)
  Pallas kernels  31.6 us (13%)
  matrix products  8.95 us (4%)
  local copies, waits for them, and re-layouts  8.37 us (3%)
    ppermute x16, waiting for transfers between devices, from_partner(): return lax.ppermute(value, axis, pairs)  63.3 us
    all_to_all x1, waiting for transfers between devices, body(): lax.all_to_all(head_out, 'gy', split_axis=0, concat_axis=0, tiled=True)  45.4 us
    ppermute x16, starting transfers between devices, from_partner(): return lax.ppermute(value, axis, pairs)  27.7 us
    pallas_call x2, Pallas kernels, lift(): pl.pallas_call(functools.partial(lift_kernel, feeds, brick_cells, paired)...  21.7 us
    another operation x3, other arithmetic, body(): l22 = jnp.linalg.cholesky(schur)  12.4 us
    another operation x3, other arithmetic, body(): l11 = jnp.linalg.cholesky(c11)  12.4 us
    all_to_all x1, starting transfers between devices, body(): lax.all_to_all(head_out, 'gy', split_axis=0, concat_axis=0, tiled=True)  11.1 us
    another operation x2, other arithmetic, body(): lax.linalg.triangular_solve(l11, jnp.eye(kept, dtype=jnp.float32), left_s...  10.5 us
  transfers between devices with their start and end apart: 18, of which 14 were waited for; matrix products, arithmetic and copies ran while one was open for 14% of the time, Pallas kernels for 6%

profile of v6, /device:TPU:6, one launch (start us, length us, event | category | flops | bytes accessed | tf_op | source)
XLA Modules:
  0.0 241.2 jit_solution(9752560017272221660)
XLA Ops:
  3.4 5.1 %shard_map.77 = bf16[64,128,128]{2,1,0:T(8,128)(2,1)} custom-call(s32[64]{0:T(128)} %reshape.32.index_ref, s32[64]{0:T(128)} %reshape.33.live_ref, bf16[256,4096]{1,0:T(8,128)(2,1)} %cells_ref.3), custom_call_target="tpu_custom_call" | custom-call | bytes 4194304 | tf_op jit(solution)/shard_map/pallas_call | solution.py:130
  8.4 11.1 %all-to-all-start = ((bf16[64,128,128]{2,1,0:T(8,128)(2,1)}), bf16[64,128,128]{2,1,0:T(8,128)(2,1)S(1)}, u32[]{:S(2)}, u32[]{:S(2)}) async-start(bf16[64,128,128]{2,1,0:T(8,128)(2,1)} %shard_map.77), calls=%async_computation | async-start | bytes 4194304 | tf_op jit(solution)/shard_map/all_to_all | solution.py:154
  19.6 4.9 %shard_map.78 = bf16[64,128,128]{2,1,0:T(8,128)(2,1)} custom-call(s32[64]{0:T(128)} %reshape.32.index_ref, s32[64]{0:T(128)} %reshape.33.live_ref, bf16[256,4096]{1,0:T(8,128)(2,1)} %cells_ref.3), custom_call_target="tpu_custom_call" | custom-call | bytes 4194304 | tf_op jit(solution)/shard_map/pallas_call | solution.py:130
  24.5 45.4 %all-to-all-done.recv_ref = bf16[64,128,128]{2,1,0:T(8,128)(2,1)S(1)} async-done(((bf16[64,128,128]{2,1,0:T(8,128)(2,1)}), bf16[64,128,128]{2,1,0:T(8,128)(2,1)S(1)}, u32[]{:S(2)}, u32[]{:S(2)}) %all-to-all-start) | async-done | bytes 2097184 | tf_op jit(solution)/shard_map/all_to_all | solution.py:154
  71.2 6.1 %all-to-all-start.1 = ((bf16[64,128,128]{2,1,0:T(8,128)(2,1)}), bf16[64,128,128]{2,1,0:T(8,128)(2,1)S(1)}, u32[]{:S(2)}, u32[]{:S(2)}) async-start(bf16[64,128,128]{2,1,0:T(8,128)(2,1)} %shard_map.78), calls=%async_computation.1 | async-start | bytes 4194304 | tf_op jit(solution)/shard_map/all_to_all | solution.py:156
  78.8 9.6 %shard_map.79 = (bf16[128,16384]{1,0:T(8,128)(2,1)}, f32[128,128]{1,0:T(8,128)}) custom-call(s32[128]{0:T(128)} %reshape.30.blocks_ref, s32[128]{0:T(128)} %reshape.31.levels_ref, bf16[64,128,128]{2,1,0:T(8,128)(2,1)} %copy-done.2, bf16[4,128,512]{2,1,0:T(8,128)(2,1)} %maps_ref.3), custom_call_target="tpu_custom_call" | custom-call | flops 2684354560 | bytes 6815744 | tf_op jit(solution)/shard_map/pallas_call | solution.py:96
  91.6 3.5 %collective-permute-done.1 = f32[128,128]{0,1:T(8,128)S(1)} collective-permute-done((f32[128,128]{0,1:T(8,128)S(1)}, f32[128,128]{0,1:T(8,128)S(1)}, u32[]{:S(2)}, u32[]{:S(2)}) %collective-permute-start.1) | collective-permute-done | bytes 65568 | tf_op jit(solution)/shard_map/ppermute | solution.py:18
  96.4 4.5 %collective-permute-done.2 = f32[128,128]{0,1:T(8,128)S(1)} collective-permute-done((f32[128,128]{0,1:T(8,128)S(1)}, f32[128,128]{0,1:T(8,128)S(1)}, u32[]{:S(2)}, u32[]{:S(2)}) %collective-permute-start.2) | collective-permute-done | bytes 65568 | tf_op jit(solution)/shard_map/ppermute | solution.py:18
  102.8 22.2 %collective-permute-done.3 = f32[128,128]{0,1:T(8,128)S(1)} collective-permute-done((f32[128,128]{0,1:T(8,128)S(1)}, f32[128,128]{0,1:T(8,128)S(1)}, u32[]{:S(2)}, u32[]{:S(2)}) %collective-permute-start.3) | collective-permute-done | bytes 65568 | tf_op jit(solution)/shard_map/ppermute | solution.py:18
  125.1 2.9 %collective-permute-start.4 = (f32[128,128]{0,1:T(8,128)S(1)}, f32[128,128]{0,1:T(8,128)S(1)}, u32[]{:S(2)}, u32[]{:S(2)}) collective-permute-start(f32[128,128]{0,1:T(8,128)S(1)} %add.65), channel_id=1, source_target_pairs={{0,2},{1,3},{2,0},{3,1},{4,6},{5,7},{6,4},{7,5},{8,10},{9,11},{10,... | collective-permute-start | bytes 196616 | tf_op jit(solution)/shard_map/ppermute | solution.py:18
  130.9 5.9 %collective-permute-start.5 = (f32[128,128]{0,1:T(8,128)S(1)}, f32[128,128]{0,1:T(8,128)S(1)}, u32[]{:S(2)}, u32[]{:S(2)}) collective-permute-start(f32[128,128]{0,1:T(8,128)S(1)} %add.66), channel_id=1, source_target_pairs={{0,4},{1,5},{2,6},{3,7},{4,0},{5,1},{6,2},{7,3},{8,12},{9,13},{10,... | collective-permute-start | bytes 196616 | tf_op jit(solution)/shard_map/ppermute | solution.py:18
  136.8 3.0 %collective-permute-done.5 = f32[128,128]{0,1:T(8,128)S(1)} collective-permute-done((f32[128,128]{0,1:T(8,128)S(1)}, f32[128,128]{0,1:T(8,128)S(1)}, u32[]{:S(2)}, u32[]{:S(2)}) %collective-permute-start.5) | collective-permute-done | bytes 65568 | tf_op jit(solution)/shard_map/ppermute | solution.py:18
  141.5 3.1 %collective-permute-done.6 = f32[128,128]{0,1:T(8,128)S(1)} collective-permute-done((f32[128,128]{0,1:T(8,128)S(1)}, f32[128,128]{0,1:T(8,128)S(1)}, u32[]{:S(2)}, u32[]{:S(2)}) %collective-permute-start.6) | collective-permute-done | bytes 65568 | tf_op jit(solution)/shard_map/ppermute | solution.py:18
  147.4 3.1 %collective-permute-done.7 = f32[128,128]{0,1:T(8,128)S(1)} collective-permute-done((f32[128,128]{0,1:T(8,128)S(1)}, f32[128,128]{0,1:T(8,128)S(1)}, u32[]{:S(2)}, u32[]{:S(2)}) %collective-permute-start.7) | collective-permute-done | bytes 65568 | tf_op jit(solution)/shard_map/ppermute | solution.py:18
  151.9 12.1 %shard_map.80 = (bf16[128,16384]{1,0:T(8,128)(2,1)}, f32[128,256]{1,0:T(8,128)}) custom-call(s32[128]{0:T(128)} %reshape.30.blocks_ref, s32[128]{0:T(128)} %reshape.31.levels_ref, bf16[64,128,128]{2,1,0:T(8,128)(2,1)} %copy-done.1, bf16[4,128,512]{2,1,0:T(8,128)(2,1)} %maps_ref.3, bf16[128,16384]{1,0:T(8,128)(2,1)} %get-tuple-element.24.refs_0_), custom_call_target="tpu_custom_call" | custom-call | flops 3221225472 | bytes 11010048 | tf_op jit(solution)/shard_map/pallas_call | solution.py:96
  167.3 4.8 %collective-permute-done.9 = f32[128,256]{0,1:T(8,128)S(1)} collective-permute-done((f32[128,256]{0,1:T(8,128)S(1)}, f32[128,256]{0,1:T(8,128)S(1)}, u32[]{:S(2)}, u32[]{:S(2)}) %collective-permute-start.9) | collective-permute-done | bytes 131104 | tf_op jit(solution)/shard_map/ppermute | solution.py:18
  173.1 11.7 %cholesky.44 = f32[128,128]{1,0:T(8,128)S(1)} custom-call(f32[128,128]{1,0:T(8,128)S(1)} %fusion.6), custom_call_target="Cholesky" | custom-call | tf_op jit(solution)/shard_map/jit(cholesky)/cholesky | solution.py:163
  185.6 4.3 %collective-permute-done.11 = f32[128,256]{0,1:T(8,128)S(1)} collective-permute-done((f32[128,256]{0,1:T(8,128)S(1)}, f32[128,256]{0,1:T(8,128)S(1)}, u32[]{:S(2)}, u32[]{:S(2)}) %collective-permute-start.11) | collective-permute-done | bytes 131104 | tf_op jit(solution)/shard_map/ppermute | solution.py:18
  189.9 3.6 %collective-permute-start.12 = (f32[128,256]{0,1:T(8,128)S(1)}, f32[128,256]{0,1:T(8,128)S(1)}, u32[]{:S(2)}, u32[]{:S(2)}) collective-permute-start(f32[128,256]{0,1:T(8,128)S(1)} %add.73), channel_id=1, source_target_pairs={{0,2},{1,3},{2,0},{3,1},{4,6},{5,7},{6,4},{7,5},{8,10},{9,11},{10,... | collective-permute-start | bytes 393224 | tf_op jit(solution)/shard_map/ppermute | solution.py:18
  194.2 9.8 %custom-call.5 = f32[1,128,128]{1,2,0:T(8,128)S(1)} custom-call(f32[1,128,128]{2,1,0:T(8,128)S(1)} %get-tuple-element.25), custom_call_target="InvertDiagBlocksLowerTriangular" | custom-call | tf_op jit(solution)/shard_map/triangular_solve | solution.py:164
  206.3 6.7 %collective-permute-done.13 = f32[128,256]{0,1:T(8,128)S(1)} collective-permute-done((f32[128,256]{0,1:T(8,128)S(1)}, f32[128,256]{0,1:T(8,128)S(1)}, u32[]{:S(2)}, u32[]{:S(2)}) %collective-permute-start.13) | collective-permute-done | bytes 131104 | tf_op jit(solution)/shard_map/ppermute | solution.py:18
  213.3 3.6 %fusion.10 = f32[128,16384]{1,0:T(8,128)S(1)} fusion(bf16[128,16384]{1,0:T(8,128)(2,1)} %get-tuple-element.24.refs_0_, f32[128,128]{1,0:T(8,128)S(1)} %fusion.4), kind=kOutput, calls=%fused_computation.25 | convolution fusion | flops 536903680 | bytes 12648448 | tf_op jit(solution)/shard_map/dot_general | solution.py:170
  222.0 4.6 %convolution_add_fusion = f32[128,16384]{1,0:T(8,128)} fusion(f32[128,16384]{1,0:T(8,128)S(1)} %fusion.10, bf16[128,16384]{1,0:T(8,128)(2,1)S(1)} %copy-done, f32[128,128]{1,0:T(8,128)S(1)} %fusion.4), kind=kOutput, calls=%fused_computation | convolution fusion | flops 539017216 | bytes 21037056 | tf_op jit(solution)/shard_map/dot_general | solution.py:170
  227.4 11.7 %cholesky.55 = f32[128,128]{1,0:T(8,128)S(1)} custom-call(f32[128,128]{1,0:T(8,128)S(1)} %fusion.3), custom_call_target="Cholesky" | custom-call | tf_op jit(solution)/shard_map/jit(cholesky)/cholesky | solution.py:177
  (72 shorter events, 36.8 us)
Async XLA Ops:
  8.4 61.4 %all-to-all-start = ((bf16[64,128,128]{2,1,0:T(8,128)(2,1)}), bf16[64,128,128]{2,1,0:T(8,128)(2,1)S(1)}, u32[]{:S(2)}, u32[]{:S(2)}) async-start(bf16[64,128,128]{2,1,0:T(8,128)(2,1)} %shard_map.77), calls=%async_computation | async-start | bytes 4194304 | tf_op jit(solution)/shard_map/all_to_all | solution.py:154
  19.6 57.8 %copy-start.3 = (s32[32,4]{0,1:T(4,128)S(1)}, s32[32,4]{0,1:T(4,128)}, u32[]{:S(2)}) copy-start(s32[32,4]{0,1:T(4,128)} %param.10) | copy-start | bytes 1540
  19.6 58.5 %copy-start.4 = (s32[32,4]{0,1:T(4,128)S(1)}, s32[32,4]{0,1:T(4,128)}, u32[]{:S(2)}) copy-start(s32[32,4]{0,1:T(4,128)} %param.11) | copy-start | bytes 1540
  69.9 1.3 copy-start.2
  71.2 79.3 %all-to-all-start.1 = ((bf16[64,128,128]{2,1,0:T(8,128)(2,1)}), bf16[64,128,128]{2,1,0:T(8,128)(2,1)S(1)}, u32[]{:S(2)}, u32[]{:S(2)}) async-start(bf16[64,128,128]{2,1,0:T(8,128)(2,1)} %shard_map.78), calls=%async_computation.1 | async-start | bytes 4194304 | tf_op jit(solution)/shard_map/all_to_all | solution.py:156
  89.4 1.3 collective-permute-start
  90.7 4.4 %collective-permute-start.1 = (f32[128,128]{0,1:T(8,128)S(1)}, f32[128,128]{0,1:T(8,128)S(1)}, u32[]{:S(2)}, u32[]{:S(2)}) collective-permute-start(f32[128,128]{0,1:T(8,128)S(1)} %add.62), channel_id=1, source_target_pairs={{0,64},{32,96},{64,0},{96,32},{128,192},{160,224},{192,128},{224,1... | collective-permute-start | bytes 196616 | tf_op jit(solution)/shard_map/ppermute | solution.py:18
  95.1 5.9 %collective-permute-start.2 = (f32[128,128]{0,1:T(8,128)S(1)}, f32[128,128]{0,1:T(8,128)S(1)}, u32[]{:S(2)}, u32[]{:S(2)}) collective-permute-start(f32[128,128]{0,1:T(8,128)S(1)} %add.63), channel_id=1, source_target_pairs={{0,128},{32,160},{64,192},{96,224},{128,0},{160,32},{192,64},{224,... | collective-permute-start | bytes 196616 | tf_op jit(solution)/shard_map/ppermute | solution.py:18
  101.0 24.1 %collective-permute-start.3 = (f32[128,128]{0,1:T(8,128)S(1)}, f32[128,128]{0,1:T(8,128)S(1)}, u32[]{:S(2)}, u32[]{:S(2)}) collective-permute-start(f32[128,128]{0,1:T(8,128)S(1)} %add.64), channel_id=1, source_target_pairs={{0,1},{1,0},{2,3},{3,2},{4,5},{5,4},{6,7},{7,6},{8,9},{9,8},{10,11... | collective-permute-start | bytes 196616 | tf_op jit(solution)/shard_map/ppermute | solution.py:18
  125.1 5.8 %collective-permute-start.4 = (f32[128,128]{0,1:T(8,128)S(1)}, f32[128,128]{0,1:T(8,128)S(1)}, u32[]{:S(2)}, u32[]{:S(2)}) collective-permute-start(f32[128,128]{0,1:T(8,128)S(1)} %add.65), channel_id=1, source_target_pairs={{0,2},{1,3},{2,0},{3,1},{4,6},{5,7},{6,4},{7,5},{8,10},{9,11},{10,... | collective-permute-start | bytes 196616 | tf_op jit(solution)/shard_map/ppermute | solution.py:18
  130.9 8.9 %collective-permute-start.5 = (f32[128,128]{0,1:T(8,128)S(1)}, f32[128,128]{0,1:T(8,128)S(1)}, u32[]{:S(2)}, u32[]{:S(2)}) collective-permute-start(f32[128,128]{0,1:T(8,128)S(1)} %add.66), channel_id=1, source_target_pairs={{0,4},{1,5},{2,6},{3,7},{4,0},{5,1},{6,2},{7,3},{8,12},{9,13},{10,... | collective-permute-start | bytes 196616 | tf_op jit(solution)/shard_map/ppermute | solution.py:18
  139.8 4.8 %collective-permute-start.6 = (f32[128,128]{0,1:T(8,128)S(1)}, f32[128,128]{0,1:T(8,128)S(1)}, u32[]{:S(2)}, u32[]{:S(2)}) collective-permute-start(f32[128,128]{0,1:T(8,128)S(1)} %add.67), channel_id=1, source_target_pairs={{0,8},{1,9},{2,10},{3,11},{4,12},{5,13},{6,14},{7,15},{8,0},{9,1},... | collective-permute-start | bytes 196616 | tf_op jit(solution)/shard_map/ppermute | solution.py:18
  144.7 5.9 %collective-permute-start.7 = (f32[128,128]{0,1:T(8,128)S(1)}, f32[128,128]{0,1:T(8,128)S(1)}, u32[]{:S(2)}, u32[]{:S(2)}) collective-permute-start(f32[128,128]{0,1:T(8,128)S(1)} %add.68), channel_id=1, source_target_pairs={{0,16},{1,17},{2,18},{3,19},{4,20},{5,21},{6,22},{7,23},{8,24},{9,... | collective-permute-start | bytes 196616 | tf_op jit(solution)/shard_map/ppermute | solution.py:18
  150.5 1.4 copy-start.1
  165.0 1.4 collective-permute-start.8
  166.4 5.6 %collective-permute-start.9 = (f32[128,256]{0,1:T(8,128)S(1)}, f32[128,256]{0,1:T(8,128)S(1)}, u32[]{:S(2)}, u32[]{:S(2)}) collective-permute-start(f32[128,256]{0,1:T(8,128)S(1)} %add.70), channel_id=1, source_target_pairs={{0,64},{32,96},{64,0},{96,32},{128,192},{160,224},{192,128},{224,1... | collective-permute-start | bytes 393224 | tf_op jit(solution)/shard_map/ppermute | solution.py:18
  172.1 12.7 %collective-permute-start.10 = (f32[128,256]{0,1:T(8,128)S(1)}, f32[128,256]{0,1:T(8,128)S(1)}, u32[]{:S(2)}, u32[]{:S(2)}) collective-permute-start(f32[128,256]{0,1:T(8,128)S(1)} %add.71), channel_id=1, source_target_pairs={{0,128},{32,160},{64,192},{96,224},{128,0},{160,32},{192,64},{224,... | collective-permute-start | bytes 393224 | tf_op jit(solution)/shard_map/ppermute | solution.py:18
  184.9 5.1 %collective-permute-start.11 = (f32[128,256]{0,1:T(8,128)S(1)}, f32[128,256]{0,1:T(8,128)S(1)}, u32[]{:S(2)}, u32[]{:S(2)}) collective-permute-start(f32[128,256]{0,1:T(8,128)S(1)} %add.72), channel_id=1, source_target_pairs={{0,1},{1,0},{2,3},{3,2},{4,5},{5,4},{6,7},{7,6},{8,9},{9,8},{10,11... | collective-permute-start | bytes 393224 | tf_op jit(solution)/shard_map/ppermute | solution.py:18
  189.9 14.1 %collective-permute-start.12 = (f32[128,256]{0,1:T(8,128)S(1)}, f32[128,256]{0,1:T(8,128)S(1)}, u32[]{:S(2)}, u32[]{:S(2)}) collective-permute-start(f32[128,256]{0,1:T(8,128)S(1)} %add.73), channel_id=1, source_target_pairs={{0,2},{1,3},{2,0},{3,1},{4,6},{5,7},{6,4},{7,5},{8,10},{9,11},{10,... | collective-permute-start | bytes 393224 | tf_op jit(solution)/shard_map/ppermute | solution.py:18
  204.0 9.0 %collective-permute-start.13 = (f32[128,256]{0,1:T(8,128)S(1)}, f32[128,256]{0,1:T(8,128)S(1)}, u32[]{:S(2)}, u32[]{:S(2)}) collective-permute-start(f32[128,256]{0,1:T(8,128)S(1)} %add.74), channel_id=1, source_target_pairs={{0,4},{1,5},{2,6},{3,7},{4,0},{5,1},{6,2},{7,3},{8,12},{9,13},{10,... | collective-permute-start | bytes 393224 | tf_op jit(solution)/shard_map/ppermute | solution.py:18
  213.0 9.0 %copy-start = (bf16[128,16384]{1,0:T(8,128)(2,1)S(1)}, bf16[128,16384]{1,0:T(8,128)(2,1)}, u32[]{:S(2)}) copy-start(bf16[128,16384]{1,0:T(8,128)(2,1)} %get-tuple-element.24.refs_0_) | copy-start | bytes 12582916
  213.0 6.4 %collective-permute-start.14 = (f32[128,256]{0,1:T(8,128)S(1)}, f32[128,256]{0,1:T(8,128)S(1)}, u32[]{:S(2)}, u32[]{:S(2)}) collective-permute-start(f32[128,256]{0,1:T(8,128)S(1)} %add.75), channel_id=1, source_target_pairs={{0,8},{1,9},{2,10},{3,11},{4,12},{5,13},{6,14},{7,15},{8,0},{9,1},... | collective-permute-start | bytes 393224 | tf_op jit(solution)/shard_map/ppermute | solution.py:18
  219.4 7.3 %collective-permute-start.15 = (f32[128,256]{0,1:T(8,128)S(1)}, f32[128,256]{0,1:T(8,128)S(1)}, u32[]{:S(2)}, u32[]{:S(2)}) collective-permute-start(f32[128,256]{0,1:T(8,128)S(1)} %add.76), channel_id=1, source_target_pairs={{0,16},{1,17},{2,18},{3,19},{4,20},{5,21},{6,22},{7,23},{8,24},{9,... | collective-permute-start | bytes 393224 | tf_op jit(solution)/shard_map/ppermute | solution.py:18

commit v7 on v5

--- a/solution.py
+++ b/solution.py
@@ -18,8 +18,8 @@
     return lax.ppermute(value, axis, pairs)
 
 
-def all_sum(value):
-    for axis in ("gx", "gy"):
+def all_sum(value, axes=("gx", "gy")):
+    for axis in axes:
         for bit in range(lax.axis_size(axis).bit_length() - 1):
             value = value + from_partner(value, axis, bit)
     return value
@@ -177,7 +177,7 @@
     modes = jnp.dot(inv_hi, head, preferred_element_type=jnp.float32) + jnp.dot(
         inv_lo, head, preferred_element_type=jnp.float32
     )
-    lower = all_sum(g2) / total_cells
+    lower = all_sum(g2, ("gy", "gx")) / total_cells
     c21, c22 = lower[:, :kept], lower[:, kept:]
     l21 = jnp.dot(c21, inv11.T, precision=lax.Precision.HIGHEST)
     schur = c22 - jnp.dot(l21, l21.T, precision=lax.Precision.HIGHEST)

time: 243 us -> 246 us (1.012)
  transfers between devices with their start and end apart: 17 -> 17, of which waited for: 13 -> 14; matrix products, arithmetic and copies ran while one was open for 14% -> 14% of each run, Pallas kernels for 4% -> 4%
where the time goes in v7:
time: 246 us; the launch traced here: 244 us
  blocking collectives  63.1 us (26%)
  waiting for transfers between devices  62.5 us (25%)
  other arithmetic  37.6 us (15%)
  starting transfers between devices  35.4 us (14%)
  Pallas kernels  28.7 us (12%)
  matrix products  9.08 us (4%)
  local copies, waits for them, and re-layouts  6.99 us (3%)
    all_to_all x1, blocking collectives, body(): lax.all_to_all(head_out, 'gy', split_axis=0, concat_axis=0, tiled=True)  63.1 us
    ppermute x16, waiting for transfers between devices, from_partner(): return lax.ppermute(value, axis, pairs)  62.5 us
    ppermute x16, starting transfers between devices, from_partner(): return lax.ppermute(value, axis, pairs)  30.3 us
    pallas_call x2, Pallas kernels, lift(): pl.pallas_call(functools.partial(lift_kernel, feeds, brick_cells, paired)...  21.7 us
    another operation x3, other arithmetic, body(): l22 = jnp.linalg.cholesky(schur)  12.4 us
    another operation x3, other arithmetic, body(): l11 = jnp.linalg.cholesky(c11)  12.4 us
    another operation x2, other arithmetic, body(): lax.linalg.triangular_solve(l11, jnp.eye(kept, dtype=jnp.float32), left_s...  10.5 us
    pallas_call x1, Pallas kernels, gather(): pl.pallas_call(functools.partial(gather_kernel, rows), out_shape=[out, ou...  7.03 us
  transfers between devices with their start and end apart: 17, of which 14 were waited for; matrix products, arithmetic and copies ran while one was open for 14% of the time, Pallas kernels for 4%

profile of v7, /device:TPU:6, one launch (start us, length us, event | category | flops | bytes accessed | tf_op | source)
XLA Modules:
  0.0 244.3 jit_solution(7965519131299818279)
XLA Ops:
  3.4 7.0 %shard_map.77 = (bf16[64,128,128]{2,1,0:T(8,128)(2,1)}, bf16[64,128,128]{2,1,0:T(8,128)(2,1)}) custom-call(s32[64]{0:T(128)} %reshape.32.index_ref, s32[64]{0:T(128)} %reshape.33.live_ref, bf16[256,4096]{1,0:T(8,128)(2,1)} %cells_ref.1), custom_call_target="tpu_custom_call" | custom-call | bytes 8388608 | tf_op jit(solution)/shard_map/pallas_call | solution.py:136
  10.4 63.1 %all_to_all.10.recv_ref = bf16[64,128,128]{2,1,0:T(8,128)(2,1)} all-to-all(bf16[64,128,128]{2,1,0:T(8,128)(2,1)} %get-tuple-element.16), channel_id=1, replica_groups=mesh['gx'=8,'gy'=32] {'gy'}, dimensions={0} | all-to-all | bytes 4194304 | tf_op jit(solution)/shard_map/all_to_all | solution.py:161
  73.5 5.1 %all-to-all-start.1 = ((bf16[64,128,128]{2,1,0:T(8,128)(2,1)}), bf16[64,128,128]{2,1,0:T(8,128)(2,1)S(1)}, u32[]{:S(2)}, u32[]{:S(2)}) async-start(bf16[64,128,128]{2,1,0:T(8,128)(2,1)} %get-tuple-element.18), calls=%async_computation.1 | async-start | bytes 4194304 | tf_op jit(solution)/shard_map/all_to_all | solution.py:163
  80.1 9.6 %shard_map.78 = (bf16[128,16384]{1,0:T(8,128)(2,1)}, f32[128,128]{1,0:T(8,128)}) custom-call(s32[128]{0:T(128)} %reshape.30.blocks_ref, s32[128]{0:T(128)} %reshape.31.levels_ref, bf16[64,128,128]{2,1,0:T(8,128)(2,1)} %all_to_all.10.recv_ref, bf16[4,128,512]{2,1,0:T(8,128)(2,1)} %maps_ref.3), custom_call_target="tpu_custom_call" | custom-call | flops 2684354560 | bytes 6815744 | tf_op jit(solution)/shard_map/pallas_call | solution.py:96
  92.5 3.8 %collective-permute-done.1 = f32[128,128]{0,1:T(8,128)S(1)} collective-permute-done((f32[128,128]{0,1:T(8,128)S(1)}, f32[128,128]{0,1:T(8,128)S(1)}, u32[]{:S(2)}, u32[]{:S(2)}) %collective-permute-start.1) | collective-permute-done | bytes 65568 | tf_op jit(solution)/shard_map/ppermute | solution.py:18
  97.6 4.6 %collective-permute-done.2 = f32[128,128]{0,1:T(8,128)S(1)} collective-permute-done((f32[128,128]{0,1:T(8,128)S(1)}, f32[128,128]{0,1:T(8,128)S(1)}, u32[]{:S(2)}, u32[]{:S(2)}) %collective-permute-start.2) | collective-permute-done | bytes 65568 | tf_op jit(solution)/shard_map/ppermute | solution.py:18
  104.1 22.2 %collective-permute-done.3 = f32[128,128]{0,1:T(8,128)S(1)} collective-permute-done((f32[128,128]{0,1:T(8,128)S(1)}, f32[128,128]{0,1:T(8,128)S(1)}, u32[]{:S(2)}, u32[]{:S(2)}) %collective-permute-start.3) | collective-permute-done | bytes 65568 | tf_op jit(solution)/shard_map/ppermute | solution.py:18
  128.7 3.1 %collective-permute-done.4 = f32[128,128]{0,1:T(8,128)S(1)} collective-permute-done((f32[128,128]{0,1:T(8,128)S(1)}, f32[128,128]{0,1:T(8,128)S(1)}, u32[]{:S(2)}, u32[]{:S(2)}) %collective-permute-start.4) | collective-permute-done | bytes 65568 | tf_op jit(solution)/shard_map/ppermute | solution.py:18
  131.7 4.8 %collective-permute-start.5 = (f32[128,128]{0,1:T(8,128)S(1)}, f32[128,128]{0,1:T(8,128)S(1)}, u32[]{:S(2)}, u32[]{:S(2)}) collective-permute-start(f32[128,128]{0,1:T(8,128)S(1)} %add.66), channel_id=1, source_target_pairs={{0,4},{1,5},{2,6},{3,7},{4,0},{5,1},{6,2},{7,3},{8,12},{9,13},{10,... | collective-permute-start | bytes 196616 | tf_op jit(solution)/shard_map/ppermute | solution.py:18
  136.5 3.6 %collective-permute-done.5 = f32[128,128]{0,1:T(8,128)S(1)} collective-permute-done((f32[128,128]{0,1:T(8,128)S(1)}, f32[128,128]{0,1:T(8,128)S(1)}, u32[]{:S(2)}, u32[]{:S(2)}) %collective-permute-start.5) | collective-permute-done | bytes 65568 | tf_op jit(solution)/shard_map/ppermute | solution.py:18
  142.2 2.6 %collective-permute-done.6 = f32[128,128]{0,1:T(8,128)S(1)} collective-permute-done((f32[128,128]{0,1:T(8,128)S(1)}, f32[128,128]{0,1:T(8,128)S(1)}, u32[]{:S(2)}, u32[]{:S(2)}) %collective-permute-start.6) | collective-permute-done | bytes 65568 | tf_op jit(solution)/shard_map/ppermute | solution.py:18
  144.8 3.0 %collective-permute-start.7 = (f32[128,128]{0,1:T(8,128)S(1)}, f32[128,128]{0,1:T(8,128)S(1)}, u32[]{:S(2)}, u32[]{:S(2)}) collective-permute-start(f32[128,128]{0,1:T(8,128)S(1)} %add.68), channel_id=1, source_target_pairs={{0,16},{1,17},{2,18},{3,19},{4,20},{5,21},{6,22},{7,23},{8,24},{9,... | collective-permute-start | bytes 196616 | tf_op jit(solution)/shard_map/ppermute | solution.py:18
  147.8 2.9 %collective-permute-done.7 = f32[128,128]{0,1:T(8,128)S(1)} collective-permute-done((f32[128,128]{0,1:T(8,128)S(1)}, f32[128,128]{0,1:T(8,128)S(1)}, u32[]{:S(2)}, u32[]{:S(2)}) %collective-permute-start.7) | collective-permute-done | bytes 65568 | tf_op jit(solution)/shard_map/ppermute | solution.py:18
  152.0 12.1 %shard_map.79 = (bf16[128,16384]{1,0:T(8,128)(2,1)}, f32[128,256]{1,0:T(8,128)}) custom-call(s32[128]{0:T(128)} %reshape.30.blocks_ref, s32[128]{0:T(128)} %reshape.31.levels_ref, bf16[64,128,128]{2,1,0:T(8,128)(2,1)} %copy-done.1, bf16[4,128,512]{2,1,0:T(8,128)(2,1)} %maps_ref.3, bf16[128,16384]{1,0:T(8,128)(2,1)} %get-tuple-element.28.refs_0_), custom_call_target="tpu_custom_call" | custom-call | flops 3221225472 | bytes 11010048 | tf_op jit(solution)/shard_map/pallas_call | solution.py:96
  165.6 5.3 %collective-permute-done.8 = f32[128,256]{0,1:T(8,128)S(1)} collective-permute-done((f32[128,256]{0,1:T(8,128)S(1)}, f32[128,256]{0,1:T(8,128)S(1)}, u32[]{:S(2)}, u32[]{:S(2)}) %collective-permute-start.8) | collective-permute-done | bytes 131104 | tf_op jit(solution)/shard_map/ppermute | solution.py:18
  173.4 7.7 %collective-permute-done.9 = f32[128,256]{0,1:T(8,128)S(1)} collective-permute-done((f32[128,256]{0,1:T(8,128)S(1)}, f32[128,256]{0,1:T(8,128)S(1)}, u32[]{:S(2)}, u32[]{:S(2)}) %collective-permute-start.9) | collective-permute-done | bytes 131104 | tf_op jit(solution)/shard_map/ppermute | solution.py:18
  181.1 4.2 %collective-permute-start.10 = (f32[128,256]{0,1:T(8,128)S(1)}, f32[128,256]{0,1:T(8,128)S(1)}, u32[]{:S(2)}, u32[]{:S(2)}) collective-permute-start(f32[128,256]{0,1:T(8,128)S(1)} %add.71), channel_id=1, source_target_pairs={{0,4},{1,5},{2,6},{3,7},{4,0},{5,1},{6,2},{7,3},{8,12},{9,13},{10,... | collective-permute-start | bytes 393224 | tf_op jit(solution)/shard_map/ppermute | solution.py:18
  185.3 11.7 %cholesky.44 = f32[128,128]{1,0:T(8,128)S(1)} custom-call(f32[128,128]{1,0:T(8,128)S(1)} %fusion.6), custom_call_target="Cholesky" | custom-call | tf_op jit(solution)/shard_map/jit(cholesky)/cholesky | solution.py:170
  199.7 2.5 %collective-permute-done.11 = f32[128,256]{0,1:T(8,128)S(1)} collective-permute-done((f32[128,256]{0,1:T(8,128)S(1)}, f32[128,256]{0,1:T(8,128)S(1)}, u32[]{:S(2)}, u32[]{:S(2)}) %collective-permute-start.11) | collective-permute-done | bytes 131104 | tf_op jit(solution)/shard_map/ppermute | solution.py:18
  202.1 3.2 %collective-permute-start.12 = (f32[128,256]{0,1:T(8,128)S(1)}, f32[128,256]{0,1:T(8,128)S(1)}, u32[]{:S(2)}, u32[]{:S(2)}) collective-permute-start(f32[128,256]{0,1:T(8,128)S(1)} %add.73), channel_id=1, source_target_pairs={{0,16},{1,17},{2,18},{3,19},{4,20},{5,21},{6,22},{7,23},{8,24},{9,... | collective-permute-start | bytes 393224 | tf_op jit(solution)/shard_map/ppermute | solution.py:18
  206.0 9.8 %custom-call.5 = f32[1,128,128]{1,2,0:T(8,128)S(1)} custom-call(f32[1,128,128]{2,1,0:T(8,128)S(1)} %get-tuple-element.29), custom_call_target="InvertDiagBlocksLowerTriangular" | custom-call | tf_op jit(solution)/shard_map/triangular_solve | solution.py:171
  217.8 3.7 %fusion.10 = f32[128,16384]{1,0:T(8,128)S(1)} fusion(bf16[128,16384]{1,0:T(8,128)(2,1)} %get-tuple-element.28.refs_0_, f32[128,128]{1,0:T(8,128)S(1)} %fusion.4), kind=kOutput, calls=%fused_computation.25 | convolution fusion | flops 536903680 | bytes 12648448 | tf_op jit(solution)/shard_map/dot_general | solution.py:177
  224.5 4.6 %convolution_add_fusion = f32[128,16384]{1,0:T(8,128)} fusion(f32[128,16384]{1,0:T(8,128)S(1)} %fusion.10, bf16[128,16384]{1,0:T(8,128)(2,1)S(1)} %copy-done, f32[128,128]{1,0:T(8,128)S(1)} %fusion.4), kind=kOutput, calls=%fused_computation | convolution fusion | flops 539017216 | bytes 21037056 | tf_op jit(solution)/shard_map/dot_general | solution.py:177
  230.5 11.7 %cholesky.55 = f32[128,128]{1,0:T(8,128)S(1)} custom-call(f32[128,128]{1,0:T(8,128)S(1)} %fusion.3), custom_call_target="Cholesky" | custom-call | tf_op jit(solution)/shard_map/jit(cholesky)/cholesky | solution.py:184
  (68 shorter events, 31.5 us)
Async XLA Ops:
  10.4 68.2 %copy-start.2 = (s32[32,4]{0,1:T(4,128)S(1)}, s32[32,4]{0,1:T(4,128)}, u32[]{:S(2)}) copy-start(s32[32,4]{0,1:T(4,128)} %param.10) | copy-start | bytes 1540
  10.4 68.9 %copy-start.3 = (s32[32,4]{0,1:T(4,128)S(1)}, s32[32,4]{0,1:T(4,128)}, u32[]{:S(2)}) copy-start(s32[32,4]{0,1:T(4,128)} %param.11) | copy-start | bytes 1540
  73.5 77.2 %all-to-all-start.1 = ((bf16[64,128,128]{2,1,0:T(8,128)(2,1)}), bf16[64,128,128]{2,1,0:T(8,128)(2,1)S(1)}, u32[]{:S(2)}, u32[]{:S(2)}) async-start(bf16[64,128,128]{2,1,0:T(8,128)(2,1)} %get-tuple-element.18), calls=%async_computation.1 | async-start | bytes 4194304 | tf_op jit(solution)/shard_map/all_to_all | solution.py:163
  90.6 1.3 collective-permute-start
  92.0 4.4 %collective-permute-start.1 = (f32[128,128]{0,1:T(8,128)S(1)}, f32[128,128]{0,1:T(8,128)S(1)}, u32[]{:S(2)}, u32[]{:S(2)}) collective-permute-start(f32[128,128]{0,1:T(8,128)S(1)} %add.62), channel_id=1, source_target_pairs={{0,64},{32,96},{64,0},{96,32},{128,192},{160,224},{192,128},{224,1... | collective-permute-start | bytes 196616 | tf_op jit(solution)/shard_map/ppermute | solution.py:18
  96.3 5.9 %collective-permute-start.2 = (f32[128,128]{0,1:T(8,128)S(1)}, f32[128,128]{0,1:T(8,128)S(1)}, u32[]{:S(2)}, u32[]{:S(2)}) collective-permute-start(f32[128,128]{0,1:T(8,128)S(1)} %add.63), channel_id=1, source_target_pairs={{0,128},{32,160},{64,192},{96,224},{128,0},{160,32},{192,64},{224,... | collective-permute-start | bytes 196616 | tf_op jit(solution)/shard_map/ppermute | solution.py:18
  102.2 24.1 %collective-permute-start.3 = (f32[128,128]{0,1:T(8,128)S(1)}, f32[128,128]{0,1:T(8,128)S(1)}, u32[]{:S(2)}, u32[]{:S(2)}) collective-permute-start(f32[128,128]{0,1:T(8,128)S(1)} %add.64), channel_id=1, source_target_pairs={{0,1},{1,0},{2,3},{3,2},{4,5},{5,4},{6,7},{7,6},{8,9},{9,8},{10,11... | collective-permute-start | bytes 196616 | tf_op jit(solution)/shard_map/ppermute | solution.py:18
  126.3 5.5 %collective-permute-start.4 = (f32[128,128]{0,1:T(8,128)S(1)}, f32[128,128]{0,1:T(8,128)S(1)}, u32[]{:S(2)}, u32[]{:S(2)}) collective-permute-start(f32[128,128]{0,1:T(8,128)S(1)} %add.65), channel_id=1, source_target_pairs={{0,2},{1,3},{2,0},{3,1},{4,6},{5,7},{6,4},{7,5},{8,10},{9,11},{10,... | collective-permute-start | bytes 196616 | tf_op jit(solution)/shard_map/ppermute | solution.py:18
  131.7 8.4 %collective-permute-start.5 = (f32[128,128]{0,1:T(8,128)S(1)}, f32[128,128]{0,1:T(8,128)S(1)}, u32[]{:S(2)}, u32[]{:S(2)}) collective-permute-start(f32[128,128]{0,1:T(8,128)S(1)} %add.66), channel_id=1, source_target_pairs={{0,4},{1,5},{2,6},{3,7},{4,0},{5,1},{6,2},{7,3},{8,12},{9,13},{10,... | collective-permute-start | bytes 196616 | tf_op jit(solution)/shard_map/ppermute | solution.py:18
  140.2 4.7 %collective-permute-start.6 = (f32[128,128]{0,1:T(8,128)S(1)}, f32[128,128]{0,1:T(8,128)S(1)}, u32[]{:S(2)}, u32[]{:S(2)}) collective-permute-start(f32[128,128]{0,1:T(8,128)S(1)} %add.67), channel_id=1, source_target_pairs={{0,8},{1,9},{2,10},{3,11},{4,12},{5,13},{6,14},{7,15},{8,0},{9,1},... | collective-permute-start | bytes 196616 | tf_op jit(solution)/shard_map/ppermute | solution.py:18
  144.8 5.9 %collective-permute-start.7 = (f32[128,128]{0,1:T(8,128)S(1)}, f32[128,128]{0,1:T(8,128)S(1)}, u32[]{:S(2)}, u32[]{:S(2)}) collective-permute-start(f32[128,128]{0,1:T(8,128)S(1)} %add.68), channel_id=1, source_target_pairs={{0,16},{1,17},{2,18},{3,19},{4,20},{5,21},{6,22},{7,23},{8,24},{9,... | collective-permute-start | bytes 196616 | tf_op jit(solution)/shard_map/ppermute | solution.py:18
  150.7 1.3 copy-start.1
  165.2 5.7 %collective-permute-start.8 = (f32[128,256]{0,1:T(8,128)S(1)}, f32[128,256]{0,1:T(8,128)S(1)}, u32[]{:S(2)}, u32[]{:S(2)}) collective-permute-start(f32[128,256]{0,1:T(8,128)S(1)} %copy.26), channel_id=1, source_target_pairs={{0,1},{1,0},{2,3},{3,2},{4,5},{5,4},{6,7},{7,6},{8,9},{9,8},{10,11... | collective-permute-start | bytes 393224 | tf_op jit(solution)/shard_map/ppermute | solution.py:18
  170.9 10.2 %collective-permute-start.9 = (f32[128,256]{0,1:T(8,128)S(1)}, f32[128,256]{0,1:T(8,128)S(1)}, u32[]{:S(2)}, u32[]{:S(2)}) collective-permute-start(f32[128,256]{0,1:T(8,128)S(1)} %add.70), channel_id=1, source_target_pairs={{0,2},{1,3},{2,0},{3,1},{4,6},{5,7},{6,4},{7,5},{8,10},{9,11},{10,... | collective-permute-start | bytes 393224 | tf_op jit(solution)/shard_map/ppermute | solution.py:18
  181.1 16.0 %collective-permute-start.10 = (f32[128,256]{0,1:T(8,128)S(1)}, f32[128,256]{0,1:T(8,128)S(1)}, u32[]{:S(2)}, u32[]{:S(2)}) collective-permute-start(f32[128,256]{0,1:T(8,128)S(1)} %add.71), channel_id=1, source_target_pairs={{0,4},{1,5},{2,6},{3,7},{4,0},{5,1},{6,2},{7,3},{8,12},{9,13},{10,... | collective-permute-start | bytes 393224 | tf_op jit(solution)/shard_map/ppermute | solution.py:18
  197.1 5.1 %collective-permute-start.11 = (f32[128,256]{0,1:T(8,128)S(1)}, f32[128,256]{0,1:T(8,128)S(1)}, u32[]{:S(2)}, u32[]{:S(2)}) collective-permute-start(f32[128,256]{0,1:T(8,128)S(1)} %add.72), channel_id=1, source_target_pairs={{0,8},{1,9},{2,10},{3,11},{4,12},{5,13},{6,14},{7,15},{8,0},{9,1},... | collective-permute-start | bytes 393224 | tf_op jit(solution)/shard_map/ppermute | solution.py:18
  202.1 13.7 %collective-permute-start.12 = (f32[128,256]{0,1:T(8,128)S(1)}, f32[128,256]{0,1:T(8,128)S(1)}, u32[]{:S(2)}, u32[]{:S(2)}) collective-permute-start(f32[128,256]{0,1:T(8,128)S(1)} %add.73), channel_id=1, source_target_pairs={{0,16},{1,17},{2,18},{3,19},{4,20},{5,21},{6,22},{7,23},{8,24},{9,... | collective-permute-start | bytes 393224 | tf_op jit(solution)/shard_map/ppermute | solution.py:18
  215.8 1.4 collective-permute-start.13
  217.3 7.2 %copy-start = (bf16[128,16384]{1,0:T(8,128)(2,1)S(1)}, bf16[128,16384]{1,0:T(8,128)(2,1)}, u32[]{:S(2)}) copy-start(bf16[128,16384]{1,0:T(8,128)(2,1)} %get-tuple-element.28.refs_0_) | copy-start | bytes 12582916
  217.3 5.6 %collective-permute-start.14 = (f32[128,256]{0,1:T(8,128)S(1)}, f32[128,256]{0,1:T(8,128)S(1)}, u32[]{:S(2)}, u32[]{:S(2)}) collective-permute-start(f32[128,256]{0,1:T(8,128)S(1)} %add.75), channel_id=1, source_target_pairs={{0,64},{32,96},{64,0},{96,32},{128,192},{160,224},{192,128},{224,1... | collective-permute-start | bytes 393224 | tf_op jit(solution)/shard_map/ppermute | solution.py:18
  223.0 6.8 %collective-permute-start.15 = (f32[128,256]{0,1:T(8,128)S(1)}, f32[128,256]{0,1:T(8,128)S(1)}, u32[]{:S(2)}, u32[]{:S(2)}) collective-permute-start(f32[128,256]{0,1:T(8,128)S(1)} %add.76), channel_id=1, source_target_pairs={{0,128},{32,160},{64,192},{96,224},{128,0},{160,32},{192,64},{224,... | collective-permute-start | bytes 393224 | tf_op jit(solution)/shard_map/ppermute | solution.py:18

commit v8 on v5

--- a/solution.py
+++ b/solution.py
@@ -9,7 +9,7 @@
 
 RANK = 128
 BLK = 128
-PER = 8
+PER = 16
 
 
 def from_partner(value, axis, bit):

time: 243 us -> 244 us (level)
  no operation moved by 1% of the time
where the time goes in v8:
time: 244 us; the launch traced here: 242 us
  blocking collectives  62.9 us (26%)
  waiting for transfers between devices  62.4 us (26%)
  other arithmetic  37.6 us (15%)
  starting transfers between devices  33.4 us (14%)
  Pallas kernels  28.8 us (12%)
  matrix products  8.96 us (4%)
  local copies, waits for them, and re-layouts  6.99 us (3%)
    all_to_all x1, blocking collectives, body(): lax.all_to_all(head_out, 'gy', split_axis=0, concat_axis=0, tiled=True)  62.9 us
    ppermute x16, waiting for transfers between devices, from_partner(): return lax.ppermute(value, axis, pairs)  62.4 us
    ppermute x16, starting transfers between devices, from_partner(): return lax.ppermute(value, axis, pairs)  28.4 us
    pallas_call x2, Pallas kernels, lift(): pl.pallas_call(functools.partial(lift_kernel, feeds, brick_cells, paired)...  21.6 us
    another operation x3, other arithmetic, body(): l22 = jnp.linalg.cholesky(schur)  12.4 us
    another operation x3, other arithmetic, body(): l11 = jnp.linalg.cholesky(c11)  12.4 us
    another operation x2, other arithmetic, body(): lax.linalg.triangular_solve(l11, jnp.eye(kept, dtype=jnp.float32), left_s...  10.5 us
    pallas_call x1, Pallas kernels, gather(): pl.pallas_call(functools.partial(gather_kernel, rows), out_shape=[out, ou...  7.17 us
  transfers between devices with their start and end apart: 17, of which 13 were waited for; matrix products, arithmetic and copies ran while one was open for 14% of the time, Pallas kernels for 4%

profile of v8, /device:TPU:6, one launch (start us, length us, event | category | flops | bytes accessed | tf_op | source)
XLA Modules:
  0.0 241.9 jit_solution(15385227452997407576)
XLA Ops:
  3.4 7.2 %shard_map.77 = (bf16[64,128,128]{2,1,0:T(8,128)(2,1)}, bf16[64,128,128]{2,1,0:T(8,128)(2,1)}) custom-call(s32[64]{0:T(128)} %reshape.32.index_ref, s32[64]{0:T(128)} %reshape.33.live_ref, bf16[256,4096]{1,0:T(8,128)(2,1)} %cells_ref.1), custom_call_target="tpu_custom_call" | custom-call | bytes 8388608 | tf_op jit(solution)/shard_map/pallas_call | solution.py:136
  10.6 62.9 %all_to_all.10.recv_ref = bf16[64,128,128]{2,1,0:T(8,128)(2,1)} all-to-all(bf16[64,128,128]{2,1,0:T(8,128)(2,1)} %get-tuple-element.16), channel_id=1, replica_groups=mesh['gx'=8,'gy'=32] {'gy'}, dimensions={0} | all-to-all | bytes 4194304 | tf_op jit(solution)/shard_map/all_to_all | solution.py:161
  73.5 5.0 %all-to-all-start.1 = ((bf16[64,128,128]{2,1,0:T(8,128)(2,1)}), bf16[64,128,128]{2,1,0:T(8,128)(2,1)S(1)}, u32[]{:S(2)}, u32[]{:S(2)}) async-start(bf16[64,128,128]{2,1,0:T(8,128)(2,1)} %get-tuple-element.18), calls=%async_computation.1 | async-start | bytes 4194304 | tf_op jit(solution)/shard_map/all_to_all | solution.py:163
  79.9 9.4 %shard_map.78 = (bf16[128,16384]{1,0:T(8,128)(2,1)}, f32[128,128]{1,0:T(8,128)}) custom-call(s32[128]{0:T(128)} %reshape.30.blocks_ref, s32[128]{0:T(128)} %reshape.31.levels_ref, bf16[64,128,128]{2,1,0:T(8,128)(2,1)} %all_to_all.10.recv_ref, bf16[4,128,512]{2,1,0:T(8,128)(2,1)} %maps_ref.3), custom_call_target="tpu_custom_call" | custom-call | flops 2684354560 | bytes 6815744 | tf_op jit(solution)/shard_map/pallas_call | solution.py:96
  92.4 3.6 %collective-permute-done.1 = f32[128,128]{0,1:T(8,128)S(1)} collective-permute-done((f32[128,128]{0,1:T(8,128)S(1)}, f32[128,128]{0,1:T(8,128)S(1)}, u32[]{:S(2)}, u32[]{:S(2)}) %collective-permute-start.1) | collective-permute-done | bytes 65568 | tf_op jit(solution)/shard_map/ppermute | solution.py:18
  97.3 4.5 %collective-permute-done.2 = f32[128,128]{0,1:T(8,128)S(1)} collective-permute-done((f32[128,128]{0,1:T(8,128)S(1)}, f32[128,128]{0,1:T(8,128)S(1)}, u32[]{:S(2)}, u32[]{:S(2)}) %collective-permute-start.2) | collective-permute-done | bytes 65568 | tf_op jit(solution)/shard_map/ppermute | solution.py:18
  103.7 22.4 %collective-permute-done.3 = f32[128,128]{0,1:T(8,128)S(1)} collective-permute-done((f32[128,128]{0,1:T(8,128)S(1)}, f32[128,128]{0,1:T(8,128)S(1)}, u32[]{:S(2)}, u32[]{:S(2)}) %collective-permute-start.3) | collective-permute-done | bytes 65568 | tf_op jit(solution)/shard_map/ppermute | solution.py:18
  128.6 3.1 %collective-permute-done.4 = f32[128,128]{0,1:T(8,128)S(1)} collective-permute-done((f32[128,128]{0,1:T(8,128)S(1)}, f32[128,128]{0,1:T(8,128)S(1)}, u32[]{:S(2)}, u32[]{:S(2)}) %collective-permute-start.4) | collective-permute-done | bytes 65568 | tf_op jit(solution)/shard_map/ppermute | solution.py:18
  131.7 5.5 %collective-permute-start.5 = (f32[128,128]{0,1:T(8,128)S(1)}, f32[128,128]{0,1:T(8,128)S(1)}, u32[]{:S(2)}, u32[]{:S(2)}) collective-permute-start(f32[128,128]{0,1:T(8,128)S(1)} %add.66), channel_id=1, source_target_pairs={{0,4},{1,5},{2,6},{3,7},{4,0},{5,1},{6,2},{7,3},{8,12},{9,13},{10,... | collective-permute-start | bytes 196616 | tf_op jit(solution)/shard_map/ppermute | solution.py:18
  137.2 2.8 %collective-permute-done.5 = f32[128,128]{0,1:T(8,128)S(1)} collective-permute-done((f32[128,128]{0,1:T(8,128)S(1)}, f32[128,128]{0,1:T(8,128)S(1)}, u32[]{:S(2)}, u32[]{:S(2)}) %collective-permute-start.5) | collective-permute-done | bytes 65568 | tf_op jit(solution)/shard_map/ppermute | solution.py:18
  142.2 2.5 %collective-permute-done.6 = f32[128,128]{0,1:T(8,128)S(1)} collective-permute-done((f32[128,128]{0,1:T(8,128)S(1)}, f32[128,128]{0,1:T(8,128)S(1)}, u32[]{:S(2)}, u32[]{:S(2)}) %collective-permute-start.6) | collective-permute-done | bytes 65568 | tf_op jit(solution)/shard_map/ppermute | solution.py:18
  144.7 3.5 %collective-permute-start.7 = (f32[128,128]{0,1:T(8,128)S(1)}, f32[128,128]{0,1:T(8,128)S(1)}, u32[]{:S(2)}, u32[]{:S(2)}) collective-permute-start(f32[128,128]{0,1:T(8,128)S(1)} %add.68), channel_id=1, source_target_pairs={{0,16},{1,17},{2,18},{3,19},{4,20},{5,21},{6,22},{7,23},{8,24},{9,... | collective-permute-start | bytes 196616 | tf_op jit(solution)/shard_map/ppermute | solution.py:18
  148.2 2.5 %collective-permute-done.7 = f32[128,128]{0,1:T(8,128)S(1)} collective-permute-done((f32[128,128]{0,1:T(8,128)S(1)}, f32[128,128]{0,1:T(8,128)S(1)}, u32[]{:S(2)}, u32[]{:S(2)}) %collective-permute-start.7) | collective-permute-done | bytes 65568 | tf_op jit(solution)/shard_map/ppermute | solution.py:18
  152.1 12.3 %shard_map.79 = (bf16[128,16384]{1,0:T(8,128)(2,1)}, f32[128,256]{1,0:T(8,128)}) custom-call(s32[128]{0:T(128)} %reshape.30.blocks_ref, s32[128]{0:T(128)} %reshape.31.levels_ref, bf16[64,128,128]{2,1,0:T(8,128)(2,1)} %copy-done.1, bf16[4,128,512]{2,1,0:T(8,128)(2,1)} %maps_ref.3, bf16[128,16384]{1,0:T(8,128)(2,1)} %get-tuple-element.28.refs_0_), custom_call_target="tpu_custom_call" | custom-call | flops 3221225472 | bytes 11010048 | tf_op jit(solution)/shard_map/pallas_call | solution.py:96
  167.7 4.8 %collective-permute-done.9 = f32[128,256]{0,1:T(8,128)S(1)} collective-permute-done((f32[128,256]{0,1:T(8,128)S(1)}, f32[128,256]{0,1:T(8,128)S(1)}, u32[]{:S(2)}, u32[]{:S(2)}) %collective-permute-start.9) | collective-permute-done | bytes 131104 | tf_op jit(solution)/shard_map/ppermute | solution.py:18
  173.8 11.7 %cholesky.44 = f32[128,128]{1,0:T(8,128)S(1)} custom-call(f32[128,128]{1,0:T(8,128)S(1)} %fusion.6), custom_call_target="Cholesky" | custom-call | tf_op jit(solution)/shard_map/jit(cholesky)/cholesky | solution.py:170
  186.7 3.9 %collective-permute-done.11 = f32[128,256]{0,1:T(8,128)S(1)} collective-permute-done((f32[128,256]{0,1:T(8,128)S(1)}, f32[128,256]{0,1:T(8,128)S(1)}, u32[]{:S(2)}, u32[]{:S(2)}) %collective-permute-start.11) | collective-permute-done | bytes 131104 | tf_op jit(solution)/shard_map/ppermute | solution.py:18
  190.6 3.8 %collective-permute-start.12 = (f32[128,256]{0,1:T(8,128)S(1)}, f32[128,256]{0,1:T(8,128)S(1)}, u32[]{:S(2)}, u32[]{:S(2)}) collective-permute-start(f32[128,256]{0,1:T(8,128)S(1)} %add.73), channel_id=1, source_target_pairs={{0,2},{1,3},{2,0},{3,1},{4,6},{5,7},{6,4},{7,5},{8,10},{9,11},{10,... | collective-permute-start | bytes 393224 | tf_op jit(solution)/shard_map/ppermute | solution.py:18
  195.1 9.8 %custom-call.5 = f32[1,128,128]{1,2,0:T(8,128)S(1)} custom-call(f32[1,128,128]{2,1,0:T(8,128)S(1)} %get-tuple-element.29), custom_call_target="InvertDiagBlocksLowerTriangular" | custom-call | tf_op jit(solution)/shard_map/triangular_solve | solution.py:171
  207.1 7.1 %collective-permute-done.13 = f32[128,256]{0,1:T(8,128)S(1)} collective-permute-done((f32[128,256]{0,1:T(8,128)S(1)}, f32[128,256]{0,1:T(8,128)S(1)}, u32[]{:S(2)}, u32[]{:S(2)}) %collective-permute-start.13) | collective-permute-done | bytes 131104 | tf_op jit(solution)/shard_map/ppermute | solution.py:18
  214.3 3.6 %fusion.10 = f32[128,16384]{1,0:T(8,128)S(1)} fusion(bf16[128,16384]{1,0:T(8,128)(2,1)} %get-tuple-element.28.refs_0_, f32[128,128]{1,0:T(8,128)S(1)} %fusion.4), kind=kOutput, calls=%fused_computation.25 | convolution fusion | flops 536903680 | bytes 12648448 | tf_op jit(solution)/shard_map/dot_general | solution.py:177
  217.9 2.7 %collective-permute-done.14 = f32[128,256]{0,1:T(8,128)S(1)} collective-permute-done((f32[128,256]{0,1:T(8,128)S(1)}, f32[128,256]{0,1:T(8,128)S(1)}, u32[]{:S(2)}, u32[]{:S(2)}) %collective-permute-start.14) | collective-permute-done | bytes 131104 | tf_op jit(solution)/shard_map/ppermute | solution.py:18
  222.7 4.6 %convolution_add_fusion = f32[128,16384]{1,0:T(8,128)} fusion(f32[128,16384]{1,0:T(8,128)S(1)} %fusion.10, bf16[128,16384]{1,0:T(8,128)(2,1)S(1)} %copy-done, f32[128,128]{1,0:T(8,128)S(1)} %fusion.4), kind=kOutput, calls=%fused_computation | convolution fusion | flops 539017216 | bytes 21037056 | tf_op jit(solution)/shard_map/dot_general | solution.py:177
  228.1 11.7 %cholesky.55 = f32[128,128]{1,0:T(8,128)S(1)} custom-call(f32[128,128]{1,0:T(8,128)S(1)} %fusion.3), custom_call_target="Cholesky" | custom-call | tf_op jit(solution)/shard_map/jit(cholesky)/cholesky | solution.py:184
  (68 shorter events, 30.2 us)
Async XLA Ops:
  10.6 67.9 %copy-start.2 = (s32[32,4]{0,1:T(4,128)S(1)}, s32[32,4]{0,1:T(4,128)}, u32[]{:S(2)}) copy-start(s32[32,4]{0,1:T(4,128)} %param.10) | copy-start | bytes 1540
  10.6 68.6 %copy-start.3 = (s32[32,4]{0,1:T(4,128)S(1)}, s32[32,4]{0,1:T(4,128)}, u32[]{:S(2)}) copy-start(s32[32,4]{0,1:T(4,128)} %param.11) | copy-start | bytes 1540
  73.5 77.2 %all-to-all-start.1 = ((bf16[64,128,128]{2,1,0:T(8,128)(2,1)}), bf16[64,128,128]{2,1,0:T(8,128)(2,1)S(1)}, u32[]{:S(2)}, u32[]{:S(2)}) async-start(bf16[64,128,128]{2,1,0:T(8,128)(2,1)} %get-tuple-element.18), calls=%async_computation.1 | async-start | bytes 4194304 | tf_op jit(solution)/shard_map/all_to_all | solution.py:163
  90.2 1.3 collective-permute-start
  91.6 4.4 %collective-permute-start.1 = (f32[128,128]{0,1:T(8,128)S(1)}, f32[128,128]{0,1:T(8,128)S(1)}, u32[]{:S(2)}, u32[]{:S(2)}) collective-permute-start(f32[128,128]{0,1:T(8,128)S(1)} %add.62), channel_id=1, source_target_pairs={{0,64},{32,96},{64,0},{96,32},{128,192},{160,224},{192,128},{224,1... | collective-permute-start | bytes 196616 | tf_op jit(solution)/shard_map/ppermute | solution.py:18
  96.0 5.9 %collective-permute-start.2 = (f32[128,128]{0,1:T(8,128)S(1)}, f32[128,128]{0,1:T(8,128)S(1)}, u32[]{:S(2)}, u32[]{:S(2)}) collective-permute-start(f32[128,128]{0,1:T(8,128)S(1)} %add.63), channel_id=1, source_target_pairs={{0,128},{32,160},{64,192},{96,224},{128,0},{160,32},{192,64},{224,... | collective-permute-start | bytes 196616 | tf_op jit(solution)/shard_map/ppermute | solution.py:18
  101.8 24.3 %collective-permute-start.3 = (f32[128,128]{0,1:T(8,128)S(1)}, f32[128,128]{0,1:T(8,128)S(1)}, u32[]{:S(2)}, u32[]{:S(2)}) collective-permute-start(f32[128,128]{0,1:T(8,128)S(1)} %add.64), channel_id=1, source_target_pairs={{0,1},{1,0},{2,3},{3,2},{4,5},{5,4},{6,7},{7,6},{8,9},{9,8},{10,11... | collective-permute-start | bytes 196616 | tf_op jit(solution)/shard_map/ppermute | solution.py:18
  126.1 5.5 %collective-permute-start.4 = (f32[128,128]{0,1:T(8,128)S(1)}, f32[128,128]{0,1:T(8,128)S(1)}, u32[]{:S(2)}, u32[]{:S(2)}) collective-permute-start(f32[128,128]{0,1:T(8,128)S(1)} %add.65), channel_id=1, source_target_pairs={{0,2},{1,3},{2,0},{3,1},{4,6},{5,7},{6,4},{7,5},{8,10},{9,11},{10,... | collective-permute-start | bytes 196616 | tf_op jit(solution)/shard_map/ppermute | solution.py:18
  131.7 8.4 %collective-permute-start.5 = (f32[128,128]{0,1:T(8,128)S(1)}, f32[128,128]{0,1:T(8,128)S(1)}, u32[]{:S(2)}, u32[]{:S(2)}) collective-permute-start(f32[128,128]{0,1:T(8,128)S(1)} %add.66), channel_id=1, source_target_pairs={{0,4},{1,5},{2,6},{3,7},{4,0},{5,1},{6,2},{7,3},{8,12},{9,13},{10,... | collective-permute-start | bytes 196616 | tf_op jit(solution)/shard_map/ppermute | solution.py:18
  140.1 4.6 %collective-permute-start.6 = (f32[128,128]{0,1:T(8,128)S(1)}, f32[128,128]{0,1:T(8,128)S(1)}, u32[]{:S(2)}, u32[]{:S(2)}) collective-permute-start(f32[128,128]{0,1:T(8,128)S(1)} %add.67), channel_id=1, source_target_pairs={{0,8},{1,9},{2,10},{3,11},{4,12},{5,13},{6,14},{7,15},{8,0},{9,1},... | collective-permute-start | bytes 196616 | tf_op jit(solution)/shard_map/ppermute | solution.py:18
  144.7 6.0 %collective-permute-start.7 = (f32[128,128]{0,1:T(8,128)S(1)}, f32[128,128]{0,1:T(8,128)S(1)}, u32[]{:S(2)}, u32[]{:S(2)}) collective-permute-start(f32[128,128]{0,1:T(8,128)S(1)} %add.68), channel_id=1, source_target_pairs={{0,16},{1,17},{2,18},{3,19},{4,20},{5,21},{6,22},{7,23},{8,24},{9,... | collective-permute-start | bytes 196616 | tf_op jit(solution)/shard_map/ppermute | solution.py:18
  150.7 1.3 copy-start.1
  165.3 1.4 collective-permute-start.8
  166.8 5.6 %collective-permute-start.9 = (f32[128,256]{0,1:T(8,128)S(1)}, f32[128,256]{0,1:T(8,128)S(1)}, u32[]{:S(2)}, u32[]{:S(2)}) collective-permute-start(f32[128,256]{0,1:T(8,128)S(1)} %add.70), channel_id=1, source_target_pairs={{0,64},{32,96},{64,0},{96,32},{128,192},{160,224},{192,128},{224,1... | collective-permute-start | bytes 393224 | tf_op jit(solution)/shard_map/ppermute | solution.py:18
  172.4 13.1 %collective-permute-start.10 = (f32[128,256]{0,1:T(8,128)S(1)}, f32[128,256]{0,1:T(8,128)S(1)}, u32[]{:S(2)}, u32[]{:S(2)}) collective-permute-start(f32[128,256]{0,1:T(8,128)S(1)} %add.71), channel_id=1, source_target_pairs={{0,128},{32,160},{64,192},{96,224},{128,0},{160,32},{192,64},{224,... | collective-permute-start | bytes 393224 | tf_op jit(solution)/shard_map/ppermute | solution.py:18
  185.5 5.1 %collective-permute-start.11 = (f32[128,256]{0,1:T(8,128)S(1)}, f32[128,256]{0,1:T(8,128)S(1)}, u32[]{:S(2)}, u32[]{:S(2)}) collective-permute-start(f32[128,256]{0,1:T(8,128)S(1)} %add.72), channel_id=1, source_target_pairs={{0,1},{1,0},{2,3},{3,2},{4,5},{5,4},{6,7},{7,6},{8,9},{9,8},{10,11... | collective-permute-start | bytes 393224 | tf_op jit(solution)/shard_map/ppermute | solution.py:18
  190.6 14.3 %collective-permute-start.12 = (f32[128,256]{0,1:T(8,128)S(1)}, f32[128,256]{0,1:T(8,128)S(1)}, u32[]{:S(2)}, u32[]{:S(2)}) collective-permute-start(f32[128,256]{0,1:T(8,128)S(1)} %add.73), channel_id=1, source_target_pairs={{0,2},{1,3},{2,0},{3,1},{4,6},{5,7},{6,4},{7,5},{8,10},{9,11},{10,... | collective-permute-start | bytes 393224 | tf_op jit(solution)/shard_map/ppermute | solution.py:18
  205.0 9.2 %collective-permute-start.13 = (f32[128,256]{0,1:T(8,128)S(1)}, f32[128,256]{0,1:T(8,128)S(1)}, u32[]{:S(2)}, u32[]{:S(2)}) collective-permute-start(f32[128,256]{0,1:T(8,128)S(1)} %add.74), channel_id=1, source_target_pairs={{0,4},{1,5},{2,6},{3,7},{4,0},{5,1},{6,2},{7,3},{8,12},{9,13},{10,... | collective-permute-start | bytes 393224 | tf_op jit(solution)/shard_map/ppermute | solution.py:18
  214.2 8.6 %copy-start = (bf16[128,16384]{1,0:T(8,128)(2,1)S(1)}, bf16[128,16384]{1,0:T(8,128)(2,1)}, u32[]{:S(2)}) copy-start(bf16[128,16384]{1,0:T(8,128)(2,1)} %get-tuple-element.28.refs_0_) | copy-start | bytes 12582916
  214.2 6.4 %collective-permute-start.14 = (f32[128,256]{0,1:T(8,128)S(1)}, f32[128,256]{0,1:T(8,128)S(1)}, u32[]{:S(2)}, u32[]{:S(2)}) collective-permute-start(f32[128,256]{0,1:T(8,128)S(1)} %add.75), channel_id=1, source_target_pairs={{0,8},{1,9},{2,10},{3,11},{4,12},{5,13},{6,14},{7,15},{8,0},{9,1},... | collective-permute-start | bytes 393224 | tf_op jit(solution)/shard_map/ppermute | solution.py:18
  220.6 6.8 %collective-permute-start.15 = (f32[128,256]{0,1:T(8,128)S(1)}, f32[128,256]{0,1:T(8,128)S(1)}, u32[]{:S(2)}, u32[]{:S(2)}) collective-permute-start(f32[128,256]{0,1:T(8,128)S(1)} %add.76), channel_id=1, source_target_pairs={{0,16},{1,17},{2,18},{3,19},{4,20},{5,21},{6,22},{7,23},{8,24},{9,... | collective-permute-start | bytes 393224 | tf_op jit(solution)/shard_map/ppermute | solution.py:18
